TPU v7x, 128 devices: a whole 4x4x4 slice. The times are simulated.
128 devices in a mesh: blk: 8 (over y_hi, z), group: 16 (over y_lo, x, core).
Axes of the slice: x: 4, y: 4 (y_hi: 2, y_lo: 2; y = y_hi * 2 + y_lo), z: 4, core: 2. Of those that a mesh axis runs over, the one named last changes fastest.
Arguments:
- positions: float32 [3, 1048576], P(None, ('blk', 'group')), may hold values from -6 to 6
- velocities: float32 [3, 1048576], P(None, ('blk', 'group')), may hold values from -6 to 6
- accelerations: float32 [3, 1048576], P(None, ('blk', 'group')), may hold values from -6 to 6
- jerk_rates: float32 [3, 1048576], P(None, ('blk', 'group')), may hold values from -24 to 24
- masses: float32 [1048576], P(('blk', 'group')), may hold values from 0.1 to 10
- elapsed_time: float32 [1048576], P(('blk', 'group')), may hold values from 0.05 to 0.5
- active_index: int32 [2048], P(('blk', 'group')), may hold values from 0 to 1048575
Outputs:
- new_pos: float32 [3, 2048], P(None, ('blk', 'group'))
- new_vel: float32 [3, 2048], P(None, ('blk', 'group'))
- new_acc: float32 [3, 2048], P(None, ('blk', 'group'))
- new_jerk: float32 [3, 2048], P(None, ('blk', 'group'))
All inputs are finite; a program needn't handle non-finite values.
Results may differ from a plain program's by a relative error of at most 0.0003.
Values sent between devices are 32-bit elements; how exact they have to be, the bound alone decides.
No kernel may reach another device: no remote copies, remote signals or barrier semaphores. Data moves between devices by JAX's collectives and lax.ppermute only.
A program may use at most 128 MiB of HBM per device.

v0:
```python
import math

import jax
import jax.numpy as jnp
from jax import lax
from jax.sharding import PartitionSpec as P

softening = 0.001


def predict(pos_now, vel_now, acc_now, jerk_now, elapsed):
    pred_pos = pos_now + elapsed * (
        vel_now + elapsed * (0.5 * acc_now + elapsed * (jerk_now / 6.0))
    )
    pred_vel = vel_now + elapsed * (acc_now + elapsed * (0.5 * jerk_now))
    return (pred_pos, pred_vel)


def block_forces(active_data, field_piece):
    offset = field_piece[0:3, None, :] - active_data[0:3, :, None]
    motion = field_piece[3:6, None, :] - active_data[3:6, :, None]
    dist_sq = jnp.sum(offset * offset, axis=0) + softening
    inverse = lax.rsqrt(dist_sq)
    weight = field_piece[6][None, :] * inverse * inverse * inverse
    factor = 3.0 * jnp.sum(offset * motion, axis=0) / dist_sq
    accel_part = jnp.sum(offset * weight, axis=2)
    jerk_part = jnp.sum((motion - factor * offset) * weight, axis=2)
    return jnp.concatenate([accel_part, jerk_part], axis=0)


def pair_forces(active_data, field):
    num_active = active_data.shape[1]
    num_field = field.shape[1]
    columns = math.gcd(num_field, max(1, 524288 // num_active))

    def advance(summed, which):
        field_piece = lax.dynamic_slice_in_dim(field, which * columns, columns, 1)
        return (summed + block_forces(active_data, field_piece), None)

    summed, _ = lax.scan(
        advance,
        jnp.zeros((6, num_active), jnp.float32),
        jnp.arange(num_field // columns, dtype=jnp.int32),
    )
    return summed


def corrector(owner_rows, forces):
    old_pos = owner_rows[0:3]
    old_vel = owner_rows[3:6]
    old_acc = owner_rows[6:9]
    old_jerk = owner_rows[9:12]
    elapsed = owner_rows[12]
    new_acc = forces[0:3]
    new_jerk = forces[3:6]
    squared = elapsed * elapsed / 12.0
    new_vel = old_vel + 0.5 * elapsed * (old_acc + new_acc) + squared * (old_jerk - new_jerk)
    new_pos = old_pos + 0.5 * elapsed * (old_vel + new_vel) + squared * (old_acc - new_acc)
    return (new_pos, new_vel, new_acc, new_jerk)


def on_device(positions, velocities, accelerations, jerk_rates, masses, elapsed_time, active_index):
    own_stars = positions.shape[1]
    total_stars = own_stars * lax.axis_size("blk") * lax.axis_size("group")
    gravity = 1.0 / total_stars
    pred_pos, pred_vel = predict(positions, velocities, accelerations, jerk_rates, elapsed_time)
    own_field = jnp.concatenate([pred_pos, pred_vel, masses[None, :]], axis=0)
    packed = jnp.concatenate(
        [positions, velocities, accelerations, jerk_rates, elapsed_time[None, :]], axis=0
    )
    every_index = lax.all_gather(active_index, ("blk", "group"), axis=0, tiled=True)
    first_row = lax.axis_index(("blk", "group")) * own_stars
    local_row = every_index - first_row
    is_owned = (local_row >= 0) & (local_row < own_stars)
    picked = jnp.take(packed, jnp.clip(local_row, 0, own_stars - 1), axis=1)
    picked = picked * is_owned.astype(jnp.float32)[None, :]
    owner_rows = lax.psum_scatter(picked, ("blk", "group"), scatter_dimension=1, tiled=True)
    mine_pos, mine_vel = predict(
        owner_rows[0:3], owner_rows[3:6], owner_rows[6:9], owner_rows[9:12], owner_rows[12]
    )
    mine_state = jnp.concatenate([mine_pos, mine_vel], axis=0)
    field_group = lax.all_gather(own_field, "group", axis=1, tiled=True)
    group_state = lax.all_gather(mine_state, "blk", axis=1, tiled=True)
    partial_sum = pair_forces(group_state, field_group)
    forces = lax.psum_scatter(partial_sum, "blk", scatter_dimension=1, tiled=True)
    return corrector(owner_rows, forces * gravity)


def solution(mesh):
    return jax.shard_map(
        on_device,
        mesh=mesh,
        in_specs=(
            P(None, ("blk", "group")),
            P(None, ("blk", "group")),
            P(None, ("blk", "group")),
            P(None, ("blk", "group")),
            P(("blk", "group")),
            P(("blk", "group")),
            P(("blk", "group")),
        ),
        out_specs=(
            P(None, ("blk", "group")),
            P(None, ("blk", "group")),
            P(None, ("blk", "group")),
            P(None, ("blk", "group")),
        ),
        check_vma=False,
    )
```

profile of v0, /device:TPU:1, one launch (start us, length us, event | category | flops | bytes accessed | tf_op | source)
XLA Modules:
  0.0 1198.4 jit_solution(1584363948806928686)
XLA Ops:
  8.9 68.7 %all-reduce = s32[2048]{0:T(1024)S(1)} all-reduce(s32[2048]{0:T(1024)S(1)} %dynamic-update-slice), channel_id=1, replica_groups=mesh['blk'=8,'group'=16] {'blk','group'}, use_global_device_ids=true, to_apply=%add | all-reduce | flops 2048 | bytes 16384
  77.6 4.0 concatenate.12
  81.8 2.6 copy.41
  84.4 7.6 gather_fusion
  94.7 634.7 %reduce-scatter.3.cloned.1.call-done = f32[13,16]{0,1:T(8,128)} async-done(((f32[13,2048]{0,1:T(8,128)}), f32[13,16]{0,1:T(8,128)}) %reduce-scatter.3.cloned.1.call-update) | async-done | bytes 848 | tf_op jit(solution)/shard_map/reduce_scatter | solution.py:77
  731.5 27.9 %all-gather = f32[8,16,6]{1,2,0:T(8,128)S(1)} all-gather(f32[1,16,6]{1,2,0:T(8,128)S(1)} %bitcast.20), channel_id=1, replica_groups=mesh['blk'=8,'group'=16] {'blk'}, dimensions={0}, use_global_device_ids=true | all-gather | bytes 3456 | tf_op jit(solution)/shard_map/all_gather | solution.py:83
  759.5 350.3 %while.11 = (s32[]{:T(128)}, f32[6,128]{1,0:T(8,128)S(1)}, s32[32]{0:T(128)S(1)}, f32[7,131072]{1,0:T(8,128)}, f32[6,128]{1,0:T(8,128)S(1)}, /*index=5*/s32[]{:T...) while((s32[]{:T(128)}, f32[6,128]{1,0:T(8,128)S(1)}, s32[32]{0:T(128)S(1)}, ...), condition=%wide.region_6.7_spmd.clone, body=%wide.region_1.6_spmd.clone.sunk | while | flops 24118792 | bytes 17244372 | solution.py:40
  761.8 3.3 fusion.14
  772.8 3.3 fusion.14
  779.2 2.1 fusion.15
  783.7 3.3 fusion.14
  790.1 2.1 fusion.15
  794.7 3.3 fusion.14
  801.1 2.1 fusion.15
  805.6 3.3 fusion.14
  812.0 2.1 fusion.15
  816.6 3.3 fusion.14
  823.0 2.1 fusion.15
  827.5 3.3 fusion.14
  833.9 2.1 fusion.15
  838.4 3.3 fusion.14
  849.4 3.3 fusion.14
  860.3 3.3 fusion.14
  871.3 3.3 fusion.14
  877.7 2.1 fusion.15
  882.2 3.3 fusion.14
  888.7 2.1 fusion.15
  893.2 3.3 fusion.14
  904.1 3.3 fusion.14
  915.1 3.3 fusion.14
  926.0 3.3 fusion.14
  937.0 3.3 fusion.14
  947.9 3.3 fusion.14
  958.9 3.3 fusion.14
  969.8 3.3 fusion.14
  980.8 3.3 fusion.14
  991.7 3.3 fusion.14
  1002.7 3.3 fusion.14
  1013.6 3.3 fusion.14
  1024.5 3.3 fusion.14
  1035.5 3.3 fusion.14
  1046.4 3.3 fusion.14
  1057.4 3.3 fusion.14
  1068.3 3.3 fusion.14
  1079.3 3.3 fusion.14
  1090.2 3.3 fusion.14
  1101.2 3.3 fusion.14
  1110.5 77.0 %reduce-scatter.5.cloned.1.call-done = f32[6,16]{0,1:T(8,128)} async-done(((f32[6,128]{0,1:T(8,128)}), f32[6,16]{0,1:T(8,128)}) %reduce-scatter.5.cloned.1.call-update) | async-done | bytes 400 | tf_op jit(solution)/shard_map/reduce_scatter | solution.py:85
  (261 shorter events, 215.7 us)
Async XLA Ops:
  8.0 721.5 %reduce-scatter.3.cloned.1.call-start = ((), (), s32[]{:S(2)}) async-start(), calls=%async_computation.2 | async-start | bytes 1056768 | tf_op jit(solution)/shard_map/reduce_scatter | solution.py:77
  81.7 11.9 copy-start.5
  81.7 12.0 copy-start.1
  81.7 12.0 copy-start.2
  81.7 12.0 copy-start.3
  81.7 12.0 copy-start.4
  81.7 12.1 %copy-start.6 = (f32[8192]{0:T(1024)S(1)}, f32[8192]{0:T(1024)}, u32[]{:S(2)}) copy-start(f32[8192]{0:T(1024)} %param.13) | copy-start | bytes 98308
  93.6 665.9 %all-gather.3.cloned.1.call-start = ((), (), s32[]{:S(2)}) async-start(), calls=%async_computation.3 | async-start | bytes 4456448 | tf_op jit(solution)/shard_map/all_gather | solution.py:82
  94.7 1092.9 %reduce-scatter.5.cloned.1.call-start = ((), (), s32[]{:S(2)}) async-start(), calls=%async_computation.4 | async-start | bytes 73728 | tf_op jit(solution)/shard_map/reduce_scatter | solution.py:85
  759.5 428.8 %copy-start = (f32[13,16]{0,1:T(8,128)S(1)}, f32[13,16]{0,1:T(8,128)}, u32[]{:S(2)}) copy-start(f32[13,16]{0,1:T(8,128)} %reduce-scatter.3.cloned.1.call-done) | copy-start | bytes 2500
Sparse Core Ops, SparseCore 0:
  93.7 635.7 reduce-scatter.2
  1110.7 76.8 reduce-scatter.4
Sparse Core Ops, SparseCore 1:
  95.8 34.1 all-gather.2
where the time goes:
time: 1200 us
  waiting for transfers between devices  712 us (59%)
  other arithmetic  247 us (21%)
  local copies, waits for them, and re-layouts  104 us (9%)
  blocking collectives  96.6 us (8%)
  loops' own time  22.7 us (2%)
  between operations  15.7 us (1%)
    reduce_scatter x1, waiting for transfers between devices, on_device(): lax.psum_scatter(picked, ('blk', 'group'), scatter_dimension=1, tiled=True)  635 us
    reduce_sum x32, other arithmetic, block_forces(): dist_sq = jnp.sum(offset * offset, axis=0) + softening  105 us
    reduce_scatter x1, waiting for transfers between devices, on_device(): lax.psum_scatter(partial_sum, 'blk', scatter_dimension=1, tiled=True)  77 us
    reduce_sum x32, other arithmetic, block_forces(): accel_part = jnp.sum(offset * weight, axis=2)  68.8 us
    unnamed x1, blocking collectives  68.7 us
    div x32, other arithmetic, block_forces(): factor = 3.0 * jnp.sum(offset * motion, axis=0) / dist_sq  68.7 us
    slice x64, local copies, waits for them, and re-layouts, block_forces(): motion = field_piece[3:6, None, :] - active_data[3:6, :, None]  34.7 us
    slice x32, local copies, waits for them, and re-layouts, block_forces(): weight = field_piece[6][None, :] * inverse * inverse * inverse  31.8 us
  transfers between devices with their start and end apart: 3, of which 2 were waited for; matrix products, arithmetic and copies ran while one was open for 0% of the time, Pallas kernels for 0%

commit v1 on v0

v1 whole, which is shorter than its diff:
```python
import functools

import jax
import jax.numpy as jnp
from jax import lax
from jax.experimental import pallas as pl
from jax.experimental.pallas import tpu as pltpu
from jax.sharding import PartitionSpec as P

softening = 0.001
ALL = ("blk", "group")
LEVELS = (("core", 1, 2), ("x", 2, 4), ("y_lo", 8, 2), ("z", 16, 4), ("y_hi", 64, 2))
SUB = 2


def predict(pos_now, vel_now, acc_now, jerk_now, elapsed):
    pred_pos = pos_now + elapsed * (
        vel_now + elapsed * (0.5 * acc_now + elapsed * (jerk_now / 6.0))
    )
    pred_vel = vel_now + elapsed * (acc_now + elapsed * (0.5 * jerk_now))
    return (pred_pos, pred_vel)


def corrector(owner_rows, forces):
    old_pos = owner_rows[0:3]
    old_vel = owner_rows[3:6]
    old_acc = owner_rows[6:9]
    old_jerk = owner_rows[9:12]
    elapsed = owner_rows[12]
    new_acc = forces[0:3]
    new_jerk = forces[3:6]
    squared = elapsed * elapsed / 12.0
    new_vel = old_vel + 0.5 * elapsed * (old_acc + new_acc) + squared * (old_jerk - new_jerk)
    new_pos = old_pos + 0.5 * elapsed * (old_vel + new_vel) + squared * (old_acc - new_acc)
    return (new_pos, new_vel, new_acc, new_jerk)


def _perm(stride, size, shift, ndev):
    pairs = []
    for d in range(ndev):
        c = (d // stride) % size
        pairs.append((d, d + (((c + shift) % size) - c) * stride))
    return pairs


def _coord(stride, size):
    return (lax.axis_index(ALL) // stride) % size


def gather_level(x, level, ndev):
    _, stride, size = level
    parts = [x] + [lax.ppermute(x, ALL, _perm(stride, size, s, ndev)) for s in range(1, size)]
    stack = jnp.stack(parts, axis=0)
    c = _coord(stride, size)
    order = (c - jnp.arange(size)) % size
    picked = jnp.take(stack, order, axis=0)
    picked = jnp.moveaxis(picked, 0, -2)
    return picked.reshape(x.shape[:-1] + (size * x.shape[-1],))


def reduce_level(x, level, ndev):
    _, stride, size = level
    m = x.shape[-1] // size
    blocks = x.reshape(x.shape[:-1] + (size, m))
    blocks = jnp.moveaxis(blocks, -2, 0)
    c = _coord(stride, size)
    total = jnp.take(blocks, c, axis=0)
    for s in range(1, size):
        piece = jnp.take(blocks, (c + s) % size, axis=0)
        total = total + lax.ppermute(piece, ALL, _perm(stride, size, s, ndev))
    return total


def sum_level(x, level, ndev):
    _, stride, size = level
    total = x
    for s in range(1, size):
        total = total + lax.ppermute(x, ALL, _perm(stride, size, s, ndev))
    return total


def forces_kernel(act_ref, fld_ref, out_ref):
    num_k = act_ref.shape[0]
    num_j = fld_ref.shape[2]
    step_k = 8 * SUB

    def kblock(kb, carry):
        k0 = pl.multiple_of(kb * step_k, step_k)
        acts = []
        for s in range(SUB):
            a = act_ref[pl.ds(k0 + 8 * s, 8), :]
            acts.append([jnp.broadcast_to(a[:, c:c + 1], (8, 128)) for c in range(6)])

        def jstep(jc, accs):
            j0 = pl.multiple_of(jc * 128, 128)
            f = [fld_ref[c, :, pl.ds(j0, 128)] for c in range(7)]
            new = []
            for s in range(SUB):
                ax, ay, az, avx, avy, avz = acts[s]
                dx = f[0] - ax
                dy = f[1] - ay
                dz = f[2] - az
                mx = f[3] - avx
                my = f[4] - avy
                mz = f[5] - avz
                dist_sq = dx * dx + dy * dy + dz * dz + softening
                inverse = lax.rsqrt(dist_sq)
                inv2 = inverse * inverse
                weight = f[6] * inv2 * inverse
                factor = 3.0 * (dx * mx + dy * my + dz * mz) * inv2
                a6 = accs[s]
                new.append((
                    a6[0] + dx * weight,
                    a6[1] + dy * weight,
                    a6[2] + dz * weight,
                    a6[3] + (mx - factor * dx) * weight,
                    a6[4] + (my - factor * dy) * weight,
                    a6[5] + (mz - factor * dz) * weight,
                ))
            return tuple(new)

        zero = jnp.zeros((8, 128), jnp.float32)
        init = tuple(tuple(zero for _ in range(6)) for _ in range(SUB))
        accs = lax.fori_loop(0, num_j // 128, jstep, init, unroll=2)
        for s in range(SUB):
            for c in range(6):
                out_ref[pl.ds(k0 + 8 * s, 8), c:c + 1] = jnp.sum(accs[s][c], axis=1, keepdims=True)
        return carry

    lax.fori_loop(0, num_k // step_k, kblock, 0)


def pair_forces(active_t, field_b):
    num_k = active_t.shape[0]
    return pl.pallas_call(
        forces_kernel,
        out_shape=jax.ShapeDtypeStruct((num_k, 8), jnp.float32),
    )(active_t, field_b)


def on_device(positions, velocities, accelerations, jerk_rates, masses, elapsed_time, active_index):
    ndev = lax.axis_size("blk") * lax.axis_size("group")
    own_stars = positions.shape[1]
    total_stars = own_stars * ndev
    gravity = 1.0 / total_stars
    every_index = active_index
    for level in LEVELS:
        every_index = gather_level(every_index, level, ndev)
    pred_pos, pred_vel = predict(positions, velocities, accelerations, jerk_rates, elapsed_time)
    own_field = jnp.concatenate(
        [pred_pos, pred_vel, masses[None, :], jnp.zeros_like(masses)[None, :]], axis=0
    )
    field_b = jnp.broadcast_to(own_field[:, None, :], (8, 8, own_stars))
    packed = jnp.concatenate(
        [positions, velocities, accelerations, jerk_rates, elapsed_time[None, :]], axis=0
    )
    first_row = lax.axis_index(ALL) * own_stars
    local_row = every_index - first_row
    is_owned = (local_row >= 0) & (local_row < own_stars)
    picked = jnp.take(packed, jnp.clip(local_row, 0, own_stars - 1), axis=1)
    picked = jnp.where(is_owned[None, :], picked, 0.0)
    rows = picked
    for level in LEVELS:
        rows = sum_level(rows, level, ndev)
    act_pos, act_vel = predict(rows[0:3], rows[3:6], rows[6:9], rows[9:12], rows[12])
    num_k = rows.shape[1]
    active_t = jnp.concatenate(
        [act_pos, act_vel, jnp.zeros((2, num_k), jnp.float32)], axis=0
    ).T
    partial = pair_forces(active_t, field_b)[:, 0:6].T
    for level in reversed(LEVELS):
        partial = reduce_level(partial, level, ndev)
    mine = lax.axis_index(ALL) * active_index.shape[0]
    owner_rows = lax.dynamic_slice_in_dim(rows, mine, active_index.shape[0], axis=1)
    return corrector(owner_rows, partial * gravity)


def solution(mesh):
    return jax.shard_map(
        on_device,
        mesh=mesh,
        in_specs=(
            P(None, ALL),
            P(None, ALL),
            P(None, ALL),
            P(None, ALL),
            P(ALL),
            P(ALL),
            P(ALL),
        ),
        out_specs=(
            P(None, ALL),
            P(None, ALL),
            P(None, ALL),
            P(None, ALL),
        ),
        check_vma=False,
    )
```

time: 1200 us -> 260 us (0.22)
  waiting for transfers between devices: 712 us -> 41.2 us
  other arithmetic: 247 us -> 2.7 us
  Pallas kernels: 0 us -> 151 us
  blocking collectives: 96.6 us -> 0 us
  local copies, waits for them, and re-layouts: 104 us -> 22.6 us
  starting transfers between devices: 0.12 us -> 41.6 us
  loops' own time: 22.7 us -> 0 us
  between operations: 15.7 us -> 1.08 us
    reduce_scatter x2 -> x0, waiting for transfers between devices: 712 us -> none  [the longest x1 635 us: on_device(): lax.psum_scatter(picked, ('blk', 'group'), scatter_dimension=1, tiled=True)]
    reduce_sum x64 -> x0, other arithmetic: 173 us -> none  [the longest x32 105 us: block_forces(): dist_sq = jnp.sum(offset * offset, axis=0) + softening]
    pallas_call x0 -> x1, Pallas kernels: none -> 151 us  [pair_forces(): pl.pallas_call(forces_kernel, out_shape=jax.ShapeDtypeStruct((num_k, 8),...]
    unnamed x1 -> x0, blocking collectives: 68.7 us -> none
    div x32 -> x0, other arithmetic: 68.7 us -> none  [block_forces(): factor = 3.0 * jnp.sum(offset * motion, axis=0) / dist_sq]
    slice x96 -> x1, local copies, waits for them, and re-layouts: 66.5 us -> 0.01 us  [on_device(): rows[12]]
    ppermute x0 -> x27, starting transfers between devices: none -> 41.6 us  [the longest x9 15.7 us: reduce_level(): total = total + lax.ppermute(piece, ALL, _perm(stride, size, s, ndev))]
    ppermute x0 -> x27, waiting for transfers between devices: none -> 41.2 us  [the longest x9 21.7 us: sum_level(): total = total + lax.ppermute(x, ALL, _perm(stride, size, s, ndev))]
  transfers between devices with their start and end apart: 3 -> 27, of which waited for: 2 -> 22; matrix products, arithmetic and copies ran while one was open for 0% -> 3% of each run, Pallas kernels for 0% -> 0%
where the time goes in v1:
time: 260 us
  Pallas kernels  151 us (58%)
  starting transfers between devices  41.6 us (16%)
  waiting for transfers between devices  41.2 us (16%)
  local copies, waits for them, and re-layouts  22.6 us (9%)
  other arithmetic  2.7 us (1%)
    pallas_call x1, Pallas kernels, pair_forces(): pl.pallas_call(forces_kernel, out_shape=jax.ShapeDtypeStruct((num_k, 8),...  151 us
    ppermute x9, waiting for transfers between devices, sum_level(): total = total + lax.ppermute(x, ALL, _perm(stride, size, s, ndev))  21.7 us
    ppermute x9, starting transfers between devices, reduce_level(): total = total + lax.ppermute(piece, ALL, _perm(stride, size, s, ndev))  15.7 us
    ppermute x9, starting transfers between devices, gather_level(): lax.ppermute(x, ALL, _perm(stride, size, s, ndev))  13.9 us
    ppermute x9, starting transfers between devices, sum_level(): total = total + lax.ppermute(x, ALL, _perm(stride, size, s, ndev))  12 us
    ppermute x9, waiting for transfers between devices, reduce_level(): total = total + lax.ppermute(piece, ALL, _perm(stride, size, s, ndev))  11.6 us
    gather x2, local copies, waits for them, and re-layouts, on_device(): picked = jnp.take(packed, jnp.clip(local_row, 0, own_stars - 1), axis=1)  7.98 us
    ppermute x9, waiting for transfers between devices, gather_level(): lax.ppermute(x, ALL, _perm(stride, size, s, ndev))  7.85 us
  transfers between devices with their start and end apart: 27, of which 22 were waited for; matrix products, arithmetic and copies ran while one was open for 3% of the time, Pallas kernels for 0%

profile of v1, /device:TPU:1, one launch (start us, length us, event | category | flops | bytes accessed | tf_op | source)
XLA Modules:
  0.0 259.8 jit_solution(881387421505516500)
XLA Ops:
  0.6 1.5 collective-permute-start
  2.3 0.7 collective-permute-done
  3.0 0.7 pad_add_fusion.3
  4.4 2.6 collective-permute-start.3
  8.2 2.7 %collective-permute-done.2 = s32[32]{0:T(128)S(1)} collective-permute-done((s32[32]{0:T(128)S(1)}, s32[32]{0:T(128)S(1)}, u32[]{:S(2)}, u32[]{:S(2)}) %collective-permute-start.2) | collective-permute-done | bytes 160 | tf_op jit(solution)/shard_map/ppermute | solution.py:52
  11.9 1.3 collective-permute-start.4
  13.3 1.0 collective-permute-done.4
  15.0 3.8 %collective-permute-start.7 = (s32[256]{0:T(256)S(1)}, s32[256]{0:T(256)S(1)}, u32[]{:S(2)}, u32[]{:S(2)}) collective-permute-start(s32[256]{0:T(256)S(1)} %fusion.36), channel_id=1, source_target_pairs={{0,48},{1,49},{2,50},{3,51},{4,52},{5,53},{6,54},{7,55},{8,56},{9,... | collective-permute-start | bytes 3080 | tf_op jit(solution)/shard_map/ppermute | solution.py:52
  18.7 0.7 collective-permute-start.5
  19.5 3.2 %collective-permute-done.6 = s32[256]{0:T(256)S(1)} collective-permute-done((s32[256]{0:T(256)S(1)}, s32[256]{0:T(256)S(1)}, u32[]{:S(2)}, u32[]{:S(2)}) %collective-permute-start.6) | collective-permute-done | bytes 1056 | tf_op jit(solution)/shard_map/ppermute | solution.py:52
  23.3 2.9 %collective-permute-start.8 = (s32[1024]{0:T(1024)S(1)}, s32[1024]{0:T(1024)S(1)}, u32[]{:S(2)}, u32[]{:S(2)}) collective-permute-start(s32[1024]{0:T(1024)S(1)} %bitcast.131), channel_id=1, source_target_pairs={{0,64},{1,65},{2,66},{3,67},{4,68},{5,69},{6,70},{7,71},{8,72},{9,... | collective-permute-start | bytes 12296 | tf_op jit(solution)/shard_map/ppermute | solution.py:52
  26.3 4.0 %concatenate.9 = f32[13,8192]{1,0:T(8,128)S(1)} concatenate(f32[3,8192]{1,0:T(4,128)} %param.17, f32[3,8192]{1,0:T(4,128)} %param.18, f32[3,8192]{1,0:T(4,128)} %param.19, f32[3,8192]{1,0:T(4,128)} %param.20, f32[1,8192]{1,0:T(1,128)} %bitcast.114), dimensions={0} | concatenate | bytes 851968 | tf_op jit(solution)/shard_map/concatenate | solution.py:154
  30.4 2.7 %copy.118 = f32[13,8192]{0,1:T(8,128)} copy(f32[13,8192]{1,0:T(8,128)S(1)} %concatenate.9) | data formatting | bytes 851968 | tf_op jit(solution)/shard_map/concatenate | solution.py:154
  33.8 7.6 %gather_fusion.5 = f32[2048,13]{1,0:T(8,128)S(1)} fusion(f32[13,8192]{0,1:T(8,128)} %copy.118, s32[2048]{0:T(1024)S(1)} %broadcast_clamp_fusion), kind=kCustom, calls=%fused_computation.5 | custom fusion | bytes 221184 | tf_op jit(solution)/shard_map/jit(_take)/gather | solution.py:160
  41.9 5.0 %collective-permute-start.9 = (f32[13,2048]{1,0:T(8,128)S(1)}, f32[13,2048]{1,0:T(8,128)S(1)}, u32[]{:S(2)}, u32[]{:S(2)}) collective-permute-start(f32[13,2048]{1,0:T(8,128)S(1)} %select_bitcast_fusion), channel_id=1, source_target_pairs={{0,1},{1,0},{2,3},{3,2},{4,5},{5,4},{6,7},{7,6},{8,9},{9,8},{10,11... | collective-permute-start | bytes 319496 | tf_op jit(solution)/shard_map/ppermute | solution.py:78
  46.8 1.0 collective-permute-done.9
  48.0 1.3 collective-permute-start.11
  49.3 0.8 collective-permute-start.10
  50.0 2.6 collective-permute-done.12
  52.6 1.4 collective-permute-done.11
  54.0 3.8 %collective-permute-done.10 = f32[13,2048]{1,0:T(8,128)S(1)} collective-permute-done((f32[13,2048]{1,0:T(8,128)S(1)}, f32[13,2048]{1,0:T(8,128)S(1)}, u32[]{:S(2)}, u32[]{:S(2)}) %collective-permute-start.10) | collective-permute-done | bytes 106528 | tf_op jit(solution)/shard_map/ppermute | solution.py:78
  58.3 4.1 %collective-permute-done.13 = f32[13,2048]{1,0:T(8,128)S(1)} collective-permute-done((f32[13,2048]{1,0:T(8,128)S(1)}, f32[13,2048]{1,0:T(8,128)S(1)}, u32[]{:S(2)}, u32[]{:S(2)}) %collective-permute-start.13) | collective-permute-done | bytes 106528 | tf_op jit(solution)/shard_map/ppermute | solution.py:78
  62.8 1.6 collective-permute-start.15
  64.4 0.8 collective-permute-start.14
  65.3 1.0 collective-permute-done.16
  66.3 1.8 collective-permute-done.15
  68.1 2.6 collective-permute-done.14
  70.7 1.7 collective-permute-start.17
  72.6 3.5 %collective-permute-done.17 = f32[13,2048]{1,0:T(8,128)S(1)} collective-permute-done((f32[13,2048]{1,0:T(8,128)S(1)}, f32[13,2048]{1,0:T(8,128)S(1)}, u32[]{:S(2)}, u32[]{:S(2)}) %collective-permute-start.17) | collective-permute-done | bytes 106528 | tf_op jit(solution)/shard_map/ppermute | solution.py:78
  76.3 1.3 copy.120
  77.6 1.5 broadcast_in_dim.159.fld_ref
  79.1 150.6 %shard_map.102 = f32[2048,8]{1,0:T(8,128)} custom-call(f32[2048,8]{1,0:T(8,128)} %bitcast.112, f32[8,8,8192]{2,1,0:T(8,128)} %broadcast_in_dim.159.fld_ref), custom_call_target="tpu_custom_call" | custom-call | tf_op jit(solution)/shard_map/pallas_call | solution.py:135
  229.7 1.5 copy.121
  231.3 1.7 collective-permute-start.18
  233.0 2.7 %collective-permute-done.18 = f32[6,1024]{1,0:T(8,128)S(1)} collective-permute-done((f32[6,1024]{1,0:T(8,128)S(1)}, f32[6,1024]{1,0:T(8,128)S(1)}, u32[]{:S(2)}, u32[]{:S(2)}) %collective-permute-start.18) | collective-permute-done | bytes 24608 | tf_op jit(solution)/shard_map/ppermute | solution.py:70
  235.7 0.7 collective-permute-start.21
  236.4 2.2 collective-permute-start.20
  238.6 0.8 collective-permute-start.19
  239.3 1.1 collective-permute-done.20
  240.4 1.9 collective-permute-done.19
  242.8 2.4 collective-permute-done.22
  245.4 1.3 collective-permute-start.24
  246.7 0.8 collective-permute-start.23
  247.8 1.6 collective-permute-done.24
  249.4 1.0 collective-permute-done.23
  250.5 7.8 %collective-permute-start.26 = (f32[6,16]{1,0:T(8,128)S(1)}, f32[6,16]{1,0:T(8,128)S(1)}, u32[]{:S(2)}, u32[]{:S(2)}) collective-permute-start(f32[6,16]{1,0:T(8,128)S(1)} %bitcast.130), channel_id=1, source_target_pairs={{0,1},{1,0},{2,3},{3,2},{4,5},{5,4},{6,7},{7,6},{8,9},{9,8},{10,11... | collective-permute-start | bytes 1160 | tf_op jit(solution)/shard_map/ppermute | solution.py:70
  258.4 0.7 collective-permute-done.26
  259.1 0.7 fusion.16
  (108 shorter events, 8.5 us)
Async XLA Ops:
  0.6 2.4 collective-permute-start
  4.4 3.8 %collective-permute-start.3 = (s32[32]{0:T(128)S(1)}, s32[32]{0:T(128)S(1)}, u32[]{:S(2)}, u32[]{:S(2)}) collective-permute-start(s32[32]{0:T(128)S(1)} %select_n.416), channel_id=1, source_target_pairs={{0,6},{1,7},{2,0},{3,1},{4,2},{5,3},{6,4},{7,5},{8,14},{9,15},{10,... | collective-permute-start | bytes 392 | tf_op jit(solution)/shard_map/ppermute | solution.py:52
  7.0 3.9 %collective-permute-start.2 = (s32[32]{0:T(128)S(1)}, s32[32]{0:T(128)S(1)}, u32[]{:S(2)}, u32[]{:S(2)}) collective-permute-start(s32[32]{0:T(128)S(1)} %select_n.416), channel_id=1, source_target_pairs={{0,4},{1,5},{2,6},{3,7},{4,0},{5,1},{6,2},{7,3},{8,12},{9,13},{10,... | collective-permute-start | bytes 392 | tf_op jit(solution)/shard_map/ppermute | solution.py:52
  7.5 3.6 %collective-permute-start.1 = (s32[32]{0:T(128)S(1)}, s32[32]{0:T(128)S(1)}, u32[]{:S(2)}, u32[]{:S(2)}) collective-permute-start(s32[32]{0:T(128)S(1)} %select_n.416), channel_id=1, source_target_pairs={{0,2},{1,3},{2,4},{3,5},{4,6},{5,7},{6,0},{7,1},{8,10},{9,11},{10,... | collective-permute-start | bytes 392 | tf_op jit(solution)/shard_map/ppermute | solution.py:52
  11.9 2.4 collective-permute-start.4
  15.0 4.5 %collective-permute-start.7 = (s32[256]{0:T(256)S(1)}, s32[256]{0:T(256)S(1)}, u32[]{:S(2)}, u32[]{:S(2)}) collective-permute-start(s32[256]{0:T(256)S(1)} %fusion.36), channel_id=1, source_target_pairs={{0,48},{1,49},{2,50},{3,51},{4,52},{5,53},{6,54},{7,55},{8,56},{9,... | collective-permute-start | bytes 3080 | tf_op jit(solution)/shard_map/ppermute | solution.py:52
  18.7 3.9 %collective-permute-start.6 = (s32[256]{0:T(256)S(1)}, s32[256]{0:T(256)S(1)}, u32[]{:S(2)}, u32[]{:S(2)}) collective-permute-start(s32[256]{0:T(256)S(1)} %fusion.36), channel_id=1, source_target_pairs={{0,32},{1,33},{2,34},{3,35},{4,36},{5,37},{6,38},{7,39},{8,40},{9,... | collective-permute-start | bytes 3080 | tf_op jit(solution)/shard_map/ppermute | solution.py:52
  18.7 3.9 %collective-permute-start.5 = (s32[256]{0:T(256)S(1)}, s32[256]{0:T(256)S(1)}, u32[]{:S(2)}, u32[]{:S(2)}) collective-permute-start(s32[256]{0:T(256)S(1)} %fusion.36), channel_id=1, source_target_pairs={{0,16},{1,17},{2,18},{3,19},{4,20},{5,21},{6,22},{7,23},{8,24},{9,... | collective-permute-start | bytes 3080 | tf_op jit(solution)/shard_map/ppermute | solution.py:52
  23.3 9.7 %collective-permute-start.8 = (s32[1024]{0:T(1024)S(1)}, s32[1024]{0:T(1024)S(1)}, u32[]{:S(2)}, u32[]{:S(2)}) collective-permute-start(s32[1024]{0:T(1024)S(1)} %bitcast.131), channel_id=1, source_target_pairs={{0,64},{1,65},{2,66},{3,67},{4,68},{5,69},{6,70},{7,71},{8,72},{9,... | collective-permute-start | bytes 12296 | tf_op jit(solution)/shard_map/ppermute | solution.py:52
  30.3 27.9 %copy-start.4 = (f32[8192]{0:T(1024)S(1)}, f32[8192]{0:T(1024)}, u32[]{:S(2)}) copy-start(f32[8192]{0:T(1024)} %param.22) | copy-start | bytes 98308
  30.3 34.8 %copy-start = (f32[3,8192]{1,0:T(4,128)S(1)}, f32[3,8192]{1,0:T(4,128)}, u32[]{:S(2)}) copy-start(f32[3,8192]{1,0:T(4,128)} %param.17) | copy-start | bytes 294916
  30.3 34.8 %copy-start.1 = (f32[3,8192]{1,0:T(4,128)S(1)}, f32[3,8192]{1,0:T(4,128)}, u32[]{:S(2)}) copy-start(f32[3,8192]{1,0:T(4,128)} %param.18) | copy-start | bytes 294916
  30.4 34.8 %copy-start.2 = (f32[3,8192]{1,0:T(4,128)S(1)}, f32[3,8192]{1,0:T(4,128)}, u32[]{:S(2)}) copy-start(f32[3,8192]{1,0:T(4,128)} %param.19) | copy-start | bytes 294916
  30.4 34.8 %copy-start.3 = (f32[3,8192]{1,0:T(4,128)S(1)}, f32[3,8192]{1,0:T(4,128)}, u32[]{:S(2)}) copy-start(f32[3,8192]{1,0:T(4,128)} %param.20) | copy-start | bytes 294916
  30.4 42.0 %copy-start.5 = (f32[8192]{0:T(1024)S(1)}, f32[8192]{0:T(1024)}, u32[]{:S(2)}) copy-start(f32[8192]{0:T(1024)} %param.21) | copy-start | bytes 98308
  41.9 6.0 %collective-permute-start.9 = (f32[13,2048]{1,0:T(8,128)S(1)}, f32[13,2048]{1,0:T(8,128)S(1)}, u32[]{:S(2)}, u32[]{:S(2)}) collective-permute-start(f32[13,2048]{1,0:T(8,128)S(1)} %select_bitcast_fusion), channel_id=1, source_target_pairs={{0,1},{1,0},{2,3},{3,2},{4,5},{5,4},{6,7},{7,6},{8,9},{9,8},{10,11... | collective-permute-start | bytes 319496 | tf_op jit(solution)/shard_map/ppermute | solution.py:78
  47.9 4.8 %collective-permute-start.12 = (f32[13,2048]{1,0:T(8,128)S(1)}, f32[13,2048]{1,0:T(8,128)S(1)}, u32[]{:S(2)}, u32[]{:S(2)}) collective-permute-start(f32[13,2048]{1,0:T(8,128)S(1)} %fusion.35), channel_id=1, source_target_pairs={{0,6},{1,7},{2,0},{3,1},{4,2},{5,3},{6,4},{7,5},{8,14},{9,15},{10,... | collective-permute-start | bytes 319496 | tf_op jit(solution)/shard_map/ppermute | solution.py:78
  48.0 6.0 %collective-permute-start.11 = (f32[13,2048]{1,0:T(8,128)S(1)}, f32[13,2048]{1,0:T(8,128)S(1)}, u32[]{:S(2)}, u32[]{:S(2)}) collective-permute-start(f32[13,2048]{1,0:T(8,128)S(1)} %fusion.35), channel_id=1, source_target_pairs={{0,4},{1,5},{2,6},{3,7},{4,0},{5,1},{6,2},{7,3},{8,12},{9,13},{10,... | collective-permute-start | bytes 319496 | tf_op jit(solution)/shard_map/ppermute | solution.py:78
  49.3 8.5 %collective-permute-start.10 = (f32[13,2048]{1,0:T(8,128)S(1)}, f32[13,2048]{1,0:T(8,128)S(1)}, u32[]{:S(2)}, u32[]{:S(2)}) collective-permute-start(f32[13,2048]{1,0:T(8,128)S(1)} %fusion.35), channel_id=1, source_target_pairs={{0,2},{1,3},{2,4},{3,5},{4,6},{5,7},{6,0},{7,1},{8,10},{9,11},{10,... | collective-permute-start | bytes 319496 | tf_op jit(solution)/shard_map/ppermute | solution.py:78
  57.8 4.6 %collective-permute-start.13 = (f32[13,2048]{1,0:T(8,128)S(1)}, f32[13,2048]{1,0:T(8,128)S(1)}, u32[]{:S(2)}, u32[]{:S(2)}) collective-permute-start(f32[13,2048]{1,0:T(8,128)S(1)} %add_add_fusion.1), channel_id=1, source_target_pairs={{0,8},{1,9},{2,10},{3,11},{4,12},{5,13},{6,14},{7,15},{8,0},{9,1},... | collective-permute-start | bytes 319496 | tf_op jit(solution)/shard_map/ppermute | solution.py:78
  62.4 3.9 %collective-permute-start.16 = (f32[13,2048]{1,0:T(8,128)S(1)}, f32[13,2048]{1,0:T(8,128)S(1)}, u32[]{:S(2)}, u32[]{:S(2)}) collective-permute-start(f32[13,2048]{1,0:T(8,128)S(1)} %add.417), channel_id=1, source_target_pairs={{0,48},{1,49},{2,50},{3,51},{4,52},{5,53},{6,54},{7,55},{8,56},{9,... | collective-permute-start | bytes 319496 | tf_op jit(solution)/shard_map/ppermute | solution.py:78
  62.8 5.3 %collective-permute-start.15 = (f32[13,2048]{1,0:T(8,128)S(1)}, f32[13,2048]{1,0:T(8,128)S(1)}, u32[]{:S(2)}, u32[]{:S(2)}) collective-permute-start(f32[13,2048]{1,0:T(8,128)S(1)} %add.417), channel_id=1, source_target_pairs={{0,32},{1,33},{2,34},{3,35},{4,36},{5,37},{6,38},{7,39},{8,40},{9,... | collective-permute-start | bytes 319496 | tf_op jit(solution)/shard_map/ppermute | solution.py:78
  64.4 6.3 %collective-permute-start.14 = (f32[13,2048]{1,0:T(8,128)S(1)}, f32[13,2048]{1,0:T(8,128)S(1)}, u32[]{:S(2)}, u32[]{:S(2)}) collective-permute-start(f32[13,2048]{1,0:T(8,128)S(1)} %add.417), channel_id=1, source_target_pairs={{0,16},{1,17},{2,18},{3,19},{4,20},{5,21},{6,22},{7,23},{8,24},{9,... | collective-permute-start | bytes 319496 | tf_op jit(solution)/shard_map/ppermute | solution.py:78
  70.7 5.4 %collective-permute-start.17 = (f32[13,2048]{1,0:T(8,128)S(1)}, f32[13,2048]{1,0:T(8,128)S(1)}, u32[]{:S(2)}, u32[]{:S(2)}) collective-permute-start(f32[13,2048]{1,0:T(8,128)S(1)} %add_add_fusion), channel_id=1, source_target_pairs={{0,64},{1,65},{2,66},{3,67},{4,68},{5,69},{6,70},{7,71},{8,72},{9,... | collective-permute-start | bytes 319496 | tf_op jit(solution)/shard_map/ppermute | solution.py:78
  231.3 4.3 %collective-permute-start.18 = (f32[6,1024]{1,0:T(8,128)S(1)}, f32[6,1024]{1,0:T(8,128)S(1)}, u32[]{:S(2)}, u32[]{:S(2)}) collective-permute-start(f32[6,1024]{1,0:T(8,128)S(1)} %select_bitcast_fusion.1), channel_id=1, source_target_pairs={{0,64},{1,65},{2,66},{3,67},{4,68},{5,69},{6,70},{7,71},{8,72},{9,... | collective-permute-start | bytes 73736 | tf_op jit(solution)/shard_map/ppermute | solution.py:70
  235.7 3.6 %collective-permute-start.21 = (f32[6,256]{1,0:T(8,128)S(1)}, f32[6,256]{1,0:T(8,128)S(1)}, u32[]{:S(2)}, u32[]{:S(2)}) collective-permute-start(f32[6,256]{1,0:T(8,128)S(1)} %bitcast.127), channel_id=1, source_target_pairs={{0,48},{1,49},{2,50},{3,51},{4,52},{5,53},{6,54},{7,55},{8,56},{9,... | collective-permute-start | bytes 18440 | tf_op jit(solution)/shard_map/ppermute | solution.py:70
  236.4 4.0 %collective-permute-start.20 = (f32[6,256]{1,0:T(8,128)S(1)}, f32[6,256]{1,0:T(8,128)S(1)}, u32[]{:S(2)}, u32[]{:S(2)}) collective-permute-start(f32[6,256]{1,0:T(8,128)S(1)} %fusion), channel_id=1, source_target_pairs={{0,32},{1,33},{2,34},{3,35},{4,36},{5,37},{6,38},{7,39},{8,40},{9,... | collective-permute-start | bytes 18440 | tf_op jit(solution)/shard_map/ppermute | solution.py:70
  238.6 3.7 %collective-permute-start.19 = (f32[6,256]{1,0:T(8,128)S(1)}, f32[6,256]{1,0:T(8,128)S(1)}, u32[]{:S(2)}, u32[]{:S(2)}) collective-permute-start(f32[6,256]{1,0:T(8,128)S(1)} %fusion.1), channel_id=1, source_target_pairs={{0,16},{1,17},{2,18},{3,19},{4,20},{5,21},{6,22},{7,23},{8,24},{9,... | collective-permute-start | bytes 18440 | tf_op jit(solution)/shard_map/ppermute | solution.py:70
  242.3 2.8 %collective-permute-start.22 = (f32[6,128]{1,0:T(8,128)S(1)}, f32[6,128]{1,0:T(8,128)S(1)}, u32[]{:S(2)}, u32[]{:S(2)}) collective-permute-start(f32[6,128]{1,0:T(8,128)S(1)} %bitcast.128), channel_id=1, source_target_pairs={{0,8},{1,9},{2,10},{3,11},{4,12},{5,13},{6,14},{7,15},{8,0},{9,1},... | collective-permute-start | bytes 9224 | tf_op jit(solution)/shard_map/ppermute | solution.py:70
  245.3 2.5 collective-permute-start.25
  245.4 4.0 %collective-permute-start.24 = (f32[6,32]{1,0:T(8,128)S(1)}, f32[6,32]{1,0:T(8,128)S(1)}, u32[]{:S(2)}, u32[]{:S(2)}) collective-permute-start(f32[6,32]{1,0:T(8,128)S(1)} %fusion.6), channel_id=1, source_target_pairs={{0,4},{1,5},{2,6},{3,7},{4,0},{5,1},{6,2},{7,3},{8,12},{9,13},{10,... | collective-permute-start | bytes 2312 | tf_op jit(solution)/shard_map/ppermute | solution.py:70
  246.7 3.7 %collective-permute-start.23 = (f32[6,32]{1,0:T(8,128)S(1)}, f32[6,32]{1,0:T(8,128)S(1)}, u32[]{:S(2)}, u32[]{:S(2)}) collective-permute-start(f32[6,32]{1,0:T(8,128)S(1)} %fusion.7), channel_id=1, source_target_pairs={{0,2},{1,3},{2,4},{3,5},{4,6},{5,7},{6,0},{7,1},{8,10},{9,11},{10,... | collective-permute-start | bytes 2312 | tf_op jit(solution)/shard_map/ppermute | solution.py:70
  250.5 8.6 %collective-permute-start.26 = (f32[6,16]{1,0:T(8,128)S(1)}, f32[6,16]{1,0:T(8,128)S(1)}, u32[]{:S(2)}, u32[]{:S(2)}) collective-permute-start(f32[6,16]{1,0:T(8,128)S(1)} %bitcast.130), channel_id=1, source_target_pairs={{0,1},{1,0},{2,3},{3,2},{4,5},{5,4},{6,7},{7,6},{8,9},{9,8},{10,11... | collective-permute-start | bytes 1160 | tf_op jit(solution)/shard_map/ppermute | solution.py:70

commit v2 on v1

--- a/solution.py
+++ b/solution.py
@@ -121,7 +121,7 @@
 
         zero = jnp.zeros((8, 128), jnp.float32)
         init = tuple(tuple(zero for _ in range(6)) for _ in range(SUB))
-        accs = lax.fori_loop(0, num_j // 128, jstep, init, unroll=2)
+        accs = lax.fori_loop(0, num_j // 128, jstep, init, unroll=8)
         for s in range(SUB):
             for c in range(6):
                 out_ref[pl.ds(k0 + 8 * s, 8), c:c + 1] = jnp.sum(accs[s][c], axis=1, keepdims=True)

time: 260 us -> 231 us (0.89)
  Pallas kernels: 151 us -> 121 us
    pallas_call x1, Pallas kernels: 151 us -> 121 us  [pair_forces(): pl.pallas_call(forces_kernel, out_shape=jax.ShapeDtypeStruct((num_k, 8),...]
where the time goes in v2:
time: 231 us; the launch traced here: 230 us
  Pallas kernels  121 us (52%)
  starting transfers between devices  41.7 us (18%)
  waiting for transfers between devices  41.1 us (18%)
  local copies, waits for them, and re-layouts  22.6 us (10%)
  other arithmetic  2.7 us (1%)
    pallas_call x1, Pallas kernels, pair_forces(): pl.pallas_call(forces_kernel, out_shape=jax.ShapeDtypeStruct((num_k, 8),...  121 us
    ppermute x9, waiting for transfers between devices, sum_level(): total = total + lax.ppermute(x, ALL, _perm(stride, size, s, ndev))  21.7 us
    ppermute x9, starting transfers between devices, reduce_level(): total = total + lax.ppermute(piece, ALL, _perm(stride, size, s, ndev))  15.8 us
    ppermute x9, starting transfers between devices, gather_level(): lax.ppermute(x, ALL, _perm(stride, size, s, ndev))  13.9 us
    ppermute x9, starting transfers between devices, sum_level(): total = total + lax.ppermute(x, ALL, _perm(stride, size, s, ndev))  12 us
    ppermute x9, waiting for transfers between devices, reduce_level(): total = total + lax.ppermute(piece, ALL, _perm(stride, size, s, ndev))  11.6 us
    gather x2, local copies, waits for them, and re-layouts, on_device(): picked = jnp.take(packed, jnp.clip(local_row, 0, own_stars - 1), axis=1)  7.98 us
    ppermute x9, waiting for transfers between devices, gather_level(): lax.ppermute(x, ALL, _perm(stride, size, s, ndev))  7.85 us
  transfers between devices with their start and end apart: 27, of which 22 were waited for; matrix products, arithmetic and copies ran while one was open for 3% of the time, Pallas kernels for 0%

profile of v2, /device:TPU:1, one launch (start us, length us, event | category | flops | bytes accessed | tf_op | source)
XLA Modules:
  0.0 230.2 jit_solution(3715149560576579933)
XLA Ops:
  0.6 1.5 collective-permute-start
  2.3 0.7 collective-permute-done
  3.0 0.7 pad_add_fusion.3
  4.4 2.6 %collective-permute-start.3 = (s32[32]{0:T(128)S(1)}, s32[32]{0:T(128)S(1)}, u32[]{:S(2)}, u32[]{:S(2)}) collective-permute-start(s32[32]{0:T(128)S(1)} %select_n.416), channel_id=1, source_target_pairs={{0,6},{1,7},{2,0},{3,1},{4,2},{5,3},{6,4},{7,5},{8,14},{9,15},{10,... | collective-permute-start | bytes 392 | tf_op jit(solution)/shard_map/ppermute | solution.py:52
  8.2 2.7 %collective-permute-done.2 = s32[32]{0:T(128)S(1)} collective-permute-done((s32[32]{0:T(128)S(1)}, s32[32]{0:T(128)S(1)}, u32[]{:S(2)}, u32[]{:S(2)}) %collective-permute-start.2) | collective-permute-done | bytes 160 | tf_op jit(solution)/shard_map/ppermute | solution.py:52
  11.9 1.3 collective-permute-start.4
  13.3 1.0 collective-permute-done.4
  15.0 3.8 %collective-permute-start.7 = (s32[256]{0:T(256)S(1)}, s32[256]{0:T(256)S(1)}, u32[]{:S(2)}, u32[]{:S(2)}) collective-permute-start(s32[256]{0:T(256)S(1)} %fusion.36), channel_id=1, source_target_pairs={{0,48},{1,49},{2,50},{3,51},{4,52},{5,53},{6,54},{7,55},{8,56},{9,... | collective-permute-start | bytes 3080 | tf_op jit(solution)/shard_map/ppermute | solution.py:52
  18.7 0.7 collective-permute-start.5
  19.5 3.2 %collective-permute-done.6 = s32[256]{0:T(256)S(1)} collective-permute-done((s32[256]{0:T(256)S(1)}, s32[256]{0:T(256)S(1)}, u32[]{:S(2)}, u32[]{:S(2)}) %collective-permute-start.6) | collective-permute-done | bytes 1056 | tf_op jit(solution)/shard_map/ppermute | solution.py:52
  23.3 2.9 %collective-permute-start.8 = (s32[1024]{0:T(1024)S(1)}, s32[1024]{0:T(1024)S(1)}, u32[]{:S(2)}, u32[]{:S(2)}) collective-permute-start(s32[1024]{0:T(1024)S(1)} %bitcast.131), channel_id=1, source_target_pairs={{0,64},{1,65},{2,66},{3,67},{4,68},{5,69},{6,70},{7,71},{8,72},{9,... | collective-permute-start | bytes 12296 | tf_op jit(solution)/shard_map/ppermute | solution.py:52
  26.3 4.0 %concatenate.9 = f32[13,8192]{1,0:T(8,128)S(1)} concatenate(f32[3,8192]{1,0:T(4,128)} %param.17, f32[3,8192]{1,0:T(4,128)} %param.18, f32[3,8192]{1,0:T(4,128)} %param.19, f32[3,8192]{1,0:T(4,128)} %param.20, f32[1,8192]{1,0:T(1,128)} %bitcast.114), dimensions={0} | concatenate | bytes 851968 | tf_op jit(solution)/shard_map/concatenate | solution.py:154
  30.4 2.7 %copy.118 = f32[13,8192]{0,1:T(8,128)} copy(f32[13,8192]{1,0:T(8,128)S(1)} %concatenate.9) | data formatting | bytes 851968 | tf_op jit(solution)/shard_map/concatenate | solution.py:154
  33.8 7.6 %gather_fusion.5 = f32[2048,13]{1,0:T(8,128)S(1)} fusion(f32[13,8192]{0,1:T(8,128)} %copy.118, s32[2048]{0:T(1024)S(1)} %broadcast_clamp_fusion), kind=kCustom, calls=%fused_computation.5 | custom fusion | bytes 221184 | tf_op jit(solution)/shard_map/jit(_take)/gather | solution.py:160
  41.9 5.0 %collective-permute-start.9 = (f32[13,2048]{1,0:T(8,128)S(1)}, f32[13,2048]{1,0:T(8,128)S(1)}, u32[]{:S(2)}, u32[]{:S(2)}) collective-permute-start(f32[13,2048]{1,0:T(8,128)S(1)} %select_bitcast_fusion), channel_id=1, source_target_pairs={{0,1},{1,0},{2,3},{3,2},{4,5},{5,4},{6,7},{7,6},{8,9},{9,8},{10,11... | collective-permute-start | bytes 319496 | tf_op jit(solution)/shard_map/ppermute | solution.py:78
  46.8 1.0 collective-permute-done.9
  48.0 1.3 collective-permute-start.11
  49.3 0.8 collective-permute-start.10
  50.0 2.6 %collective-permute-done.12 = f32[13,2048]{1,0:T(8,128)S(1)} collective-permute-done((f32[13,2048]{1,0:T(8,128)S(1)}, f32[13,2048]{1,0:T(8,128)S(1)}, u32[]{:S(2)}, u32[]{:S(2)}) %collective-permute-start.12) | collective-permute-done | bytes 106528 | tf_op jit(solution)/shard_map/ppermute | solution.py:78
  52.6 1.4 collective-permute-done.11
  54.0 3.8 %collective-permute-done.10 = f32[13,2048]{1,0:T(8,128)S(1)} collective-permute-done((f32[13,2048]{1,0:T(8,128)S(1)}, f32[13,2048]{1,0:T(8,128)S(1)}, u32[]{:S(2)}, u32[]{:S(2)}) %collective-permute-start.10) | collective-permute-done | bytes 106528 | tf_op jit(solution)/shard_map/ppermute | solution.py:78
  58.3 4.1 %collective-permute-done.13 = f32[13,2048]{1,0:T(8,128)S(1)} collective-permute-done((f32[13,2048]{1,0:T(8,128)S(1)}, f32[13,2048]{1,0:T(8,128)S(1)}, u32[]{:S(2)}, u32[]{:S(2)}) %collective-permute-start.13) | collective-permute-done | bytes 106528 | tf_op jit(solution)/shard_map/ppermute | solution.py:78
  62.8 1.5 collective-permute-start.15
  64.4 0.8 collective-permute-start.14
  65.3 1.0 collective-permute-done.16
  66.3 1.8 collective-permute-done.15
  68.1 2.6 %collective-permute-done.14 = f32[13,2048]{1,0:T(8,128)S(1)} collective-permute-done((f32[13,2048]{1,0:T(8,128)S(1)}, f32[13,2048]{1,0:T(8,128)S(1)}, u32[]{:S(2)}, u32[]{:S(2)}) %collective-permute-start.14) | collective-permute-done | bytes 106528 | tf_op jit(solution)/shard_map/ppermute | solution.py:78
  70.7 1.7 collective-permute-start.17
  72.6 3.5 %collective-permute-done.17 = f32[13,2048]{1,0:T(8,128)S(1)} collective-permute-done((f32[13,2048]{1,0:T(8,128)S(1)}, f32[13,2048]{1,0:T(8,128)S(1)}, u32[]{:S(2)}, u32[]{:S(2)}) %collective-permute-start.17) | collective-permute-done | bytes 106528 | tf_op jit(solution)/shard_map/ppermute | solution.py:78
  76.3 1.3 copy.120
  77.6 1.5 broadcast_in_dim.159.fld_ref
  79.1 121.0 %shard_map.102 = f32[2048,8]{1,0:T(8,128)} custom-call(f32[2048,8]{1,0:T(8,128)} %bitcast.112, f32[8,8,8192]{2,1,0:T(8,128)} %broadcast_in_dim.159.fld_ref), custom_call_target="tpu_custom_call" | custom-call | tf_op jit(solution)/shard_map/pallas_call | solution.py:135
  200.1 1.5 copy.121
  201.7 1.7 collective-permute-start.18
  203.4 2.6 %collective-permute-done.18 = f32[6,1024]{1,0:T(8,128)S(1)} collective-permute-done((f32[6,1024]{1,0:T(8,128)S(1)}, f32[6,1024]{1,0:T(8,128)S(1)}, u32[]{:S(2)}, u32[]{:S(2)}) %collective-permute-start.18) | collective-permute-done | bytes 24608 | tf_op jit(solution)/shard_map/ppermute | solution.py:70
  206.1 0.7 collective-permute-start.21
  206.8 2.2 collective-permute-start.20
  208.9 0.8 collective-permute-start.19
  209.7 1.1 collective-permute-done.20
  210.8 1.9 collective-permute-done.19
  213.2 2.3 %collective-permute-done.22 = f32[6,128]{1,0:T(8,128)S(1)} collective-permute-done((f32[6,128]{1,0:T(8,128)S(1)}, f32[6,128]{1,0:T(8,128)S(1)}, u32[]{:S(2)}, u32[]{:S(2)}) %collective-permute-start.22) | collective-permute-done | bytes 3104 | tf_op jit(solution)/shard_map/ppermute | solution.py:70
  215.8 1.3 collective-permute-start.24
  217.1 0.8 collective-permute-start.23
  218.2 1.6 collective-permute-done.24
  219.8 1.0 collective-permute-done.23
  220.9 7.8 %collective-permute-start.26 = (f32[6,16]{1,0:T(8,128)S(1)}, f32[6,16]{1,0:T(8,128)S(1)}, u32[]{:S(2)}, u32[]{:S(2)}) collective-permute-start(f32[6,16]{1,0:T(8,128)S(1)} %bitcast.130), channel_id=1, source_target_pairs={{0,1},{1,0},{2,3},{3,2},{4,5},{5,4},{6,7},{7,6},{8,9},{9,8},{10,11... | collective-permute-start | bytes 1160 | tf_op jit(solution)/shard_map/ppermute | solution.py:70
  228.8 0.7 collective-permute-done.26
  229.5 0.7 fusion.16
  (108 shorter events, 8.5 us)
Async XLA Ops:
  0.6 2.4 %collective-permute-start = (s32[16]{0:T(128)}, s32[16]{0:T(128)S(1)}, u32[]{:S(2)}, u32[]{:S(2)}) collective-permute-start(s32[16]{0:T(128)} %param.23), channel_id=1, source_target_pairs={{0,1},{1,0},{2,3},{3,2},{4,5},{5,4},{6,7},{7,6},{8,9},{9,8},{10,11... | collective-permute-start | bytes 200 | tf_op jit(solution)/shard_map/ppermute | solution.py:52
  4.4 3.8 %collective-permute-start.3 = (s32[32]{0:T(128)S(1)}, s32[32]{0:T(128)S(1)}, u32[]{:S(2)}, u32[]{:S(2)}) collective-permute-start(s32[32]{0:T(128)S(1)} %select_n.416), channel_id=1, source_target_pairs={{0,6},{1,7},{2,0},{3,1},{4,2},{5,3},{6,4},{7,5},{8,14},{9,15},{10,... | collective-permute-start | bytes 392 | tf_op jit(solution)/shard_map/ppermute | solution.py:52
  7.0 3.9 %collective-permute-start.2 = (s32[32]{0:T(128)S(1)}, s32[32]{0:T(128)S(1)}, u32[]{:S(2)}, u32[]{:S(2)}) collective-permute-start(s32[32]{0:T(128)S(1)} %select_n.416), channel_id=1, source_target_pairs={{0,4},{1,5},{2,6},{3,7},{4,0},{5,1},{6,2},{7,3},{8,12},{9,13},{10,... | collective-permute-start | bytes 392 | tf_op jit(solution)/shard_map/ppermute | solution.py:52
  7.5 3.6 %collective-permute-start.1 = (s32[32]{0:T(128)S(1)}, s32[32]{0:T(128)S(1)}, u32[]{:S(2)}, u32[]{:S(2)}) collective-permute-start(s32[32]{0:T(128)S(1)} %select_n.416), channel_id=1, source_target_pairs={{0,2},{1,3},{2,4},{3,5},{4,6},{5,7},{6,0},{7,1},{8,10},{9,11},{10,... | collective-permute-start | bytes 392 | tf_op jit(solution)/shard_map/ppermute | solution.py:52
  11.9 2.4 %collective-permute-start.4 = (s32[128]{0:T(128)S(1)}, s32[128]{0:T(128)S(1)}, u32[]{:S(2)}, u32[]{:S(2)}) collective-permute-start(s32[128]{0:T(128)S(1)} %select_n.421), channel_id=1, source_target_pairs={{0,8},{1,9},{2,10},{3,11},{4,12},{5,13},{6,14},{7,15},{8,0},{9,1},... | collective-permute-start | bytes 1544 | tf_op jit(solution)/shard_map/ppermute | solution.py:52
  15.0 4.5 %collective-permute-start.7 = (s32[256]{0:T(256)S(1)}, s32[256]{0:T(256)S(1)}, u32[]{:S(2)}, u32[]{:S(2)}) collective-permute-start(s32[256]{0:T(256)S(1)} %fusion.36), channel_id=1, source_target_pairs={{0,48},{1,49},{2,50},{3,51},{4,52},{5,53},{6,54},{7,55},{8,56},{9,... | collective-permute-start | bytes 3080 | tf_op jit(solution)/shard_map/ppermute | solution.py:52
  18.7 3.9 %collective-permute-start.6 = (s32[256]{0:T(256)S(1)}, s32[256]{0:T(256)S(1)}, u32[]{:S(2)}, u32[]{:S(2)}) collective-permute-start(s32[256]{0:T(256)S(1)} %fusion.36), channel_id=1, source_target_pairs={{0,32},{1,33},{2,34},{3,35},{4,36},{5,37},{6,38},{7,39},{8,40},{9,... | collective-permute-start | bytes 3080 | tf_op jit(solution)/shard_map/ppermute | solution.py:52
  18.7 3.9 %collective-permute-start.5 = (s32[256]{0:T(256)S(1)}, s32[256]{0:T(256)S(1)}, u32[]{:S(2)}, u32[]{:S(2)}) collective-permute-start(s32[256]{0:T(256)S(1)} %fusion.36), channel_id=1, source_target_pairs={{0,16},{1,17},{2,18},{3,19},{4,20},{5,21},{6,22},{7,23},{8,24},{9,... | collective-permute-start | bytes 3080 | tf_op jit(solution)/shard_map/ppermute | solution.py:52
  23.3 9.7 %collective-permute-start.8 = (s32[1024]{0:T(1024)S(1)}, s32[1024]{0:T(1024)S(1)}, u32[]{:S(2)}, u32[]{:S(2)}) collective-permute-start(s32[1024]{0:T(1024)S(1)} %bitcast.131), channel_id=1, source_target_pairs={{0,64},{1,65},{2,66},{3,67},{4,68},{5,69},{6,70},{7,71},{8,72},{9,... | collective-permute-start | bytes 12296 | tf_op jit(solution)/shard_map/ppermute | solution.py:52
  30.3 27.9 %copy-start.4 = (f32[8192]{0:T(1024)S(1)}, f32[8192]{0:T(1024)}, u32[]{:S(2)}) copy-start(f32[8192]{0:T(1024)} %param.22) | copy-start | bytes 98308
  30.3 34.8 %copy-start = (f32[3,8192]{1,0:T(4,128)S(1)}, f32[3,8192]{1,0:T(4,128)}, u32[]{:S(2)}) copy-start(f32[3,8192]{1,0:T(4,128)} %param.17) | copy-start | bytes 294916
  30.3 34.8 %copy-start.1 = (f32[3,8192]{1,0:T(4,128)S(1)}, f32[3,8192]{1,0:T(4,128)}, u32[]{:S(2)}) copy-start(f32[3,8192]{1,0:T(4,128)} %param.18) | copy-start | bytes 294916
  30.4 34.8 %copy-start.2 = (f32[3,8192]{1,0:T(4,128)S(1)}, f32[3,8192]{1,0:T(4,128)}, u32[]{:S(2)}) copy-start(f32[3,8192]{1,0:T(4,128)} %param.19) | copy-start | bytes 294916
  30.4 34.8 %copy-start.3 = (f32[3,8192]{1,0:T(4,128)S(1)}, f32[3,8192]{1,0:T(4,128)}, u32[]{:S(2)}) copy-start(f32[3,8192]{1,0:T(4,128)} %param.20) | copy-start | bytes 294916
  30.4 42.1 %copy-start.5 = (f32[8192]{0:T(1024)S(1)}, f32[8192]{0:T(1024)}, u32[]{:S(2)}) copy-start(f32[8192]{0:T(1024)} %param.21) | copy-start | bytes 98308
  41.9 6.0 %collective-permute-start.9 = (f32[13,2048]{1,0:T(8,128)S(1)}, f32[13,2048]{1,0:T(8,128)S(1)}, u32[]{:S(2)}, u32[]{:S(2)}) collective-permute-start(f32[13,2048]{1,0:T(8,128)S(1)} %select_bitcast_fusion), channel_id=1, source_target_pairs={{0,1},{1,0},{2,3},{3,2},{4,5},{5,4},{6,7},{7,6},{8,9},{9,8},{10,11... | collective-permute-start | bytes 319496 | tf_op jit(solution)/shard_map/ppermute | solution.py:78
  47.9 4.8 %collective-permute-start.12 = (f32[13,2048]{1,0:T(8,128)S(1)}, f32[13,2048]{1,0:T(8,128)S(1)}, u32[]{:S(2)}, u32[]{:S(2)}) collective-permute-start(f32[13,2048]{1,0:T(8,128)S(1)} %fusion.35), channel_id=1, source_target_pairs={{0,6},{1,7},{2,0},{3,1},{4,2},{5,3},{6,4},{7,5},{8,14},{9,15},{10,... | collective-permute-start | bytes 319496 | tf_op jit(solution)/shard_map/ppermute | solution.py:78
  48.0 6.0 %collective-permute-start.11 = (f32[13,2048]{1,0:T(8,128)S(1)}, f32[13,2048]{1,0:T(8,128)S(1)}, u32[]{:S(2)}, u32[]{:S(2)}) collective-permute-start(f32[13,2048]{1,0:T(8,128)S(1)} %fusion.35), channel_id=1, source_target_pairs={{0,4},{1,5},{2,6},{3,7},{4,0},{5,1},{6,2},{7,3},{8,12},{9,13},{10,... | collective-permute-start | bytes 319496 | tf_op jit(solution)/shard_map/ppermute | solution.py:78
  49.3 8.5 %collective-permute-start.10 = (f32[13,2048]{1,0:T(8,128)S(1)}, f32[13,2048]{1,0:T(8,128)S(1)}, u32[]{:S(2)}, u32[]{:S(2)}) collective-permute-start(f32[13,2048]{1,0:T(8,128)S(1)} %fusion.35), channel_id=1, source_target_pairs={{0,2},{1,3},{2,4},{3,5},{4,6},{5,7},{6,0},{7,1},{8,10},{9,11},{10,... | collective-permute-start | bytes 319496 | tf_op jit(solution)/shard_map/ppermute | solution.py:78
  57.8 4.6 %collective-permute-start.13 = (f32[13,2048]{1,0:T(8,128)S(1)}, f32[13,2048]{1,0:T(8,128)S(1)}, u32[]{:S(2)}, u32[]{:S(2)}) collective-permute-start(f32[13,2048]{1,0:T(8,128)S(1)} %add_add_fusion.1), channel_id=1, source_target_pairs={{0,8},{1,9},{2,10},{3,11},{4,12},{5,13},{6,14},{7,15},{8,0},{9,1},... | collective-permute-start | bytes 319496 | tf_op jit(solution)/shard_map/ppermute | solution.py:78
  62.4 3.9 %collective-permute-start.16 = (f32[13,2048]{1,0:T(8,128)S(1)}, f32[13,2048]{1,0:T(8,128)S(1)}, u32[]{:S(2)}, u32[]{:S(2)}) collective-permute-start(f32[13,2048]{1,0:T(8,128)S(1)} %add.417), channel_id=1, source_target_pairs={{0,48},{1,49},{2,50},{3,51},{4,52},{5,53},{6,54},{7,55},{8,56},{9,... | collective-permute-start | bytes 319496 | tf_op jit(solution)/shard_map/ppermute | solution.py:78
  62.8 5.3 %collective-permute-start.15 = (f32[13,2048]{1,0:T(8,128)S(1)}, f32[13,2048]{1,0:T(8,128)S(1)}, u32[]{:S(2)}, u32[]{:S(2)}) collective-permute-start(f32[13,2048]{1,0:T(8,128)S(1)} %add.417), channel_id=1, source_target_pairs={{0,32},{1,33},{2,34},{3,35},{4,36},{5,37},{6,38},{7,39},{8,40},{9,... | collective-permute-start | bytes 319496 | tf_op jit(solution)/shard_map/ppermute | solution.py:78
  64.4 6.3 %collective-permute-start.14 = (f32[13,2048]{1,0:T(8,128)S(1)}, f32[13,2048]{1,0:T(8,128)S(1)}, u32[]{:S(2)}, u32[]{:S(2)}) collective-permute-start(f32[13,2048]{1,0:T(8,128)S(1)} %add.417), channel_id=1, source_target_pairs={{0,16},{1,17},{2,18},{3,19},{4,20},{5,21},{6,22},{7,23},{8,24},{9,... | collective-permute-start | bytes 319496 | tf_op jit(solution)/shard_map/ppermute | solution.py:78
  70.7 5.4 %collective-permute-start.17 = (f32[13,2048]{1,0:T(8,128)S(1)}, f32[13,2048]{1,0:T(8,128)S(1)}, u32[]{:S(2)}, u32[]{:S(2)}) collective-permute-start(f32[13,2048]{1,0:T(8,128)S(1)} %add_add_fusion), channel_id=1, source_target_pairs={{0,64},{1,65},{2,66},{3,67},{4,68},{5,69},{6,70},{7,71},{8,72},{9,... | collective-permute-start | bytes 319496 | tf_op jit(solution)/shard_map/ppermute | solution.py:78
  201.7 4.3 %collective-permute-start.18 = (f32[6,1024]{1,0:T(8,128)S(1)}, f32[6,1024]{1,0:T(8,128)S(1)}, u32[]{:S(2)}, u32[]{:S(2)}) collective-permute-start(f32[6,1024]{1,0:T(8,128)S(1)} %select_bitcast_fusion.1), channel_id=1, source_target_pairs={{0,64},{1,65},{2,66},{3,67},{4,68},{5,69},{6,70},{7,71},{8,72},{9,... | collective-permute-start | bytes 73736 | tf_op jit(solution)/shard_map/ppermute | solution.py:70
  206.1 3.6 %collective-permute-start.21 = (f32[6,256]{1,0:T(8,128)S(1)}, f32[6,256]{1,0:T(8,128)S(1)}, u32[]{:S(2)}, u32[]{:S(2)}) collective-permute-start(f32[6,256]{1,0:T(8,128)S(1)} %bitcast.127), channel_id=1, source_target_pairs={{0,48},{1,49},{2,50},{3,51},{4,52},{5,53},{6,54},{7,55},{8,56},{9,... | collective-permute-start | bytes 18440 | tf_op jit(solution)/shard_map/ppermute | solution.py:70
  206.8 4.0 %collective-permute-start.20 = (f32[6,256]{1,0:T(8,128)S(1)}, f32[6,256]{1,0:T(8,128)S(1)}, u32[]{:S(2)}, u32[]{:S(2)}) collective-permute-start(f32[6,256]{1,0:T(8,128)S(1)} %fusion), channel_id=1, source_target_pairs={{0,32},{1,33},{2,34},{3,35},{4,36},{5,37},{6,38},{7,39},{8,40},{9,... | collective-permute-start | bytes 18440 | tf_op jit(solution)/shard_map/ppermute | solution.py:70
  208.9 3.7 %collective-permute-start.19 = (f32[6,256]{1,0:T(8,128)S(1)}, f32[6,256]{1,0:T(8,128)S(1)}, u32[]{:S(2)}, u32[]{:S(2)}) collective-permute-start(f32[6,256]{1,0:T(8,128)S(1)} %fusion.1), channel_id=1, source_target_pairs={{0,16},{1,17},{2,18},{3,19},{4,20},{5,21},{6,22},{7,23},{8,24},{9,... | collective-permute-start | bytes 18440 | tf_op jit(solution)/shard_map/ppermute | solution.py:70
  212.7 2.8 %collective-permute-start.22 = (f32[6,128]{1,0:T(8,128)S(1)}, f32[6,128]{1,0:T(8,128)S(1)}, u32[]{:S(2)}, u32[]{:S(2)}) collective-permute-start(f32[6,128]{1,0:T(8,128)S(1)} %bitcast.128), channel_id=1, source_target_pairs={{0,8},{1,9},{2,10},{3,11},{4,12},{5,13},{6,14},{7,15},{8,0},{9,1},... | collective-permute-start | bytes 9224 | tf_op jit(solution)/shard_map/ppermute | solution.py:70
  215.7 2.5 %collective-permute-start.25 = (f32[6,32]{1,0:T(8,128)S(1)}, f32[6,32]{1,0:T(8,128)S(1)}, u32[]{:S(2)}, u32[]{:S(2)}) collective-permute-start(f32[6,32]{1,0:T(8,128)S(1)} %bitcast.129), channel_id=1, source_target_pairs={{0,6},{1,7},{2,0},{3,1},{4,2},{5,3},{6,4},{7,5},{8,14},{9,15},{10,... | collective-permute-start | bytes 2312 | tf_op jit(solution)/shard_map/ppermute | solution.py:70
  215.8 4.0 %collective-permute-start.24 = (f32[6,32]{1,0:T(8,128)S(1)}, f32[6,32]{1,0:T(8,128)S(1)}, u32[]{:S(2)}, u32[]{:S(2)}) collective-permute-start(f32[6,32]{1,0:T(8,128)S(1)} %fusion.6), channel_id=1, source_target_pairs={{0,4},{1,5},{2,6},{3,7},{4,0},{5,1},{6,2},{7,3},{8,12},{9,13},{10,... | collective-permute-start | bytes 2312 | tf_op jit(solution)/shard_map/ppermute | solution.py:70
  217.1 3.7 %collective-permute-start.23 = (f32[6,32]{1,0:T(8,128)S(1)}, f32[6,32]{1,0:T(8,128)S(1)}, u32[]{:S(2)}, u32[]{:S(2)}) collective-permute-start(f32[6,32]{1,0:T(8,128)S(1)} %fusion.7), channel_id=1, source_target_pairs={{0,2},{1,3},{2,4},{3,5},{4,6},{5,7},{6,0},{7,1},{8,10},{9,11},{10,... | collective-permute-start | bytes 2312 | tf_op jit(solution)/shard_map/ppermute | solution.py:70
  220.9 8.6 %collective-permute-start.26 = (f32[6,16]{1,0:T(8,128)S(1)}, f32[6,16]{1,0:T(8,128)S(1)}, u32[]{:S(2)}, u32[]{:S(2)}) collective-permute-start(f32[6,16]{1,0:T(8,128)S(1)} %bitcast.130), channel_id=1, source_target_pairs={{0,1},{1,0},{2,3},{3,2},{4,5},{5,4},{6,7},{7,6},{8,9},{9,8},{10,11... | collective-permute-start | bytes 1160 | tf_op jit(solution)/shard_map/ppermute | solution.py:70

commit v3 on v2

--- a/solution.py
+++ b/solution.py
@@ -1,5 +1,3 @@
-import functools
-
 import jax
 import jax.numpy as jnp
 from jax import lax
@@ -9,7 +7,6 @@
 
 softening = 0.001
 ALL = ("blk", "group")
-LEVELS = (("core", 1, 2), ("x", 2, 4), ("y_lo", 8, 2), ("z", 16, 4), ("y_hi", 64, 2))
 SUB = 2
 
 
@@ -35,48 +32,38 @@
     return (new_pos, new_vel, new_acc, new_jerk)
 
 
-def _perm(stride, size, shift, ndev):
-    pairs = []
-    for d in range(ndev):
-        c = (d // stride) % size
-        pairs.append((d, d + (((c + shift) % size) - c) * stride))
-    return pairs
+def _partner(bit, ndev):
+    return [(d, d ^ (1 << bit)) for d in range(ndev)]
 
 
-def _coord(stride, size):
-    return (lax.axis_index(ALL) // stride) % size
+def _upper(bit):
+    return ((lax.axis_index(ALL) >> bit) & 1) == 1
 
 
-def gather_level(x, level, ndev):
-    _, stride, size = level
-    parts = [x] + [lax.ppermute(x, ALL, _perm(stride, size, s, ndev)) for s in range(1, size)]
-    stack = jnp.stack(parts, axis=0)
-    c = _coord(stride, size)
-    order = (c - jnp.arange(size)) % size
-    picked = jnp.take(stack, order, axis=0)
-    picked = jnp.moveaxis(picked, 0, -2)
-    return picked.reshape(x.shape[:-1] + (size * x.shape[-1],))
+def gather_all(x, ndev):
+    for bit in range(ndev.bit_length() - 1):
+        recv = lax.ppermute(x, ALL, _partner(bit, ndev))
+        x = jnp.where(
+            _upper(bit), jnp.concatenate([recv, x], axis=-1), jnp.concatenate([x, recv], axis=-1)
+        )
+    return x
 
 
-def reduce_level(x, level, ndev):
-    _, stride, size = level
-    m = x.shape[-1] // size
-    blocks = x.reshape(x.shape[:-1] + (size, m))
-    blocks = jnp.moveaxis(blocks, -2, 0)
-    c = _coord(stride, size)
-    total = jnp.take(blocks, c, axis=0)
-    for s in range(1, size):
-        piece = jnp.take(blocks, (c + s) % size, axis=0)
-        total = total + lax.ppermute(piece, ALL, _perm(stride, size, s, ndev))
-    return total
+def sum_all(x, ndev):
+    for bit in range(ndev.bit_length() - 1):
+        x = x + lax.ppermute(x, ALL, _partner(bit, ndev))
+    return x
 
 
-def sum_level(x, level, ndev):
-    _, stride, size = level
-    total = x
-    for s in range(1, size):
-        total = total + lax.ppermute(x, ALL, _perm(stride, size, s, ndev))
-    return total
+def reduce_scatter_all(x, ndev):
+    for bit in reversed(range(ndev.bit_length() - 1)):
+        half = x.shape[-1] // 2
+        low, high = x[..., :half], x[..., half:]
+        upper = _upper(bit)
+        keep = jnp.where(upper, high, low)
+        send = jnp.where(upper, low, high)
+        x = keep + lax.ppermute(send, ALL, _partner(bit, ndev))
+    return x
 
 
 def forces_kernel(act_ref, fld_ref, out_ref):
@@ -143,9 +130,7 @@
     own_stars = positions.shape[1]
     total_stars = own_stars * ndev
     gravity = 1.0 / total_stars
-    every_index = active_index
-    for level in LEVELS:
-        every_index = gather_level(every_index, level, ndev)
+    every_index = gather_all(active_index, ndev)
     pred_pos, pred_vel = predict(positions, velocities, accelerations, jerk_rates, elapsed_time)
     own_field = jnp.concatenate(
         [pred_pos, pred_vel, masses[None, :], jnp.zeros_like(masses)[None, :]], axis=0
@@ -159,17 +144,14 @@
     is_owned = (local_row >= 0) & (local_row < own_stars)
     picked = jnp.take(packed, jnp.clip(local_row, 0, own_stars - 1), axis=1)
     picked = jnp.where(is_owned[None, :], picked, 0.0)
-    rows = picked
-    for level in LEVELS:
-        rows = sum_level(rows, level, ndev)
+    rows = sum_all(picked, ndev)
     act_pos, act_vel = predict(rows[0:3], rows[3:6], rows[6:9], rows[9:12], rows[12])
     num_k = rows.shape[1]
     active_t = jnp.concatenate(
         [act_pos, act_vel, jnp.zeros((2, num_k), jnp.float32)], axis=0
     ).T
     partial = pair_forces(active_t, field_b)[:, 0:6].T
-    for level in reversed(LEVELS):
-        partial = reduce_level(partial, level, ndev)
+    partial = reduce_scatter_all(partial, ndev)
     mine = lax.axis_index(ALL) * active_index.shape[0]
     owner_rows = lax.dynamic_slice_in_dim(rows, mine, active_index.shape[0], axis=1)
     return corrector(owner_rows, partial * gravity)

time: 231 us -> 261 us (1.13)
  starting transfers between devices: 41.7 us -> 53.6 us
  local copies, waits for them, and re-layouts: 22.6 us -> 30 us
  other arithmetic: 2.7 us -> 9.29 us
  waiting for transfers between devices: 41.1 us -> 45.5 us
    ppermute x27 -> x21, starting transfers between devices: 41.7 us -> 53.6 us  [the longest x7 22.2 us: reduce_scatter_all(): x = keep + lax.ppermute(send, ALL, _partner(bit, ndev))]
    ppermute x27 -> x21, waiting for transfers between devices: 41.1 us -> 45.5 us  [the longest x7 23.4 us: reduce_scatter_all(): x = keep + lax.ppermute(send, ALL, _partner(bit, ndev))]
    unnamed x19 -> x13, local copies, waits for them, and re-layouts: 0.07 us -> 4.2 us
    gather x5 -> x0, local copies, waits for them, and re-layouts: 2.8 us -> none  [gather_level(): picked = jnp.take(stack, order, axis=0)]
    mul x0 -> x1, other arithmetic: none -> 2.72 us  [predict(): elapsed * (vel_now + elapsed * (0.5 * acc_now + elapsed * (jerk_now / 6.0)))]
  transfers between devices with their start and end apart: 27 -> 21, of which waited for: 22 -> 20; matrix products, arithmetic and copies ran while one was open for 3% -> 4% of each run, Pallas kernels for 0% -> 0%
where the time goes in v3:
time: 261 us; the launch traced here: 260 us
  Pallas kernels  121 us (46%)
  starting transfers between devices  53.6 us (21%)
  waiting for transfers between devices  45.5 us (17%)
  local copies, waits for them, and re-layouts  30 us (11%)
  other arithmetic  9.29 us (4%)
    pallas_call x1, Pallas kernels, pair_forces(): pl.pallas_call(forces_kernel, out_shape=jax.ShapeDtypeStruct((num_k, 8),...  121 us
    ppermute x7, waiting for transfers between devices, reduce_scatter_all(): x = keep + lax.ppermute(send, ALL, _partner(bit, ndev))  23.4 us
    ppermute x7, starting transfers between devices, reduce_scatter_all(): x = keep + lax.ppermute(send, ALL, _partner(bit, ndev))  22.2 us
    ppermute x7, starting transfers between devices, sum_all(): x = x + lax.ppermute(x, ALL, _partner(bit, ndev))  16.2 us
    ppermute x7, waiting for transfers between devices, sum_all(): x = x + lax.ppermute(x, ALL, _partner(bit, ndev))  16 us
    ppermute x7, starting transfers between devices, gather_all(): recv = lax.ppermute(x, ALL, _partner(bit, ndev))  15.2 us
    gather x2, local copies, waits for them, and re-layouts, on_device(): picked = jnp.take(packed, jnp.clip(local_row, 0, own_stars - 1), axis=1)  7.98 us
    concatenate x2, local copies, waits for them, and re-layouts, on_device(): jnp.concatenate([positions, velocities, accelerations, jerk_rates, elapse...  6.67 us
  transfers between devices with their start and end apart: 21, of which 20 were waited for; matrix products, arithmetic and copies ran while one was open for 4% of the time, Pallas kernels for 0%

profile of v3, /device:TPU:1, one launch (start us, length us, event | category | flops | bytes accessed | tf_op | source)
XLA Modules:
  0.0 260.4 jit_solution(6870548827502674925)
XLA Ops:
  0.6 1.5 collective-permute-start
  2.1 1.0 collective-permute-done
  3.9 1.3 collective-permute-start.1
  5.2 1.1 collective-permute-done.1
  6.4 2.9 %collective-permute-start.2 = (s32[64]{0:T(128)S(1)}, s32[64]{0:T(128)S(1)}, u32[]{:S(2)}, u32[]{:S(2)}) collective-permute-start(s32[64]{0:T(128)S(1)} %broadcast_select_fusion.2), channel_id=1, source_target_pairs={{0,4},{1,5},{2,6},{3,7},{4,0},{5,1},{6,2},{7,3},{8,12},{9,13},{10,... | collective-permute-start | bytes 776 | tf_op jit(solution)/shard_map/ppermute | solution.py:45
  9.2 1.1 collective-permute-done.2
  10.4 1.4 collective-permute-start.3
  11.8 1.0 collective-permute-done.3
  12.8 1.7 collective-permute-start.4
  14.6 1.0 collective-permute-done.4
  15.5 3.4 %collective-permute-start.5 = (s32[512]{0:T(512)S(1)}, s32[512]{0:T(512)S(1)}, u32[]{:S(2)}, u32[]{:S(2)}) collective-permute-start(s32[512]{0:T(512)S(1)} %add_select_fusion.2), channel_id=1, source_target_pairs={{0,32},{1,33},{2,34},{3,35},{4,36},{5,37},{6,38},{7,39},{8,40},{9,... | collective-permute-start | bytes 6152 | tf_op jit(solution)/shard_map/ppermute | solution.py:45
  19.0 1.0 collective-permute-done.5
  19.9 2.9 %collective-permute-start.6 = (s32[1024]{0:T(1024)S(1)}, s32[1024]{0:T(1024)S(1)}, u32[]{:S(2)}, u32[]{:S(2)}) collective-permute-start(s32[1024]{0:T(1024)S(1)} %add_select_fusion.1), channel_id=1, source_target_pairs={{0,64},{1,65},{2,66},{3,67},{4,68},{5,69},{6,70},{7,71},{8,72},{9,... | collective-permute-start | bytes 12296 | tf_op jit(solution)/shard_map/ppermute | solution.py:45
  22.9 4.0 %concatenate.123 = f32[13,8192]{1,0:T(8,128)S(1)} concatenate(f32[3,8192]{1,0:T(4,128)} %param.7, f32[3,8192]{1,0:T(4,128)} %param.8, f32[3,8192]{1,0:T(4,128)} %param.9, f32[3,8192]{1,0:T(4,128)} %param.10, f32[1,8192]{1,0:T(1,128)} %bitcast.14), dimensions={0} | concatenate | bytes 851968 | tf_op jit(solution)/shard_map/concatenate | solution.py:139
  26.9 2.6 %copy.52 = f32[13,8192]{0,1:T(8,128)} copy(f32[13,8192]{1,0:T(8,128)S(1)} %concatenate.123) | data formatting | bytes 851968 | tf_op jit(solution)/shard_map/concatenate | solution.py:139
  29.6 7.6 %gather_fusion = f32[2048,13]{1,0:T(8,128)S(1)} fusion(f32[13,8192]{0,1:T(8,128)} %copy.52, s32[2048]{0:T(1024)S(1)} %broadcast_clamp_fusion), kind=kCustom, calls=%fused_computation | custom fusion | bytes 221184 | tf_op jit(solution)/shard_map/jit(_take)/gather | solution.py:145
  37.6 6.2 %collective-permute-start.7 = (f32[13,2048]{1,0:T(8,128)S(1)}, f32[13,2048]{1,0:T(8,128)S(1)}, u32[]{:S(2)}, u32[]{:S(2)}) collective-permute-start(f32[13,2048]{1,0:T(8,128)S(1)} %select_bitcast_fusion), channel_id=1, source_target_pairs={{0,1},{1,0},{2,3},{3,2},{4,5},{5,4},{6,7},{7,6},{8,9},{9,8},{10,11... | collective-permute-start | bytes 319496 | tf_op jit(solution)/shard_map/ppermute | solution.py:54
  43.8 1.0 collective-permute-done.7
  44.8 1.3 collective-permute-start.8
  46.5 3.1 %collective-permute-done.8 = f32[13,2048]{1,0:T(8,128)S(1)} collective-permute-done((f32[13,2048]{1,0:T(8,128)S(1)}, f32[13,2048]{1,0:T(8,128)S(1)}, u32[]{:S(2)}, u32[]{:S(2)}) %collective-permute-start.8) | collective-permute-done | bytes 106528 | tf_op jit(solution)/shard_map/ppermute | solution.py:54
  50.4 2.8 %collective-permute-start.9 = (f32[13,2048]{1,0:T(8,128)S(1)}, f32[13,2048]{1,0:T(8,128)S(1)}, u32[]{:S(2)}, u32[]{:S(2)}) collective-permute-start(f32[13,2048]{1,0:T(8,128)S(1)} %copy.56), channel_id=1, source_target_pairs={{0,4},{1,5},{2,6},{3,7},{4,0},{5,1},{6,2},{7,3},{8,12},{9,13},{10,... | collective-permute-start | bytes 319496 | tf_op jit(solution)/shard_map/ppermute | solution.py:54
  53.2 2.6 collective-permute-done.9
  57.0 3.4 %collective-permute-done.10 = f32[13,2048]{1,0:T(8,128)S(1)} collective-permute-done((f32[13,2048]{1,0:T(8,128)S(1)}, f32[13,2048]{1,0:T(8,128)S(1)}, u32[]{:S(2)}, u32[]{:S(2)}) %collective-permute-start.10) | collective-permute-done | bytes 106528 | tf_op jit(solution)/shard_map/ppermute | solution.py:54
  61.3 1.3 collective-permute-start.11
  62.6 1.4 broadcast_multiply_fusion.1
  64.0 1.2 collective-permute-done.11
  66.0 3.3 %collective-permute-start.12 = (f32[13,2048]{1,0:T(8,128)S(1)}, f32[13,2048]{1,0:T(8,128)S(1)}, u32[]{:S(2)}, u32[]{:S(2)}) collective-permute-start(f32[13,2048]{1,0:T(8,128)S(1)} %copy.62), channel_id=1, source_target_pairs={{0,32},{1,33},{2,34},{3,35},{4,36},{5,37},{6,38},{7,39},{8,40},{9,... | collective-permute-start | bytes 319496 | tf_op jit(solution)/shard_map/ppermute | solution.py:54
  69.3 1.7 multiply_add_fusion.1
  71.1 1.3 collective-permute-done.12
  74.0 1.0 maximum_maximum_fusion
  75.1 3.4 %collective-permute-done.13 = f32[13,2048]{1,0:T(8,128)S(1)} collective-permute-done((f32[13,2048]{1,0:T(8,128)S(1)}, f32[13,2048]{1,0:T(8,128)S(1)}, u32[]{:S(2)}, u32[]{:S(2)}) %collective-permute-start.13) | collective-permute-done | bytes 106528 | tf_op jit(solution)/shard_map/ppermute | solution.py:54
  79.7 2.7 %add_multiply_fusion.1 = (f32[3,2048]{0,1:T(8,128)}, f32[3,2048]{0,1:T(8,128)S(1)}, f32[3,2048]{0,1:T(8,128)S(1)}, f32[3,2048]{0,1:T(8,128)}) fusion(f32[13,2048]{0,1:T(8,128)S(1)} %add.137, f32[2048]{0:T(1024)S(1)} %slice_reduce_fusion, f32[2048]{0:T(1024)S(1)} %get-tuple-element.34, f32[2048]{0:T(1024)S(1)} %get-tuple-element.35), kind=kLoop, calls=%fused_computation.4 | loop fusion | flops 55296 | bytes 221184 | tf_op jit(solution)/shard_map/mul | solution.py:14
  82.4 1.6 copy.69
  84.0 1.6 copy.78
  86.3 1.3 copy.73
  87.7 1.5 broadcast_in_dim.54.fld_ref
  89.1 121.0 %shard_map.102 = f32[2048,8]{1,0:T(8,128)} custom-call(f32[2048,8]{1,0:T(8,128)} %bitcast.13, f32[8,8,8192]{2,1,0:T(8,128)} %broadcast_in_dim.54.fld_ref), custom_call_target="tpu_custom_call" | custom-call | tf_op jit(solution)/shard_map/pallas_call | solution.py:122
  210.1 1.3 slice_bitcast_fusion
  212.3 8.8 %collective-permute-done.14 = f32[6,1024]{0,1:T(8,128)S(1)} collective-permute-done((f32[6,1024]{0,1:T(8,128)S(1)}, f32[6,1024]{0,1:T(8,128)S(1)}, u32[]{:S(2)}, u32[]{:S(2)}) %collective-permute-start.14) | collective-permute-done | bytes 24608 | tf_op jit(solution)/shard_map/ppermute | solution.py:65
  221.2 2.3 collective-permute-start.15
  223.5 4.8 %collective-permute-done.15 = f32[6,512]{0,1:T(8,128)S(1)} collective-permute-done((f32[6,512]{0,1:T(8,128)S(1)}, f32[6,512]{0,1:T(8,128)S(1)}, u32[]{:S(2)}, u32[]{:S(2)}) %collective-permute-start.15) | collective-permute-done | bytes 12320 | tf_op jit(solution)/shard_map/ppermute | solution.py:65
  229.2 3.0 %collective-permute-done.16 = f32[6,256]{0,1:T(8,128)S(1)} collective-permute-done((f32[6,256]{0,1:T(8,128)S(1)}, f32[6,256]{0,1:T(8,128)S(1)}, u32[]{:S(2)}, u32[]{:S(2)}) %collective-permute-start.16) | collective-permute-done | bytes 6176 | tf_op jit(solution)/shard_map/ppermute | solution.py:65
  232.5 3.3 %collective-permute-done.17 = f32[6,128]{0,1:T(8,128)S(1)} collective-permute-done((f32[6,128]{0,1:T(8,128)S(1)}, f32[6,128]{0,1:T(8,128)S(1)}, u32[]{:S(2)}, u32[]{:S(2)}) %collective-permute-start.17) | collective-permute-done | bytes 3104 | tf_op jit(solution)/shard_map/ppermute | solution.py:65
  235.8 2.8 %collective-permute-start.18 = (f32[6,64]{0,1:T(8,128)S(1)}, f32[6,64]{0,1:T(8,128)S(1)}, u32[]{:S(2)}, u32[]{:S(2)}) collective-permute-start(f32[6,64]{0,1:T(8,128)S(1)} %slice_select_fusion.4), channel_id=1, source_target_pairs={{0,4},{1,5},{2,6},{3,7},{4,0},{5,1},{6,2},{7,3},{8,12},{9,13},{10,... | collective-permute-start | bytes 4616 | tf_op jit(solution)/shard_map/ppermute | solution.py:65
  238.7 1.5 collective-permute-done.18
  240.2 1.3 collective-permute-start.19
  241.5 1.4 collective-permute-done.19
  242.9 13.9 %collective-permute-start.20 = (f32[6,16]{0,1:T(8,128)S(1)}, f32[6,16]{0,1:T(8,128)S(1)}, u32[]{:S(2)}, u32[]{:S(2)}) collective-permute-start(f32[6,16]{0,1:T(8,128)S(1)} %slice_select_fusion.6), channel_id=1, source_target_pairs={{0,1},{1,0},{2,3},{3,2},{4,5},{5,4},{6,7},{7,6},{8,9},{9,8},{10,11... | collective-permute-start | bytes 1160 | tf_op jit(solution)/shard_map/ppermute | solution.py:65
  (75 shorter events, 14.8 us)
Async XLA Ops:
  0.6 2.4 collective-permute-start
  3.9 2.4 collective-permute-start.1
  6.4 3.9 %collective-permute-start.2 = (s32[64]{0:T(128)S(1)}, s32[64]{0:T(128)S(1)}, u32[]{:S(2)}, u32[]{:S(2)}) collective-permute-start(s32[64]{0:T(128)S(1)} %broadcast_select_fusion.2), channel_id=1, source_target_pairs={{0,4},{1,5},{2,6},{3,7},{4,0},{5,1},{6,2},{7,3},{8,12},{9,13},{10,... | collective-permute-start | bytes 776 | tf_op jit(solution)/shard_map/ppermute | solution.py:45
  10.4 2.4 collective-permute-start.3
  12.8 2.7 %collective-permute-start.4 = (s32[256]{0:T(256)S(1)}, s32[256]{0:T(256)S(1)}, u32[]{:S(2)}, u32[]{:S(2)}) collective-permute-start(s32[256]{0:T(256)S(1)} %add_select_fusion.3), channel_id=1, source_target_pairs={{0,16},{1,17},{2,18},{3,19},{4,20},{5,21},{6,22},{7,23},{8,24},{9,... | collective-permute-start | bytes 3080 | tf_op jit(solution)/shard_map/ppermute | solution.py:45
  15.5 4.4 %collective-permute-start.5 = (s32[512]{0:T(512)S(1)}, s32[512]{0:T(512)S(1)}, u32[]{:S(2)}, u32[]{:S(2)}) collective-permute-start(s32[512]{0:T(512)S(1)} %add_select_fusion.2), channel_id=1, source_target_pairs={{0,32},{1,33},{2,34},{3,35},{4,36},{5,37},{6,38},{7,39},{8,40},{9,... | collective-permute-start | bytes 6152 | tf_op jit(solution)/shard_map/ppermute | solution.py:45
  19.9 9.6 %collective-permute-start.6 = (s32[1024]{0:T(1024)S(1)}, s32[1024]{0:T(1024)S(1)}, u32[]{:S(2)}, u32[]{:S(2)}) collective-permute-start(s32[1024]{0:T(1024)S(1)} %add_select_fusion.1), channel_id=1, source_target_pairs={{0,64},{1,65},{2,66},{3,67},{4,68},{5,69},{6,70},{7,71},{8,72},{9,... | collective-permute-start | bytes 12296 | tf_op jit(solution)/shard_map/ppermute | solution.py:45
  37.6 7.2 %collective-permute-start.7 = (f32[13,2048]{1,0:T(8,128)S(1)}, f32[13,2048]{1,0:T(8,128)S(1)}, u32[]{:S(2)}, u32[]{:S(2)}) collective-permute-start(f32[13,2048]{1,0:T(8,128)S(1)} %select_bitcast_fusion), channel_id=1, source_target_pairs={{0,1},{1,0},{2,3},{3,2},{4,5},{5,4},{6,7},{7,6},{8,9},{9,8},{10,11... | collective-permute-start | bytes 319496 | tf_op jit(solution)/shard_map/ppermute | solution.py:54
  44.8 4.8 %collective-permute-start.8 = (f32[13,2048]{1,0:T(8,128)S(1)}, f32[13,2048]{1,0:T(8,128)S(1)}, u32[]{:S(2)}, u32[]{:S(2)}) collective-permute-start(f32[13,2048]{1,0:T(8,128)S(1)} %fusion.7), channel_id=1, source_target_pairs={{0,2},{1,3},{2,0},{3,1},{4,6},{5,7},{6,4},{7,5},{8,10},{9,11},{10,... | collective-permute-start | bytes 319496 | tf_op jit(solution)/shard_map/ppermute | solution.py:54
  50.4 5.4 %collective-permute-start.9 = (f32[13,2048]{1,0:T(8,128)S(1)}, f32[13,2048]{1,0:T(8,128)S(1)}, u32[]{:S(2)}, u32[]{:S(2)}) collective-permute-start(f32[13,2048]{1,0:T(8,128)S(1)} %copy.56), channel_id=1, source_target_pairs={{0,4},{1,5},{2,6},{3,7},{4,0},{5,1},{6,2},{7,3},{8,12},{9,13},{10,... | collective-permute-start | bytes 319496 | tf_op jit(solution)/shard_map/ppermute | solution.py:54
  56.6 3.9 %collective-permute-start.10 = (f32[13,2048]{1,0:T(8,128)S(1)}, f32[13,2048]{1,0:T(8,128)S(1)}, u32[]{:S(2)}, u32[]{:S(2)}) collective-permute-start(f32[13,2048]{1,0:T(8,128)S(1)} %copy.58), channel_id=1, source_target_pairs={{0,8},{1,9},{2,10},{3,11},{4,12},{5,13},{6,14},{7,15},{8,0},{9,1},... | collective-permute-start | bytes 319496 | tf_op jit(solution)/shard_map/ppermute | solution.py:54
  60.8 8.5 %copy-start = (f32[3,8192]{1,0:T(4,128)S(1)}, f32[3,8192]{1,0:T(4,128)}, u32[]{:S(2)}) copy-start(f32[3,8192]{1,0:T(4,128)} %param.7) | copy-start | bytes 294916
  60.8 8.5 %copy-start.1 = (f32[3,8192]{1,0:T(4,128)S(1)}, f32[3,8192]{1,0:T(4,128)}, u32[]{:S(2)}) copy-start(f32[3,8192]{1,0:T(4,128)} %param.8) | copy-start | bytes 294916
  60.8 8.4 %copy-start.2 = (f32[3,8192]{1,0:T(4,128)S(1)}, f32[3,8192]{1,0:T(4,128)}, u32[]{:S(2)}) copy-start(f32[3,8192]{1,0:T(4,128)} %param.9) | copy-start | bytes 294916
  61.3 3.9 %collective-permute-start.11 = (f32[13,2048]{1,0:T(8,128)S(1)}, f32[13,2048]{1,0:T(8,128)S(1)}, u32[]{:S(2)}, u32[]{:S(2)}) collective-permute-start(f32[13,2048]{1,0:T(8,128)S(1)} %copy.60), channel_id=1, source_target_pairs={{0,16},{1,17},{2,18},{3,19},{4,20},{5,21},{6,22},{7,23},{8,24},{9,... | collective-permute-start | bytes 319496 | tf_op jit(solution)/shard_map/ppermute | solution.py:54
  66.0 6.4 %collective-permute-start.12 = (f32[13,2048]{1,0:T(8,128)S(1)}, f32[13,2048]{1,0:T(8,128)S(1)}, u32[]{:S(2)}, u32[]{:S(2)}) collective-permute-start(f32[13,2048]{1,0:T(8,128)S(1)} %copy.62), channel_id=1, source_target_pairs={{0,32},{1,33},{2,34},{3,35},{4,36},{5,37},{6,38},{7,39},{8,40},{9,... | collective-permute-start | bytes 319496 | tf_op jit(solution)/shard_map/ppermute | solution.py:54
  71.0 3.0 %copy-start.3 = (f32[3,8192]{1,0:T(4,128)S(1)}, f32[3,8192]{1,0:T(4,128)}, u32[]{:S(2)}) copy-start(f32[3,8192]{1,0:T(4,128)} %get-tuple-element.28) | copy-start | bytes 294916
  73.2 5.4 %collective-permute-start.13 = (f32[13,2048]{1,0:T(8,128)S(1)}, f32[13,2048]{1,0:T(8,128)S(1)}, u32[]{:S(2)}, u32[]{:S(2)}) collective-permute-start(f32[13,2048]{1,0:T(8,128)S(1)} %copy.64), channel_id=1, source_target_pairs={{0,64},{1,65},{2,66},{3,67},{4,68},{5,69},{6,70},{7,71},{8,72},{9,... | collective-permute-start | bytes 319496 | tf_op jit(solution)/shard_map/ppermute | solution.py:54
  211.5 9.6 %collective-permute-start.14 = (f32[6,1024]{0,1:T(8,128)S(1)}, f32[6,1024]{0,1:T(8,128)S(1)}, u32[]{:S(2)}, u32[]{:S(2)}) collective-permute-start(f32[6,1024]{0,1:T(8,128)S(1)} %slice_select_fusion), channel_id=1, source_target_pairs={{0,64},{1,65},{2,66},{3,67},{4,68},{5,69},{6,70},{7,71},{8,72},{9,... | collective-permute-start | bytes 73736 | tf_op jit(solution)/shard_map/ppermute | solution.py:65
  221.2 7.1 %collective-permute-start.15 = (f32[6,512]{0,1:T(8,128)S(1)}, f32[6,512]{0,1:T(8,128)S(1)}, u32[]{:S(2)}, u32[]{:S(2)}) collective-permute-start(f32[6,512]{0,1:T(8,128)S(1)} %slice_select_fusion.1), channel_id=1, source_target_pairs={{0,32},{1,33},{2,34},{3,35},{4,36},{5,37},{6,38},{7,39},{8,40},{9,... | collective-permute-start | bytes 36872 | tf_op jit(solution)/shard_map/ppermute | solution.py:65
  228.4 3.9 %collective-permute-start.16 = (f32[6,256]{0,1:T(8,128)S(1)}, f32[6,256]{0,1:T(8,128)S(1)}, u32[]{:S(2)}, u32[]{:S(2)}) collective-permute-start(f32[6,256]{0,1:T(8,128)S(1)} %slice_select_fusion.2), channel_id=1, source_target_pairs={{0,16},{1,17},{2,18},{3,19},{4,20},{5,21},{6,22},{7,23},{8,24},{9,... | collective-permute-start | bytes 18440 | tf_op jit(solution)/shard_map/ppermute | solution.py:65
  232.3 3.5 %collective-permute-start.17 = (f32[6,128]{0,1:T(8,128)S(1)}, f32[6,128]{0,1:T(8,128)S(1)}, u32[]{:S(2)}, u32[]{:S(2)}) collective-permute-start(f32[6,128]{0,1:T(8,128)S(1)} %slice_select_fusion.3), channel_id=1, source_target_pairs={{0,8},{1,9},{2,10},{3,11},{4,12},{5,13},{6,14},{7,15},{8,0},{9,1},... | collective-permute-start | bytes 9224 | tf_op jit(solution)/shard_map/ppermute | solution.py:65
  235.8 4.3 %collective-permute-start.18 = (f32[6,64]{0,1:T(8,128)S(1)}, f32[6,64]{0,1:T(8,128)S(1)}, u32[]{:S(2)}, u32[]{:S(2)}) collective-permute-start(f32[6,64]{0,1:T(8,128)S(1)} %slice_select_fusion.4), channel_id=1, source_target_pairs={{0,4},{1,5},{2,6},{3,7},{4,0},{5,1},{6,2},{7,3},{8,12},{9,13},{10,... | collective-permute-start | bytes 4616 | tf_op jit(solution)/shard_map/ppermute | solution.py:65
  240.2 2.7 %collective-permute-start.19 = (f32[6,32]{0,1:T(8,128)S(1)}, f32[6,32]{0,1:T(8,128)S(1)}, u32[]{:S(2)}, u32[]{:S(2)}) collective-permute-start(f32[6,32]{0,1:T(8,128)S(1)} %slice_select_fusion.5), channel_id=1, source_target_pairs={{0,2},{1,3},{2,0},{3,1},{4,6},{5,7},{6,4},{7,5},{8,10},{9,11},{10,... | collective-permute-start | bytes 2312 | tf_op jit(solution)/shard_map/ppermute | solution.py:65
  242.9 14.8 %collective-permute-start.20 = (f32[6,16]{0,1:T(8,128)S(1)}, f32[6,16]{0,1:T(8,128)S(1)}, u32[]{:S(2)}, u32[]{:S(2)}) collective-permute-start(f32[6,16]{0,1:T(8,128)S(1)} %slice_select_fusion.6), channel_id=1, source_target_pairs={{0,1},{1,0},{2,3},{3,2},{4,5},{5,4},{6,7},{7,6},{8,9},{9,8},{10,11... | collective-permute-start | bytes 1160 | tf_op jit(solution)/shard_map/ppermute | solution.py:65

commit v4 on v2

--- a/solution.py
+++ b/solution.py
@@ -21,17 +21,29 @@
     return (pred_pos, pred_vel)
 
 
-def corrector(owner_rows, forces):
-    old_pos = owner_rows[0:3]
-    old_vel = owner_rows[3:6]
-    old_acc = owner_rows[6:9]
-    old_jerk = owner_rows[9:12]
-    elapsed = owner_rows[12]
+def corrector_terms(rows):
+    old_pos = rows[0:3]
+    old_vel = rows[3:6]
+    old_acc = rows[6:9]
+    old_jerk = rows[9:12]
+    elapsed = rows[12]
+    half = 0.5 * elapsed
+    squared = elapsed * elapsed / 12.0
+    vel_part = old_vel + half * old_acc + squared * old_jerk
+    pos_part = old_pos + half * old_vel + squared * old_acc
+    return jnp.concatenate([pos_part, vel_part, elapsed[None, :]], axis=0)
+
+
+def corrector(terms, forces):
+    pos_part = terms[0:3]
+    vel_part = terms[3:6]
+    elapsed = terms[6]
     new_acc = forces[0:3]
     new_jerk = forces[3:6]
+    half = 0.5 * elapsed
     squared = elapsed * elapsed / 12.0
-    new_vel = old_vel + 0.5 * elapsed * (old_acc + new_acc) + squared * (old_jerk - new_jerk)
-    new_pos = old_pos + 0.5 * elapsed * (old_vel + new_vel) + squared * (old_acc - new_acc)
+    new_vel = vel_part + half * new_acc - squared * new_jerk
+    new_pos = pos_part + half * new_vel - squared * new_acc
     return (new_pos, new_vel, new_acc, new_jerk)
 
 
@@ -121,7 +133,7 @@
 
         zero = jnp.zeros((8, 128), jnp.float32)
         init = tuple(tuple(zero for _ in range(6)) for _ in range(SUB))
-        accs = lax.fori_loop(0, num_j // 128, jstep, init, unroll=8)
+        accs = lax.fori_loop(0, num_j // 128, jstep, init, unroll=16)
         for s in range(SUB):
             for c in range(6):
                 out_ref[pl.ds(k0 + 8 * s, 8), c:c + 1] = jnp.sum(accs[s][c], axis=1, keepdims=True)
@@ -159,20 +171,17 @@
     is_owned = (local_row >= 0) & (local_row < own_stars)
     picked = jnp.take(packed, jnp.clip(local_row, 0, own_stars - 1), axis=1)
     picked = jnp.where(is_owned[None, :], picked, 0.0)
-    rows = picked
+    act_pos, act_vel = predict(picked[0:3], picked[3:6], picked[6:9], picked[9:12], picked[12])
+    num_k = picked.shape[1]
+    active = jnp.concatenate([act_pos, act_vel], axis=0)
     for level in LEVELS:
-        rows = sum_level(rows, level, ndev)
-    act_pos, act_vel = predict(rows[0:3], rows[3:6], rows[6:9], rows[9:12], rows[12])
-    num_k = rows.shape[1]
-    active_t = jnp.concatenate(
-        [act_pos, act_vel, jnp.zeros((2, num_k), jnp.float32)], axis=0
-    ).T
+        active = sum_level(active, level, ndev)
+    active_t = jnp.concatenate([active, jnp.zeros((2, num_k), jnp.float32)], axis=0).T
     partial = pair_forces(active_t, field_b)[:, 0:6].T
+    payload = jnp.concatenate([partial, corrector_terms(picked)], axis=0)
     for level in reversed(LEVELS):
-        partial = reduce_level(partial, level, ndev)
-    mine = lax.axis_index(ALL) * active_index.shape[0]
-    owner_rows = lax.dynamic_slice_in_dim(rows, mine, active_index.shape[0], axis=1)
-    return corrector(owner_rows, partial * gravity)
+        payload = reduce_level(payload, level, ndev)
+    return corrector(payload[6:13], payload[0:6] * gravity)
 
 
 def solution(mesh):

time: 231 us -> 223 us (0.965)
  waiting for transfers between devices: 41.1 us -> 37 us
  Pallas kernels: 121 us -> 118 us
    ppermute x9, waiting for transfers between devices: 21.7 us -> 15.3 us  [sum_level(): total = total + lax.ppermute(x, ALL, _perm(stride, size, s, ndev))]
    pallas_call x1, Pallas kernels: 121 us -> 118 us  [pair_forces(): pl.pallas_call(forces_kernel, out_shape=jax.ShapeDtypeStruct((num_k, 8),...]
    transpose x0 -> x3, local copies, waits for them, and re-layouts: none -> 2.66 us  [the longest x2 1.62 us: on_device(): partial = pair_forces(active_t, field_b)[:, 0:6].T]
  transfers between devices with their start and end apart: 27 -> 27, of which waited for: 22 -> 23; matrix products, arithmetic and copies ran while one was open for 3% -> 3% of each run, Pallas kernels for 0% -> 0%
where the time goes in v4:
time: 223 us
  Pallas kernels  118 us (53%)
  starting transfers between devices  40.8 us (18%)
  waiting for transfers between devices  37 us (17%)
  local copies, waits for them, and re-layouts  23.2 us (10%)
  other arithmetic  2.71 us (1%)
    pallas_call x1, Pallas kernels, pair_forces(): pl.pallas_call(forces_kernel, out_shape=jax.ShapeDtypeStruct((num_k, 8),...  118 us
    ppermute x9, starting transfers between devices, reduce_level(): total = total + lax.ppermute(piece, ALL, _perm(stride, size, s, ndev))  16 us
    ppermute x9, waiting for transfers between devices, sum_level(): total = total + lax.ppermute(x, ALL, _perm(stride, size, s, ndev))  15.3 us
    ppermute x9, starting transfers between devices, gather_level(): lax.ppermute(x, ALL, _perm(stride, size, s, ndev))  13.9 us
    ppermute x9, waiting for transfers between devices, reduce_level(): total = total + lax.ppermute(piece, ALL, _perm(stride, size, s, ndev))  13.8 us
    ppermute x9, starting transfers between devices, sum_level(): total = total + lax.ppermute(x, ALL, _perm(stride, size, s, ndev))  10.9 us
    gather x2, local copies, waits for them, and re-layouts, on_device(): picked = jnp.take(packed, jnp.clip(local_row, 0, own_stars - 1), axis=1)  7.98 us
    ppermute x9, waiting for transfers between devices, gather_level(): lax.ppermute(x, ALL, _perm(stride, size, s, ndev))  7.85 us
  transfers between devices with their start and end apart: 27, of which 23 were waited for; matrix products, arithmetic and copies ran while one was open for 3% of the time, Pallas kernels for 0%

profile of v4, /device:TPU:1, one launch (start us, length us, event | category | flops | bytes accessed | tf_op | source)
XLA Modules:
  0.0 223.1 jit_solution(7204729284869261324)
XLA Ops:
  0.6 1.5 collective-permute-start
  2.3 0.7 collective-permute-done
  3.0 0.7 pad_add_fusion.3
  4.4 2.6 %collective-permute-start.3 = (s32[32]{0:T(128)S(1)}, s32[32]{0:T(128)S(1)}, u32[]{:S(2)}, u32[]{:S(2)}) collective-permute-start(s32[32]{0:T(128)S(1)} %select_n.413), channel_id=1, source_target_pairs={{0,6},{1,7},{2,0},{3,1},{4,2},{5,3},{6,4},{7,5},{8,14},{9,15},{10,... | collective-permute-start | bytes 392 | tf_op jit(solution)/shard_map/ppermute | solution.py:64
  7.5 0.6 collective-permute-start.1
  8.2 2.7 %collective-permute-done.2 = s32[32]{0:T(128)S(1)} collective-permute-done((s32[32]{0:T(128)S(1)}, s32[32]{0:T(128)S(1)}, u32[]{:S(2)}, u32[]{:S(2)}) %collective-permute-start.2) | collective-permute-done | bytes 160 | tf_op jit(solution)/shard_map/ppermute | solution.py:64
  11.9 1.3 collective-permute-start.4
  13.3 1.0 collective-permute-done.4
  15.0 3.8 %collective-permute-start.7 = (s32[256]{0:T(256)S(1)}, s32[256]{0:T(256)S(1)}, u32[]{:S(2)}, u32[]{:S(2)}) collective-permute-start(s32[256]{0:T(256)S(1)} %fusion.35), channel_id=1, source_target_pairs={{0,48},{1,49},{2,50},{3,51},{4,52},{5,53},{6,54},{7,55},{8,56},{9,... | collective-permute-start | bytes 3080 | tf_op jit(solution)/shard_map/ppermute | solution.py:64
  18.7 0.7 collective-permute-start.5
  19.5 3.2 %collective-permute-done.6 = s32[256]{0:T(256)S(1)} collective-permute-done((s32[256]{0:T(256)S(1)}, s32[256]{0:T(256)S(1)}, u32[]{:S(2)}, u32[]{:S(2)}) %collective-permute-start.6) | collective-permute-done | bytes 1056 | tf_op jit(solution)/shard_map/ppermute | solution.py:64
  22.7 0.6 gather_fusion.3
  23.3 2.9 %collective-permute-start.8 = (s32[1024]{0:T(1024)S(1)}, s32[1024]{0:T(1024)S(1)}, u32[]{:S(2)}, u32[]{:S(2)}) collective-permute-start(s32[1024]{0:T(1024)S(1)} %bitcast.132), channel_id=1, source_target_pairs={{0,64},{1,65},{2,66},{3,67},{4,68},{5,69},{6,70},{7,71},{8,72},{9,... | collective-permute-start | bytes 12296 | tf_op jit(solution)/shard_map/ppermute | solution.py:64
  26.3 4.0 %concatenate.15 = f32[13,8192]{1,0:T(8,128)S(1)} concatenate(f32[3,8192]{1,0:T(4,128)} %param.17, f32[3,8192]{1,0:T(4,128)} %param.18, f32[3,8192]{1,0:T(4,128)} %param.19, f32[3,8192]{1,0:T(4,128)} %param.20, f32[1,8192]{1,0:T(1,128)} %bitcast.115), dimensions={0} | concatenate | bytes 851968 | tf_op jit(solution)/shard_map/concatenate | solution.py:166
  30.4 2.7 %copy.96 = f32[13,8192]{0,1:T(8,128)} copy(f32[13,8192]{1,0:T(8,128)S(1)} %concatenate.15) | data formatting | bytes 851968 | tf_op jit(solution)/shard_map/concatenate | solution.py:166
  33.1 0.6 gather_fusion.4
  33.8 7.6 %gather_fusion.5 = f32[2048,13]{1,0:T(8,128)S(1)} fusion(f32[13,8192]{0,1:T(8,128)} %copy.96, s32[2048]{0:T(1024)S(1)} %broadcast_clamp_fusion), kind=kCustom, calls=%fused_computation.5 | custom fusion | bytes 221184 | tf_op jit(solution)/shard_map/jit(_take)/gather | solution.py:172
  42.0 5.0 %collective-permute-start.9 = (f32[6,2048]{1,0:T(8,128)S(1)}, f32[6,2048]{1,0:T(8,128)S(1)}, u32[]{:S(2)}, u32[]{:S(2)}) collective-permute-start(f32[6,2048]{1,0:T(8,128)S(1)} %pad_maximum_fusion.1), channel_id=1, source_target_pairs={{0,1},{1,0},{2,3},{3,2},{4,5},{5,4},{6,7},{7,6},{8,9},{9,8},{10,11... | collective-permute-start | bytes 147464 | tf_op jit(solution)/shard_map/ppermute | solution.py:90
  47.0 0.9 collective-permute-done.9
  48.0 1.3 collective-permute-start.11
  49.3 0.8 collective-permute-start.10
  50.1 1.0 collective-permute-done.12
  51.1 1.6 collective-permute-done.11
  52.7 2.1 collective-permute-done.10
  55.3 2.7 %collective-permute-done.13 = f32[6,2048]{1,0:T(8,128)S(1)} collective-permute-done((f32[6,2048]{1,0:T(8,128)S(1)}, f32[6,2048]{1,0:T(8,128)S(1)}, u32[]{:S(2)}, u32[]{:S(2)}) %collective-permute-start.13) | collective-permute-done | bytes 49184 | tf_op jit(solution)/shard_map/ppermute | solution.py:90
  58.4 1.6 collective-permute-start.15
  60.0 0.8 collective-permute-start.14
  61.2 1.8 collective-permute-done.15
  63.0 1.3 collective-permute-done.14
  64.3 0.6 collective-permute-start.17
  65.4 3.6 %collective-permute-done.17 = f32[6,2048]{1,0:T(8,128)S(1)} collective-permute-done((f32[6,2048]{1,0:T(8,128)S(1)}, f32[6,2048]{1,0:T(8,128)S(1)}, u32[]{:S(2)}, u32[]{:S(2)}) %collective-permute-start.17) | collective-permute-done | bytes 49184 | tf_op jit(solution)/shard_map/ppermute | solution.py:90
  69.5 1.0 pad_bitcast_fusion.act_ref
  70.5 1.5 broadcast_in_dim.160.fld_ref
  72.0 118.3 %shard_map.102 = f32[2048,8]{1,0:T(8,128)} custom-call(f32[2048,8]{1,0:T(8,128)} %pad_bitcast_fusion.act_ref, f32[8,8,8192]{2,1,0:T(8,128)} %broadcast_in_dim.160.fld_ref), custom_call_target="tpu_custom_call" | custom-call | tf_op jit(solution)/shard_map/pallas_call | solution.py:147
  190.3 1.3 slice_bitcast_fusion
  192.2 0.6 collective-permute-start.18
  192.7 4.1 %collective-permute-done.18 = f32[13,1024]{1,0:T(8,128)S(1)} collective-permute-done((f32[13,1024]{1,0:T(8,128)S(1)}, f32[13,1024]{1,0:T(8,128)S(1)}, u32[]{:S(2)}, u32[]{:S(2)}) %collective-permute-start.18) | collective-permute-done | bytes 53280 | tf_op jit(solution)/shard_map/ppermute | solution.py:82
  197.0 1.2 collective-permute-start.21
  198.2 0.6 collective-permute-start.20
  199.6 2.6 %collective-permute-done.20 = f32[13,256]{1,0:T(8,128)S(1)} collective-permute-done((f32[13,256]{1,0:T(8,128)S(1)}, f32[13,256]{1,0:T(8,128)S(1)}, u32[]{:S(2)}, u32[]{:S(2)}) %collective-permute-start.20) | collective-permute-done | bytes 13344 | tf_op jit(solution)/shard_map/ppermute | solution.py:82
  203.1 2.1 collective-permute-done.22
  205.4 0.9 collective-permute-start.25
  206.2 0.6 collective-permute-start.24
  207.3 1.0 collective-permute-done.25
  208.2 2.0 collective-permute-done.24
  210.7 11.0 %collective-permute-start.26 = (f32[13,16]{1,0:T(8,128)S(1)}, f32[13,16]{1,0:T(8,128)S(1)}, u32[]{:S(2)}, u32[]{:S(2)}) collective-permute-start(f32[13,16]{1,0:T(8,128)S(1)} %bitcast.131), channel_id=1, source_target_pairs={{0,1},{1,0},{2,3},{3,2},{4,5},{5,4},{6,7},{7,6},{8,9},{9,8},{10,11... | collective-permute-start | bytes 2504 | tf_op jit(solution)/shard_map/ppermute | solution.py:82
  221.6 0.8 collective-permute-done.26
  222.5 0.6 fusion.17
  (113 shorter events, 9.7 us)
Async XLA Ops:
  0.6 2.4 %collective-permute-start = (s32[16]{0:T(128)}, s32[16]{0:T(128)S(1)}, u32[]{:S(2)}, u32[]{:S(2)}) collective-permute-start(s32[16]{0:T(128)} %param.23), channel_id=1, source_target_pairs={{0,1},{1,0},{2,3},{3,2},{4,5},{5,4},{6,7},{7,6},{8,9},{9,8},{10,11... | collective-permute-start | bytes 200 | tf_op jit(solution)/shard_map/ppermute | solution.py:64
  4.4 3.8 %collective-permute-start.3 = (s32[32]{0:T(128)S(1)}, s32[32]{0:T(128)S(1)}, u32[]{:S(2)}, u32[]{:S(2)}) collective-permute-start(s32[32]{0:T(128)S(1)} %select_n.413), channel_id=1, source_target_pairs={{0,6},{1,7},{2,0},{3,1},{4,2},{5,3},{6,4},{7,5},{8,14},{9,15},{10,... | collective-permute-start | bytes 392 | tf_op jit(solution)/shard_map/ppermute | solution.py:64
  7.0 3.9 %collective-permute-start.2 = (s32[32]{0:T(128)S(1)}, s32[32]{0:T(128)S(1)}, u32[]{:S(2)}, u32[]{:S(2)}) collective-permute-start(s32[32]{0:T(128)S(1)} %select_n.413), channel_id=1, source_target_pairs={{0,4},{1,5},{2,6},{3,7},{4,0},{5,1},{6,2},{7,3},{8,12},{9,13},{10,... | collective-permute-start | bytes 392 | tf_op jit(solution)/shard_map/ppermute | solution.py:64
  7.5 3.6 %collective-permute-start.1 = (s32[32]{0:T(128)S(1)}, s32[32]{0:T(128)S(1)}, u32[]{:S(2)}, u32[]{:S(2)}) collective-permute-start(s32[32]{0:T(128)S(1)} %select_n.413), channel_id=1, source_target_pairs={{0,2},{1,3},{2,4},{3,5},{4,6},{5,7},{6,0},{7,1},{8,10},{9,11},{10,... | collective-permute-start | bytes 392 | tf_op jit(solution)/shard_map/ppermute | solution.py:64
  11.9 2.4 %collective-permute-start.4 = (s32[128]{0:T(128)S(1)}, s32[128]{0:T(128)S(1)}, u32[]{:S(2)}, u32[]{:S(2)}) collective-permute-start(s32[128]{0:T(128)S(1)} %select_n.418), channel_id=1, source_target_pairs={{0,8},{1,9},{2,10},{3,11},{4,12},{5,13},{6,14},{7,15},{8,0},{9,1},... | collective-permute-start | bytes 1544 | tf_op jit(solution)/shard_map/ppermute | solution.py:64
  15.0 4.5 %collective-permute-start.7 = (s32[256]{0:T(256)S(1)}, s32[256]{0:T(256)S(1)}, u32[]{:S(2)}, u32[]{:S(2)}) collective-permute-start(s32[256]{0:T(256)S(1)} %fusion.35), channel_id=1, source_target_pairs={{0,48},{1,49},{2,50},{3,51},{4,52},{5,53},{6,54},{7,55},{8,56},{9,... | collective-permute-start | bytes 3080 | tf_op jit(solution)/shard_map/ppermute | solution.py:64
  18.7 3.9 %collective-permute-start.6 = (s32[256]{0:T(256)S(1)}, s32[256]{0:T(256)S(1)}, u32[]{:S(2)}, u32[]{:S(2)}) collective-permute-start(s32[256]{0:T(256)S(1)} %fusion.35), channel_id=1, source_target_pairs={{0,32},{1,33},{2,34},{3,35},{4,36},{5,37},{6,38},{7,39},{8,40},{9,... | collective-permute-start | bytes 3080 | tf_op jit(solution)/shard_map/ppermute | solution.py:64
  18.7 3.9 %collective-permute-start.5 = (s32[256]{0:T(256)S(1)}, s32[256]{0:T(256)S(1)}, u32[]{:S(2)}, u32[]{:S(2)}) collective-permute-start(s32[256]{0:T(256)S(1)} %fusion.35), channel_id=1, source_target_pairs={{0,16},{1,17},{2,18},{3,19},{4,20},{5,21},{6,22},{7,23},{8,24},{9,... | collective-permute-start | bytes 3080 | tf_op jit(solution)/shard_map/ppermute | solution.py:64
  23.3 9.7 %collective-permute-start.8 = (s32[1024]{0:T(1024)S(1)}, s32[1024]{0:T(1024)S(1)}, u32[]{:S(2)}, u32[]{:S(2)}) collective-permute-start(s32[1024]{0:T(1024)S(1)} %bitcast.132), channel_id=1, source_target_pairs={{0,64},{1,65},{2,66},{3,67},{4,68},{5,69},{6,70},{7,71},{8,72},{9,... | collective-permute-start | bytes 12296 | tf_op jit(solution)/shard_map/ppermute | solution.py:64
  30.3 25.0 %copy-start.4 = (f32[8192]{0:T(1024)S(1)}, f32[8192]{0:T(1024)}, u32[]{:S(2)}) copy-start(f32[8192]{0:T(1024)} %param.22) | copy-start | bytes 98308
  30.3 30.4 %copy-start = (f32[3,8192]{1,0:T(4,128)S(1)}, f32[3,8192]{1,0:T(4,128)}, u32[]{:S(2)}) copy-start(f32[3,8192]{1,0:T(4,128)} %param.17) | copy-start | bytes 294916
  30.3 30.4 %copy-start.1 = (f32[3,8192]{1,0:T(4,128)S(1)}, f32[3,8192]{1,0:T(4,128)}, u32[]{:S(2)}) copy-start(f32[3,8192]{1,0:T(4,128)} %param.18) | copy-start | bytes 294916
  30.4 30.4 %copy-start.2 = (f32[3,8192]{1,0:T(4,128)S(1)}, f32[3,8192]{1,0:T(4,128)}, u32[]{:S(2)}) copy-start(f32[3,8192]{1,0:T(4,128)} %param.19) | copy-start | bytes 294916
  30.4 30.4 %copy-start.3 = (f32[3,8192]{1,0:T(4,128)S(1)}, f32[3,8192]{1,0:T(4,128)}, u32[]{:S(2)}) copy-start(f32[3,8192]{1,0:T(4,128)} %param.20) | copy-start | bytes 294916
  30.4 34.5 %copy-start.5 = (f32[8192]{0:T(1024)S(1)}, f32[8192]{0:T(1024)}, u32[]{:S(2)}) copy-start(f32[8192]{0:T(1024)} %param.21) | copy-start | bytes 98308
  42.0 5.9 %collective-permute-start.9 = (f32[6,2048]{1,0:T(8,128)S(1)}, f32[6,2048]{1,0:T(8,128)S(1)}, u32[]{:S(2)}, u32[]{:S(2)}) collective-permute-start(f32[6,2048]{1,0:T(8,128)S(1)} %pad_maximum_fusion.1), channel_id=1, source_target_pairs={{0,1},{1,0},{2,3},{3,2},{4,5},{5,4},{6,7},{7,6},{8,9},{9,8},{10,11... | collective-permute-start | bytes 147464 | tf_op jit(solution)/shard_map/ppermute | solution.py:90
  47.9 3.2 %collective-permute-start.12 = (f32[6,2048]{1,0:T(8,128)S(1)}, f32[6,2048]{1,0:T(8,128)S(1)}, u32[]{:S(2)}, u32[]{:S(2)}) collective-permute-start(f32[6,2048]{1,0:T(8,128)S(1)} %fusion.33), channel_id=1, source_target_pairs={{0,6},{1,7},{2,0},{3,1},{4,2},{5,3},{6,4},{7,5},{8,14},{9,15},{10,... | collective-permute-start | bytes 147464 | tf_op jit(solution)/shard_map/ppermute | solution.py:90
  48.0 4.7 %collective-permute-start.11 = (f32[6,2048]{1,0:T(8,128)S(1)}, f32[6,2048]{1,0:T(8,128)S(1)}, u32[]{:S(2)}, u32[]{:S(2)}) collective-permute-start(f32[6,2048]{1,0:T(8,128)S(1)} %fusion.33), channel_id=1, source_target_pairs={{0,4},{1,5},{2,6},{3,7},{4,0},{5,1},{6,2},{7,3},{8,12},{9,13},{10,... | collective-permute-start | bytes 147464 | tf_op jit(solution)/shard_map/ppermute | solution.py:90
  49.3 5.5 %collective-permute-start.10 = (f32[6,2048]{1,0:T(8,128)S(1)}, f32[6,2048]{1,0:T(8,128)S(1)}, u32[]{:S(2)}, u32[]{:S(2)}) collective-permute-start(f32[6,2048]{1,0:T(8,128)S(1)} %fusion.33), channel_id=1, source_target_pairs={{0,2},{1,3},{2,4},{3,5},{4,6},{5,7},{6,0},{7,1},{8,10},{9,11},{10,... | collective-permute-start | bytes 147464 | tf_op jit(solution)/shard_map/ppermute | solution.py:90
  54.8 3.2 %collective-permute-start.13 = (f32[6,2048]{1,0:T(8,128)S(1)}, f32[6,2048]{1,0:T(8,128)S(1)}, u32[]{:S(2)}, u32[]{:S(2)}) collective-permute-start(f32[6,2048]{1,0:T(8,128)S(1)} %add_add_fusion.1), channel_id=1, source_target_pairs={{0,8},{1,9},{2,10},{3,11},{4,12},{5,13},{6,14},{7,15},{8,0},{9,1},... | collective-permute-start | bytes 147464 | tf_op jit(solution)/shard_map/ppermute | solution.py:90
  58.1 3.2 %collective-permute-start.16 = (f32[6,2048]{1,0:T(8,128)S(1)}, f32[6,2048]{1,0:T(8,128)S(1)}, u32[]{:S(2)}, u32[]{:S(2)}) collective-permute-start(f32[6,2048]{1,0:T(8,128)S(1)} %add.420), channel_id=1, source_target_pairs={{0,48},{1,49},{2,50},{3,51},{4,52},{5,53},{6,54},{7,55},{8,56},{9,... | collective-permute-start | bytes 147464 | tf_op jit(solution)/shard_map/ppermute | solution.py:90
  58.4 4.6 %collective-permute-start.15 = (f32[6,2048]{1,0:T(8,128)S(1)}, f32[6,2048]{1,0:T(8,128)S(1)}, u32[]{:S(2)}, u32[]{:S(2)}) collective-permute-start(f32[6,2048]{1,0:T(8,128)S(1)} %add.420), channel_id=1, source_target_pairs={{0,32},{1,33},{2,34},{3,35},{4,36},{5,37},{6,38},{7,39},{8,40},{9,... | collective-permute-start | bytes 147464 | tf_op jit(solution)/shard_map/ppermute | solution.py:90
  60.0 4.3 %collective-permute-start.14 = (f32[6,2048]{1,0:T(8,128)S(1)}, f32[6,2048]{1,0:T(8,128)S(1)}, u32[]{:S(2)}, u32[]{:S(2)}) collective-permute-start(f32[6,2048]{1,0:T(8,128)S(1)} %add.420), channel_id=1, source_target_pairs={{0,16},{1,17},{2,18},{3,19},{4,20},{5,21},{6,22},{7,23},{8,24},{9,... | collective-permute-start | bytes 147464 | tf_op jit(solution)/shard_map/ppermute | solution.py:90
  64.3 4.7 %collective-permute-start.17 = (f32[6,2048]{1,0:T(8,128)S(1)}, f32[6,2048]{1,0:T(8,128)S(1)}, u32[]{:S(2)}, u32[]{:S(2)}) collective-permute-start(f32[6,2048]{1,0:T(8,128)S(1)} %add_add_fusion), channel_id=1, source_target_pairs={{0,64},{1,65},{2,66},{3,67},{4,68},{5,69},{6,70},{7,71},{8,72},{9,... | collective-permute-start | bytes 147464 | tf_op jit(solution)/shard_map/ppermute | solution.py:90
  192.2 4.7 %collective-permute-start.18 = (f32[13,1024]{1,0:T(8,128)S(1)}, f32[13,1024]{1,0:T(8,128)S(1)}, u32[]{:S(2)}, u32[]{:S(2)}) collective-permute-start(f32[13,1024]{1,0:T(8,128)S(1)} %select_bitcast_fusion.1), channel_id=1, source_target_pairs={{0,64},{1,65},{2,66},{3,67},{4,68},{5,69},{6,70},{7,71},{8,72},{9,... | collective-permute-start | bytes 159752 | tf_op jit(solution)/shard_map/ppermute | solution.py:82
  197.0 2.7 %collective-permute-start.21 = (f32[13,256]{1,0:T(8,128)S(1)}, f32[13,256]{1,0:T(8,128)S(1)}, u32[]{:S(2)}, u32[]{:S(2)}) collective-permute-start(f32[13,256]{1,0:T(8,128)S(1)} %bitcast.127), channel_id=1, source_target_pairs={{0,48},{1,49},{2,50},{3,51},{4,52},{5,53},{6,54},{7,55},{8,56},{9,... | collective-permute-start | bytes 39944 | tf_op jit(solution)/shard_map/ppermute | solution.py:82
  198.2 4.1 %collective-permute-start.20 = (f32[13,256]{1,0:T(8,128)S(1)}, f32[13,256]{1,0:T(8,128)S(1)}, u32[]{:S(2)}, u32[]{:S(2)}) collective-permute-start(f32[13,256]{1,0:T(8,128)S(1)} %fusion), channel_id=1, source_target_pairs={{0,32},{1,33},{2,34},{3,35},{4,36},{5,37},{6,38},{7,39},{8,40},{9,... | collective-permute-start | bytes 39944 | tf_op jit(solution)/shard_map/ppermute | solution.py:82
  198.8 3.8 %collective-permute-start.19 = (f32[13,256]{1,0:T(8,128)S(1)}, f32[13,256]{1,0:T(8,128)S(1)}, u32[]{:S(2)}, u32[]{:S(2)}) collective-permute-start(f32[13,256]{1,0:T(8,128)S(1)} %fusion.1), channel_id=1, source_target_pairs={{0,16},{1,17},{2,18},{3,19},{4,20},{5,21},{6,22},{7,23},{8,24},{9,... | collective-permute-start | bytes 39944 | tf_op jit(solution)/shard_map/ppermute | solution.py:82
  202.6 2.6 %collective-permute-start.22 = (f32[13,128]{1,0:T(8,128)S(1)}, f32[13,128]{1,0:T(8,128)S(1)}, u32[]{:S(2)}, u32[]{:S(2)}) collective-permute-start(f32[13,128]{1,0:T(8,128)S(1)} %bitcast.129), channel_id=1, source_target_pairs={{0,8},{1,9},{2,10},{3,11},{4,12},{5,13},{6,14},{7,15},{8,0},{9,1},... | collective-permute-start | bytes 19976 | tf_op jit(solution)/shard_map/ppermute | solution.py:82
  205.4 2.9 %collective-permute-start.25 = (f32[13,32]{1,0:T(8,128)S(1)}, f32[13,32]{1,0:T(8,128)S(1)}, u32[]{:S(2)}, u32[]{:S(2)}) collective-permute-start(f32[13,32]{1,0:T(8,128)S(1)} %bitcast.130), channel_id=1, source_target_pairs={{0,6},{1,7},{2,0},{3,1},{4,2},{5,3},{6,4},{7,5},{8,14},{9,15},{10,... | collective-permute-start | bytes 5000 | tf_op jit(solution)/shard_map/ppermute | solution.py:82
  206.2 4.0 %collective-permute-start.24 = (f32[13,32]{1,0:T(8,128)S(1)}, f32[13,32]{1,0:T(8,128)S(1)}, u32[]{:S(2)}, u32[]{:S(2)}) collective-permute-start(f32[13,32]{1,0:T(8,128)S(1)} %fusion.8), channel_id=1, source_target_pairs={{0,4},{1,5},{2,6},{3,7},{4,0},{5,1},{6,2},{7,3},{8,12},{9,13},{10,... | collective-permute-start | bytes 5000 | tf_op jit(solution)/shard_map/ppermute | solution.py:82
  206.8 3.7 %collective-permute-start.23 = (f32[13,32]{1,0:T(8,128)S(1)}, f32[13,32]{1,0:T(8,128)S(1)}, u32[]{:S(2)}, u32[]{:S(2)}) collective-permute-start(f32[13,32]{1,0:T(8,128)S(1)} %fusion.9), channel_id=1, source_target_pairs={{0,2},{1,3},{2,4},{3,5},{4,6},{5,7},{6,0},{7,1},{8,10},{9,11},{10,... | collective-permute-start | bytes 5000 | tf_op jit(solution)/shard_map/ppermute | solution.py:82
  210.7 11.8 %collective-permute-start.26 = (f32[13,16]{1,0:T(8,128)S(1)}, f32[13,16]{1,0:T(8,128)S(1)}, u32[]{:S(2)}, u32[]{:S(2)}) collective-permute-start(f32[13,16]{1,0:T(8,128)S(1)} %bitcast.131), channel_id=1, source_target_pairs={{0,1},{1,0},{2,3},{3,2},{4,5},{5,4},{6,7},{7,6},{8,9},{9,8},{10,11... | collective-permute-start | bytes 2504 | tf_op jit(solution)/shard_map/ppermute | solution.py:82

commit v5 on v4

--- a/solution.py
+++ b/solution.py
@@ -1,4 +1,6 @@
 import functools
+
+import math
 
 import jax
 import jax.numpy as jnp
@@ -9,7 +11,9 @@
 
 softening = 0.001
 ALL = ("blk", "group")
-LEVELS = (("core", 1, 2), ("x", 2, 4), ("y_lo", 8, 2), ("z", 16, 4), ("y_hi", 64, 2))
+GROUP_LEVELS = (("core", 1, 2), ("x", 2, 4), ("y_lo", 8, 2))
+BLK_LEVELS = (("z", 16, 4), ("y_hi", 64, 2))
+LEVELS = GROUP_LEVELS + BLK_LEVELS
 SUB = 2
 
 
@@ -91,78 +95,111 @@
     return total
 
 
-def forces_kernel(act_ref, fld_ref, out_ref):
+def forces_kernel(act_ref, fld_ref, out_ref, bfld, acc):
     num_k = act_ref.shape[0]
-    num_j = fld_ref.shape[2]
+    num_j = fld_ref.shape[1]
+    width = bfld.shape[2]
     step_k = 8 * SUB
-
-    def kblock(kb, carry):
-        k0 = pl.multiple_of(kb * step_k, step_k)
-        acts = []
-        for s in range(SUB):
-            a = act_ref[pl.ds(k0 + 8 * s, 8), :]
-            acts.append([jnp.broadcast_to(a[:, c:c + 1], (8, 128)) for c in range(6)])
-
-        def jstep(jc, accs):
-            j0 = pl.multiple_of(jc * 128, 128)
-            f = [fld_ref[c, :, pl.ds(j0, 128)] for c in range(7)]
-            new = []
+    acc[...] = jnp.zeros(acc.shape, jnp.float32)
+
+    def jblock(jb, carry):
+        base = pl.multiple_of(jb * width, width)
+
+        def spread(ci, c2):
+            j0 = pl.multiple_of(ci * 128, 128)
+            for c in range(7):
+                row = fld_ref[c:c + 1, pl.ds(base + j0, 128)]
+                bfld[c, :, pl.ds(j0, 128)] = jnp.broadcast_to(row, (8, 128))
+            return c2
+
+        lax.fori_loop(0, width // 128, spread, 0, unroll=4)
+
+        def kblock(kb, c3):
+            k0 = pl.multiple_of(kb * step_k, step_k)
+            acts = []
             for s in range(SUB):
-                ax, ay, az, avx, avy, avz = acts[s]
-                dx = f[0] - ax
-                dy = f[1] - ay
-                dz = f[2] - az
-                mx = f[3] - avx
-                my = f[4] - avy
-                mz = f[5] - avz
-                dist_sq = dx * dx + dy * dy + dz * dz + softening
-                inverse = lax.rsqrt(dist_sq)
-                inv2 = inverse * inverse
-                weight = f[6] * inv2 * inverse
-                factor = 3.0 * (dx * mx + dy * my + dz * mz) * inv2
-                a6 = accs[s]
-                new.append((
-                    a6[0] + dx * weight,
-                    a6[1] + dy * weight,
-                    a6[2] + dz * weight,
-                    a6[3] + (mx - factor * dx) * weight,
-                    a6[4] + (my - factor * dy) * weight,
-                    a6[5] + (mz - factor * dz) * weight,
-                ))
-            return tuple(new)
-
-        zero = jnp.zeros((8, 128), jnp.float32)
-        init = tuple(tuple(zero for _ in range(6)) for _ in range(SUB))
-        accs = lax.fori_loop(0, num_j // 128, jstep, init, unroll=16)
-        for s in range(SUB):
-            for c in range(6):
-                out_ref[pl.ds(k0 + 8 * s, 8), c:c + 1] = jnp.sum(accs[s][c], axis=1, keepdims=True)
+                a = act_ref[pl.ds(k0 + 8 * s, 8), :]
+                acts.append([jnp.broadcast_to(a[:, c:c + 1], (8, 128)) for c in range(6)])
+
+            def jstep(jc, accs):
+                j0 = pl.multiple_of(jc * 128, 128)
+                f = [bfld[c, :, pl.ds(j0, 128)] for c in range(7)]
+                new = []
+                for s in range(SUB):
+                    ax, ay, az, avx, avy, avz = acts[s]
+                    dx = f[0] - ax
+                    dy = f[1] - ay
+                    dz = f[2] - az
+                    mx = f[3] - avx
+                    my = f[4] - avy
+                    mz = f[5] - avz
+                    dist_sq = dx * dx + dy * dy + dz * dz + softening
+                    inverse = lax.rsqrt(dist_sq)
+                    inv2 = inverse * inverse
+                    weight = f[6] * inv2 * inverse
+                    factor = 3.0 * (dx * mx + dy * my + dz * mz) * inv2
+                    a6 = accs[s]
+                    new.append((
+                        a6[0] + dx * weight,
+                        a6[1] + dy * weight,
+                        a6[2] + dz * weight,
+                        a6[3] + (mx - factor * dx) * weight,
+                        a6[4] + (my - factor * dy) * weight,
+                        a6[5] + (mz - factor * dz) * weight,
+                    ))
+                return tuple(new)
+
+            slot = kb * SUB
+            init = tuple(tuple(acc[slot + s, c] for c in range(6)) for s in range(SUB))
+            accs = lax.fori_loop(0, width // 128, jstep, init, unroll=16)
+            for s in range(SUB):
+                for c in range(6):
+                    acc[slot + s, c] = accs[s][c]
+            return c3
+
+        lax.fori_loop(0, num_k // step_k, kblock, 0)
         return carry
 
-    lax.fori_loop(0, num_k // step_k, kblock, 0)
-
-
-def pair_forces(active_t, field_b):
+    lax.fori_loop(0, num_j // width, jblock, 0)
+    for kb in range(num_k // 8):
+        for c in range(6):
+            out_ref[pl.ds(8 * kb, 8), c:c + 1] = jnp.sum(acc[kb, c], axis=1, keepdims=True)
+
+
+def pair_forces(active_t, field):
     num_k = active_t.shape[0]
+    width = math.gcd(field.shape[1], 8192)
     return pl.pallas_call(
         forces_kernel,
         out_shape=jax.ShapeDtypeStruct((num_k, 8), jnp.float32),
-    )(active_t, field_b)
+        scratch_shapes=[
+            pltpu.VMEM((7, 8, width), jnp.float32),
+            pltpu.VMEM((num_k // 8, 6, 8, 128), jnp.float32),
+        ],
+    )(active_t, field)
+
+
+def concat_level(x, level, ndev):
+    _, stride, size = level
+    parts = [x] + [lax.ppermute(x, ALL, _perm(stride, size, s, ndev)) for s in range(1, size)]
+    return jnp.concatenate(parts, axis=-1)
 
 
 def on_device(positions, velocities, accelerations, jerk_rates, masses, elapsed_time, active_index):
-    ndev = lax.axis_size("blk") * lax.axis_size("group")
+    num_blk = lax.axis_size("blk")
+    num_group = lax.axis_size("group")
+    ndev = num_blk * num_group
     own_stars = positions.shape[1]
+    own_active = active_index.shape[0]
     total_stars = own_stars * ndev
     gravity = 1.0 / total_stars
+    pred_pos, pred_vel = predict(positions, velocities, accelerations, jerk_rates, elapsed_time)
+    field = jnp.concatenate([pred_pos, pred_vel, masses[None, :]], axis=0)
+    for level in (GROUP_LEVELS[2], GROUP_LEVELS[1], GROUP_LEVELS[0]):
+        field = concat_level(field, level, ndev)
     every_index = active_index
     for level in LEVELS:
         every_index = gather_level(every_index, level, ndev)
-    pred_pos, pred_vel = predict(positions, velocities, accelerations, jerk_rates, elapsed_time)
-    own_field = jnp.concatenate(
-        [pred_pos, pred_vel, masses[None, :], jnp.zeros_like(masses)[None, :]], axis=0
-    )
-    field_b = jnp.broadcast_to(own_field[:, None, :], (8, 8, own_stars))
     packed = jnp.concatenate(
         [positions, velocities, accelerations, jerk_rates, elapsed_time[None, :]], axis=0
     )
@@ -172,16 +209,22 @@
     picked = jnp.take(packed, jnp.clip(local_row, 0, own_stars - 1), axis=1)
     picked = jnp.where(is_owned[None, :], picked, 0.0)
     act_pos, act_vel = predict(picked[0:3], picked[3:6], picked[6:9], picked[9:12], picked[12])
-    num_k = picked.shape[1]
-    active = jnp.concatenate([act_pos, act_vel], axis=0)
-    for level in LEVELS:
-        active = sum_level(active, level, ndev)
-    active_t = jnp.concatenate([active, jnp.zeros((2, num_k), jnp.float32)], axis=0).T
-    partial = pair_forces(active_t, field_b)[:, 0:6].T
-    payload = jnp.concatenate([partial, corrector_terms(picked)], axis=0)
-    for level in reversed(LEVELS):
+    payload = jnp.concatenate([act_pos, act_vel, corrector_terms(picked)], axis=0)
+    rows = payload.shape[0]
+    payload = payload.reshape(rows, num_blk, num_group, own_active)
+    payload = payload.transpose(0, 2, 1, 3).reshape(rows, ndev * own_active)
+    for level in reversed(GROUP_LEVELS):
         payload = reduce_level(payload, level, ndev)
-    return corrector(payload[6:13], payload[0:6] * gravity)
+    for level in BLK_LEVELS:
+        payload = sum_level(payload, level, ndev)
+    num_k = payload.shape[1]
+    active_t = jnp.concatenate([payload[0:6], jnp.zeros((2, num_k), jnp.float32)], axis=0).T
+    partial = pair_forces(active_t, field)[:, 0:6].T
+    for level in reversed(BLK_LEVELS):
+        partial = reduce_level(partial, level, ndev)
+    mine = lax.axis_index("blk") * own_active
+    terms = lax.dynamic_slice_in_dim(payload[6:13], mine, own_active, axis=1)
+    return corrector(terms, partial * gravity)
 
 
 def solution(mesh):

time: 223 us -> 240 us (1.076); the launches traced: 223 us -> 236 us
  waiting for transfers between devices: 37 us -> 47.4 us
  local copies, waits for them, and re-layouts: 23.2 us -> 31.1 us
  starting transfers between devices: 40.8 us -> 36 us
  Pallas kernels: 118 us -> 114 us
  other arithmetic: 2.71 us -> 6.3 us
    ppermute x0 -> x5, waiting for transfers between devices: none -> 18.6 us  [concat_level(): lax.ppermute(x, ALL, _perm(stride, size, s, ndev))]
    ppermute x0 -> x5, starting transfers between devices: none -> 9.41 us  [concat_level(): lax.ppermute(x, ALL, _perm(stride, size, s, ndev))]
    ppermute x9, starting transfers between devices: 16 us -> 8.29 us  [reduce_level(): total = total + lax.ppermute(piece, ALL, _perm(stride, size, s, ndev))]
    ppermute x9 -> x4, waiting for transfers between devices: 15.3 us -> 7.68 us  [sum_level(): total = total + lax.ppermute(x, ALL, _perm(stride, size, s, ndev))]
    ppermute x9 -> x4, starting transfers between devices: 10.9 us -> 4.07 us  [sum_level(): total = total + lax.ppermute(x, ALL, _perm(stride, size, s, ndev))]
    unnamed x19 -> x16, local copies, waits for them, and re-layouts: 0.07 us -> 6.27 us
    pallas_call x1, Pallas kernels: 118 us -> 114 us  [pair_forces(): pl.pallas_call(forces_kernel, out_shape=jax.ShapeDtypeStruct((num_k, 8),...]
    concatenate x1 -> x3, local copies, waits for them, and re-layouts: 0.07 us -> 4.31 us  [the longest x2 4.1 us: concat_level(): return jnp.concatenate(parts, axis=-1)]
  transfers between devices with their start and end apart: 27 -> 27, of which waited for: 23 -> 21; matrix products, arithmetic and copies ran while one was open for 3% -> 11% of each run, Pallas kernels for 0% -> 0%
where the time goes in v5:
time: 240 us; the launch traced here: 236 us
  Pallas kernels  114 us (48%)
  waiting for transfers between devices  47.4 us (20%)
  starting transfers between devices  36 us (15%)
  local copies, waits for them, and re-layouts  31.1 us (13%)
  other arithmetic  6.3 us (3%)
    pallas_call x1, Pallas kernels, pair_forces(): pl.pallas_call(forces_kernel, out_shape=jax.ShapeDtypeStruct((num_k, 8),...  114 us
    ppermute x5, waiting for transfers between devices, concat_level(): lax.ppermute(x, ALL, _perm(stride, size, s, ndev))  18.6 us
    ppermute x9, waiting for transfers between devices, reduce_level(): total = total + lax.ppermute(piece, ALL, _perm(stride, size, s, ndev))  16.1 us
    ppermute x9, starting transfers between devices, gather_level(): lax.ppermute(x, ALL, _perm(stride, size, s, ndev))  14.3 us
    ppermute x5, starting transfers between devices, concat_level(): lax.ppermute(x, ALL, _perm(stride, size, s, ndev))  9.41 us
    ppermute x9, starting transfers between devices, reduce_level(): total = total + lax.ppermute(piece, ALL, _perm(stride, size, s, ndev))  8.29 us
    gather x2, local copies, waits for them, and re-layouts, on_device(): picked = jnp.take(packed, jnp.clip(local_row, 0, own_stars - 1), axis=1)  7.98 us
    ppermute x4, waiting for transfers between devices, sum_level(): total = total + lax.ppermute(x, ALL, _perm(stride, size, s, ndev))  7.68 us
  transfers between devices with their start and end apart: 27, of which 21 were waited for; matrix products, arithmetic and copies ran while one was open for 11% of the time, Pallas kernels for 0%

profile of v5, /device:TPU:1, one launch (start us, length us, event | category | flops | bytes accessed | tf_op | source)
XLA Modules:
  0.0 235.6 jit_solution(15074984215976332825)
XLA Ops:
  0.6 0.8 broadcast_multiply_fusion.1
  1.4 1.2 multiply_add_fusion.1
  2.6 1.6 constant_dynamic-update-slice_fusion.4
  4.2 2.1 collective-permute-start.18
  6.3 1.0 collective-permute-start
  7.3 0.7 constant_dynamic-update-slice_fusion.10
  8.2 0.7 pad_add_fusion.3
  9.6 1.2 collective-permute-start.1
  10.8 2.5 %collective-permute-start.2 = (s32[32]{0:T(128)S(1)}, s32[32]{0:T(128)S(1)}, u32[]{:S(2)}, u32[]{:S(2)}) collective-permute-start(s32[32]{0:T(128)S(1)} %select_n.416), channel_id=1, source_target_pairs={{0,4},{1,5},{2,6},{3,7},{4,0},{5,1},{6,2},{7,3},{8,12},{9,13},{10,... | collective-permute-start | bytes 392 | tf_op jit(solution)/shard_map/ppermute | solution.py:68
  13.3 1.2 collective-permute-start.3
  14.7 0.9 collective-permute-done.3
  16.7 2.2 collective-permute-done.4
  19.5 1.6 collective-permute-start.5
  21.1 3.3 %collective-permute-start.6 = (s32[256]{0:T(256)S(1)}, s32[256]{0:T(256)S(1)}, u32[]{:S(2)}, u32[]{:S(2)}) collective-permute-start(s32[256]{0:T(256)S(1)} %fusion.26), channel_id=1, source_target_pairs={{0,32},{1,33},{2,34},{3,35},{4,36},{5,37},{6,38},{7,39},{8,40},{9,... | collective-permute-start | bytes 3080 | tf_op jit(solution)/shard_map/ppermute | solution.py:68
  24.4 0.7 collective-permute-start.7
  25.4 1.5 collective-permute-done.7
  27.5 2.6 %collective-permute-start.8 = (s32[1024]{0:T(1024)S(1)}, s32[1024]{0:T(1024)S(1)}, u32[]{:S(2)}, u32[]{:S(2)}) collective-permute-start(s32[1024]{0:T(1024)S(1)} %bitcast.131), channel_id=1, source_target_pairs={{0,64},{1,65},{2,66},{3,67},{4,68},{5,69},{6,70},{7,71},{8,72},{9,... | collective-permute-start | bytes 12296 | tf_op jit(solution)/shard_map/ppermute | solution.py:68
  30.2 4.0 %concatenate.23 = f32[13,8192]{1,0:T(8,128)S(1)} concatenate(f32[3,8192]{1,0:T(4,128)} %param.17, f32[3,8192]{1,0:T(4,128)} %param.18, f32[3,8192]{1,0:T(4,128)} %param.19, f32[3,8192]{1,0:T(4,128)} %param.20, f32[1,8192]{1,0:T(1,128)} %bitcast.113), dimensions={0} | concatenate | bytes 851968 | tf_op jit(solution)/shard_map/concatenate | solution.py:203
  34.2 2.7 %copy.64 = f32[13,8192]{0,1:T(8,128)} copy(f32[13,8192]{1,0:T(8,128)S(1)} %concatenate.23) | data formatting | bytes 851968 | tf_op jit(solution)/shard_map/concatenate | solution.py:203
  37.7 7.6 %gather_fusion.5 = f32[2048,13]{1,0:T(8,128)S(1)} fusion(f32[13,8192]{0,1:T(8,128)} %copy.64, s32[2048]{0:T(1024)S(1)} %broadcast_clamp_fusion), kind=kCustom, calls=%fused_computation.5 | custom fusion | bytes 221184 | tf_op jit(solution)/shard_map/jit(_take)/gather | solution.py:209
  46.6 3.0 %collective-permute-start.20 = (f32[7,16384]{1,0:T(8,128)S(1)}, f32[7,16384]{1,0:T(8,128)S(1)}, u32[]{:S(2)}, u32[]{:S(2)}) collective-permute-start(f32[7,16384]{1,0:T(8,128)S(1)} %pad_maximum_fusion), channel_id=1, source_target_pairs={{0,4},{1,5},{2,6},{3,7},{4,0},{5,1},{6,2},{7,3},{8,12},{9,13},{10,... | collective-permute-start | bytes 1376264 | tf_op jit(solution)/shard_map/ppermute | solution.py:184
  49.9 0.8 constant_dynamic-update-slice_fusion.3
  50.7 4.5 %collective-permute-done.19 = f32[7,16384]{1,0:T(8,128)S(1)} collective-permute-done((f32[7,16384]{1,0:T(8,128)S(1)}, f32[7,16384]{1,0:T(8,128)S(1)}, u32[]{:S(2)}, u32[]{:S(2)}) %collective-permute-start.19) | collective-permute-done | bytes 458784 | tf_op jit(solution)/shard_map/ppermute | solution.py:184
  55.3 1.1 constant_dynamic-update-slice_fusion.2
  56.3 11.0 %collective-permute-done.20 = f32[7,16384]{1,0:T(8,128)S(1)} collective-permute-done((f32[7,16384]{1,0:T(8,128)S(1)}, f32[7,16384]{1,0:T(8,128)S(1)}, u32[]{:S(2)}, u32[]{:S(2)}) %collective-permute-start.20) | collective-permute-done | bytes 458784 | tf_op jit(solution)/shard_map/ppermute | solution.py:184
  67.3 1.0 constant_dynamic-update-slice_fusion.1
  68.4 3.0 %collective-permute-done.21 = f32[7,16384]{1,0:T(8,128)S(1)} collective-permute-done((f32[7,16384]{1,0:T(8,128)S(1)}, f32[7,16384]{1,0:T(8,128)S(1)}, u32[]{:S(2)}, u32[]{:S(2)}) %collective-permute-start.21) | collective-permute-done | bytes 458784 | tf_op jit(solution)/shard_map/ppermute | solution.py:184
  71.4 1.0 constant_dynamic-update-slice_fusion
  72.4 3.4 %collective-permute-start.22 = (f32[7,65536]{1,0:T(8,128)}, f32[7,65536]{1,0:T(8,128)}, u32[]{:S(2)}, u32[]{:S(2)}) collective-permute-start(f32[7,65536]{1,0:T(8,128)} %get-tuple-element.88), channel_id=1, source_target_pairs={{0,1},{1,0},{2,3},{3,2},{4,5},{5,4},{6,7},{7,6},{8,9},{9,8},{10,11... | collective-permute-start | bytes 5505032 | tf_op jit(solution)/shard_map/ppermute | solution.py:184
  77.4 3.6 %collective-permute-done.9 = f32[13,1024]{1,0:T(8,128)S(1)} collective-permute-done((f32[13,1024]{1,0:T(8,128)S(1)}, f32[13,1024]{1,0:T(8,128)S(1)}, u32[]{:S(2)}, u32[]{:S(2)}) %collective-permute-start.9) | collective-permute-done | bytes 53280 | tf_op jit(solution)/shard_map/ppermute | solution.py:86
  81.3 2.2 collective-permute-start.11
  84.0 3.4 %collective-permute-done.10 = f32[13,256]{0,1:T(8,128)S(1)} collective-permute-done((f32[13,256]{0,1:T(8,128)S(1)}, f32[13,256]{0,1:T(8,128)S(1)}, u32[]{:S(2)}, u32[]{:S(2)}) %collective-permute-start.10) | collective-permute-done | bytes 13344 | tf_op jit(solution)/shard_map/ppermute | solution.py:86
  87.4 1.7 collective-permute-done.11
  89.1 0.8 collective-permute-done.12
  90.0 2.0 collective-permute-start.13
  92.0 0.9 collective-permute-done.13
  93.0 3.1 %collective-permute-start.15 = (f32[13,128]{0,1:T(8,128)S(1)}, f32[13,128]{0,1:T(8,128)S(1)}, u32[]{:S(2)}, u32[]{:S(2)}) collective-permute-start(f32[13,128]{0,1:T(8,128)S(1)} %bitcast_add_fusion.1), channel_id=1, source_target_pairs={{0,32},{1,33},{2,34},{3,35},{4,36},{5,37},{6,38},{7,39},{8,40},{9,... | collective-permute-start | bytes 19976 | tf_op jit(solution)/shard_map/ppermute | solution.py:94
  96.6 0.7 collective-permute-done.14
  97.3 1.7 collective-permute-done.15
  99.0 0.9 collective-permute-done.16
  100.4 4.3 %collective-permute-done.17 = f32[13,128]{0,1:T(8,128)S(1)} collective-permute-done((f32[13,128]{0,1:T(8,128)S(1)}, f32[13,128]{0,1:T(8,128)S(1)}, u32[]{:S(2)}, u32[]{:S(2)}) %collective-permute-start.17) | collective-permute-done | bytes 6688 | tf_op jit(solution)/shard_map/ppermute | solution.py:94
  105.4 3.1 %constant_dynamic-update-slice_fusion.5.fld_ref = f32[7,131072]{1,0:T(8,128)} fusion(f32[7,131072]{1,0:T(8,128)} %get-tuple-element.89, f32[7,65536]{1,0:T(8,128)} %collective-permute-done.22), kind=kLoop, calls=%fused_computation.39 | loop fusion | bytes 4194304 | tf_op jit(solution)/shard_map/concatenate | solution.py:185
  108.4 113.7 %shard_map.102 = f32[128,8]{1,0:T(8,128)} custom-call(f32[128,8]{1,0:T(8,128)} %fusion.2.act_ref, f32[7,131072]{1,0:T(8,128)} %constant_dynamic-update-slice_fusion.5.fld_ref), custom_call_target="tpu_custom_call" | custom-call | tf_op jit(solution)/shard_map/pallas_call | solution.py:172
  222.1 0.9 copy.69
  223.5 3.5 %collective-permute-done.23 = f32[6,64]{1,0:T(8,128)S(1)} collective-permute-done((f32[6,64]{1,0:T(8,128)S(1)}, f32[6,64]{1,0:T(8,128)S(1)}, u32[]{:S(2)}, u32[]{:S(2)}) %collective-permute-start.23) | collective-permute-done | bytes 1568 | tf_op jit(solution)/shard_map/ppermute | solution.py:86
  227.4 2.9 %collective-permute-start.25 = (f32[6,16]{0,1:T(8,128)S(1)}, f32[6,16]{0,1:T(8,128)S(1)}, u32[]{:S(2)}, u32[]{:S(2)}) collective-permute-start(f32[6,16]{0,1:T(8,128)S(1)} %bitcast.129), channel_id=1, source_target_pairs={{0,32},{1,33},{2,34},{3,35},{4,36},{5,37},{6,38},{7,39},{8,40},{9,... | collective-permute-start | bytes 1160 | tf_op jit(solution)/shard_map/ppermute | solution.py:86
  231.4 1.5 collective-permute-done.26
  233.0 0.7 copy.74
  (103 shorter events, 13.9 us)
Async XLA Ops:
  4.2 41.6 %collective-permute-start.18 = (f32[7,8192]{1,0:T(8,128)S(1)}, f32[7,8192]{1,0:T(8,128)S(1)}, u32[]{:S(2)}, u32[]{:S(2)}) collective-permute-start(f32[7,8192]{1,0:T(8,128)S(1)} %get-tuple-element.85), channel_id=1, source_target_pairs={{0,8},{1,9},{2,10},{3,11},{4,12},{5,13},{6,14},{7,15},{8,0},{9,1},... | collective-permute-start | bytes 688136 | tf_op jit(solution)/shard_map/ppermute | solution.py:184
  6.3 1.9 collective-permute-start
  9.6 4.9 %collective-permute-start.1 = (s32[32]{0:T(128)S(1)}, s32[32]{0:T(128)S(1)}, u32[]{:S(2)}, u32[]{:S(2)}) collective-permute-start(s32[32]{0:T(128)S(1)} %select_n.416), channel_id=1, source_target_pairs={{0,2},{1,3},{2,4},{3,5},{4,6},{5,7},{6,0},{7,1},{8,10},{9,11},{10,... | collective-permute-start | bytes 392 | tf_op jit(solution)/shard_map/ppermute | solution.py:68
  10.8 3.9 %collective-permute-start.2 = (s32[32]{0:T(128)S(1)}, s32[32]{0:T(128)S(1)}, u32[]{:S(2)}, u32[]{:S(2)}) collective-permute-start(s32[32]{0:T(128)S(1)} %select_n.416), channel_id=1, source_target_pairs={{0,4},{1,5},{2,6},{3,7},{4,0},{5,1},{6,2},{7,3},{8,12},{9,13},{10,... | collective-permute-start | bytes 392 | tf_op jit(solution)/shard_map/ppermute | solution.py:68
  13.3 2.4 %collective-permute-start.3 = (s32[32]{0:T(128)S(1)}, s32[32]{0:T(128)S(1)}, u32[]{:S(2)}, u32[]{:S(2)}) collective-permute-start(s32[32]{0:T(128)S(1)} %select_n.416), channel_id=1, source_target_pairs={{0,6},{1,7},{2,0},{3,1},{4,2},{5,3},{6,4},{7,5},{8,14},{9,15},{10,... | collective-permute-start | bytes 392 | tf_op jit(solution)/shard_map/ppermute | solution.py:68
  16.4 2.4 %collective-permute-start.4 = (s32[128]{0:T(128)S(1)}, s32[128]{0:T(128)S(1)}, u32[]{:S(2)}, u32[]{:S(2)}) collective-permute-start(s32[128]{0:T(128)S(1)} %select_n.421), channel_id=1, source_target_pairs={{0,8},{1,9},{2,10},{3,11},{4,12},{5,13},{6,14},{7,15},{8,0},{9,1},... | collective-permute-start | bytes 1544 | tf_op jit(solution)/shard_map/ppermute | solution.py:68
  19.5 5.8 %collective-permute-start.5 = (s32[256]{0:T(256)S(1)}, s32[256]{0:T(256)S(1)}, u32[]{:S(2)}, u32[]{:S(2)}) collective-permute-start(s32[256]{0:T(256)S(1)} %fusion.26), channel_id=1, source_target_pairs={{0,16},{1,17},{2,18},{3,19},{4,20},{5,21},{6,22},{7,23},{8,24},{9,... | collective-permute-start | bytes 3080 | tf_op jit(solution)/shard_map/ppermute | solution.py:68
  21.1 4.3 %collective-permute-start.6 = (s32[256]{0:T(256)S(1)}, s32[256]{0:T(256)S(1)}, u32[]{:S(2)}, u32[]{:S(2)}) collective-permute-start(s32[256]{0:T(256)S(1)} %fusion.26), channel_id=1, source_target_pairs={{0,32},{1,33},{2,34},{3,35},{4,36},{5,37},{6,38},{7,39},{8,40},{9,... | collective-permute-start | bytes 3080 | tf_op jit(solution)/shard_map/ppermute | solution.py:68
  24.4 2.4 %collective-permute-start.7 = (s32[256]{0:T(256)S(1)}, s32[256]{0:T(256)S(1)}, u32[]{:S(2)}, u32[]{:S(2)}) collective-permute-start(s32[256]{0:T(256)S(1)} %fusion.26), channel_id=1, source_target_pairs={{0,48},{1,49},{2,50},{3,51},{4,52},{5,53},{6,54},{7,55},{8,56},{9,... | collective-permute-start | bytes 3080 | tf_op jit(solution)/shard_map/ppermute | solution.py:68
  27.5 9.5 %collective-permute-start.8 = (s32[1024]{0:T(1024)S(1)}, s32[1024]{0:T(1024)S(1)}, u32[]{:S(2)}, u32[]{:S(2)}) collective-permute-start(s32[1024]{0:T(1024)S(1)} %bitcast.131), channel_id=1, source_target_pairs={{0,64},{1,65},{2,66},{3,67},{4,68},{5,69},{6,70},{7,71},{8,72},{9,... | collective-permute-start | bytes 12296 | tf_op jit(solution)/shard_map/ppermute | solution.py:68
  30.2 15.7 %copy-start = (f32[8192]{0:T(1024)S(1)}, f32[8192]{0:T(1024)}, u32[]{:S(2)}) copy-start(f32[8192]{0:T(1024)} %param.21) | copy-start | bytes 98308
  46.0 9.3 %collective-permute-start.19 = (f32[7,16384]{1,0:T(8,128)S(1)}, f32[7,16384]{1,0:T(8,128)S(1)}, u32[]{:S(2)}, u32[]{:S(2)}) collective-permute-start(f32[7,16384]{1,0:T(8,128)S(1)} %pad_maximum_fusion), channel_id=1, source_target_pairs={{0,2},{1,3},{2,4},{3,5},{4,6},{5,7},{6,0},{7,1},{8,10},{9,11},{10,... | collective-permute-start | bytes 1376264 | tf_op jit(solution)/shard_map/ppermute | solution.py:184
  46.6 20.7 %collective-permute-start.20 = (f32[7,16384]{1,0:T(8,128)S(1)}, f32[7,16384]{1,0:T(8,128)S(1)}, u32[]{:S(2)}, u32[]{:S(2)}) collective-permute-start(f32[7,16384]{1,0:T(8,128)S(1)} %pad_maximum_fusion), channel_id=1, source_target_pairs={{0,4},{1,5},{2,6},{3,7},{4,0},{5,1},{6,2},{7,3},{8,12},{9,13},{10,... | collective-permute-start | bytes 1376264 | tf_op jit(solution)/shard_map/ppermute | solution.py:184
  49.6 21.8 %collective-permute-start.21 = (f32[7,16384]{1,0:T(8,128)S(1)}, f32[7,16384]{1,0:T(8,128)S(1)}, u32[]{:S(2)}, u32[]{:S(2)}) collective-permute-start(f32[7,16384]{1,0:T(8,128)S(1)} %pad_maximum_fusion), channel_id=1, source_target_pairs={{0,6},{1,7},{2,0},{3,1},{4,2},{5,3},{6,4},{7,5},{8,14},{9,15},{10,... | collective-permute-start | bytes 1376264 | tf_op jit(solution)/shard_map/ppermute | solution.py:184
  72.4 32.3 %copy-start.1 = (pred[8]{0:T(512)(128)(4,1)S(1)}, pred[8]{0:T(512)(128)(4,1)}, u32[]{:S(2)}) copy-start(pred[8]{0:T(512)(128)(4,1)} %constant.352.clone.1) | copy-start | bytes 28
  72.4 32.9 %collective-permute-start.22 = (f32[7,65536]{1,0:T(8,128)}, f32[7,65536]{1,0:T(8,128)}, u32[]{:S(2)}, u32[]{:S(2)}) collective-permute-start(f32[7,65536]{1,0:T(8,128)} %get-tuple-element.88), channel_id=1, source_target_pairs={{0,1},{1,0},{2,3},{3,2},{4,5},{5,4},{6,7},{7,6},{8,9},{9,8},{10,11... | collective-permute-start | bytes 5505032 | tf_op jit(solution)/shard_map/ppermute | solution.py:184
  77.2 3.7 %collective-permute-start.9 = (f32[13,1024]{1,0:T(8,128)S(1)}, f32[13,1024]{1,0:T(8,128)S(1)}, u32[]{:S(2)}, u32[]{:S(2)}) collective-permute-start(f32[13,1024]{1,0:T(8,128)S(1)} %bitcast.119), channel_id=1, source_target_pairs={{0,8},{1,9},{2,10},{3,11},{4,12},{5,13},{6,14},{7,15},{8,0},{9,1},... | collective-permute-start | bytes 159752 | tf_op jit(solution)/shard_map/ppermute | solution.py:86
  81.2 6.1 %collective-permute-start.10 = (f32[13,256]{0,1:T(8,128)S(1)}, f32[13,256]{0,1:T(8,128)S(1)}, u32[]{:S(2)}, u32[]{:S(2)}) collective-permute-start(f32[13,256]{0,1:T(8,128)S(1)} %get-tuple-element.94), channel_id=1, source_target_pairs={{0,2},{1,3},{2,4},{3,5},{4,6},{5,7},{6,0},{7,1},{8,10},{9,11},{10,... | collective-permute-start | bytes 39944 | tf_op jit(solution)/shard_map/ppermute | solution.py:86
  81.3 7.8 %collective-permute-start.11 = (f32[13,256]{0,1:T(8,128)S(1)}, f32[13,256]{0,1:T(8,128)S(1)}, u32[]{:S(2)}, u32[]{:S(2)}) collective-permute-start(f32[13,256]{0,1:T(8,128)S(1)} %get-tuple-element.96), channel_id=1, source_target_pairs={{0,4},{1,5},{2,6},{3,7},{4,0},{5,1},{6,2},{7,3},{8,12},{9,13},{10,... | collective-permute-start | bytes 39944 | tf_op jit(solution)/shard_map/ppermute | solution.py:86
  83.6 6.3 %collective-permute-start.12 = (f32[13,256]{0,1:T(8,128)S(1)}, f32[13,256]{0,1:T(8,128)S(1)}, u32[]{:S(2)}, u32[]{:S(2)}) collective-permute-start(f32[13,256]{0,1:T(8,128)S(1)} %get-tuple-element.95), channel_id=1, source_target_pairs={{0,6},{1,7},{2,0},{3,1},{4,2},{5,3},{6,4},{7,5},{8,14},{9,15},{10,... | collective-permute-start | bytes 39944 | tf_op jit(solution)/shard_map/ppermute | solution.py:86
  90.0 2.9 %collective-permute-start.13 = (f32[13,128]{0,1:T(8,128)S(1)}, f32[13,128]{0,1:T(8,128)S(1)}, u32[]{:S(2)}, u32[]{:S(2)}) collective-permute-start(f32[13,128]{0,1:T(8,128)S(1)} %select_bitcast_fusion.4), channel_id=1, source_target_pairs={{0,1},{1,0},{2,3},{3,2},{4,5},{5,4},{6,7},{7,6},{8,9},{9,8},{10,11... | collective-permute-start | bytes 19976 | tf_op jit(solution)/shard_map/ppermute | solution.py:86
  92.9 4.4 %collective-permute-start.14 = (f32[13,128]{0,1:T(8,128)S(1)}, f32[13,128]{0,1:T(8,128)S(1)}, u32[]{:S(2)}, u32[]{:S(2)}) collective-permute-start(f32[13,128]{0,1:T(8,128)S(1)} %bitcast_add_fusion.1), channel_id=1, source_target_pairs={{0,16},{1,17},{2,18},{3,19},{4,20},{5,21},{6,22},{7,23},{8,24},{9,... | collective-permute-start | bytes 19976 | tf_op jit(solution)/shard_map/ppermute | solution.py:94
  93.0 6.0 %collective-permute-start.15 = (f32[13,128]{0,1:T(8,128)S(1)}, f32[13,128]{0,1:T(8,128)S(1)}, u32[]{:S(2)}, u32[]{:S(2)}) collective-permute-start(f32[13,128]{0,1:T(8,128)S(1)} %bitcast_add_fusion.1), channel_id=1, source_target_pairs={{0,32},{1,33},{2,34},{3,35},{4,36},{5,37},{6,38},{7,39},{8,40},{9,... | collective-permute-start | bytes 19976 | tf_op jit(solution)/shard_map/ppermute | solution.py:94
  96.1 3.9 %collective-permute-start.16 = (f32[13,128]{0,1:T(8,128)S(1)}, f32[13,128]{0,1:T(8,128)S(1)}, u32[]{:S(2)}, u32[]{:S(2)}) collective-permute-start(f32[13,128]{0,1:T(8,128)S(1)} %bitcast_add_fusion.1), channel_id=1, source_target_pairs={{0,48},{1,49},{2,50},{3,51},{4,52},{5,53},{6,54},{7,55},{8,56},{9,... | collective-permute-start | bytes 19976 | tf_op jit(solution)/shard_map/ppermute | solution.py:94
  100.0 4.7 %collective-permute-start.17 = (f32[13,128]{0,1:T(8,128)S(1)}, f32[13,128]{0,1:T(8,128)S(1)}, u32[]{:S(2)}, u32[]{:S(2)}) collective-permute-start(f32[13,128]{0,1:T(8,128)S(1)} %add_add_fusion), channel_id=1, source_target_pairs={{0,64},{1,65},{2,66},{3,67},{4,68},{5,69},{6,70},{7,71},{8,72},{9,... | collective-permute-start | bytes 19976 | tf_op jit(solution)/shard_map/ppermute | solution.py:94
  223.0 4.0 %collective-permute-start.23 = (f32[6,64]{1,0:T(8,128)S(1)}, f32[6,64]{1,0:T(8,128)S(1)}, u32[]{:S(2)}, u32[]{:S(2)}) collective-permute-start(f32[6,64]{1,0:T(8,128)S(1)} %select_bitcast_fusion.5), channel_id=1, source_target_pairs={{0,64},{1,65},{2,66},{3,67},{4,68},{5,69},{6,70},{7,71},{8,72},{9,... | collective-permute-start | bytes 4616 | tf_op jit(solution)/shard_map/ppermute | solution.py:86
  227.2 3.7 %collective-permute-start.24 = (f32[6,16]{0,1:T(8,128)S(1)}, f32[6,16]{0,1:T(8,128)S(1)}, u32[]{:S(2)}, u32[]{:S(2)}) collective-permute-start(f32[6,16]{0,1:T(8,128)S(1)} %bitcast.128), channel_id=1, source_target_pairs={{0,16},{1,17},{2,18},{3,19},{4,20},{5,21},{6,22},{7,23},{8,24},{9,... | collective-permute-start | bytes 1160 | tf_op jit(solution)/shard_map/ppermute | solution.py:86
  227.4 4.0 %collective-permute-start.25 = (f32[6,16]{0,1:T(8,128)S(1)}, f32[6,16]{0,1:T(8,128)S(1)}, u32[]{:S(2)}, u32[]{:S(2)}) collective-permute-start(f32[6,16]{0,1:T(8,128)S(1)} %bitcast.129), channel_id=1, source_target_pairs={{0,32},{1,33},{2,34},{3,35},{4,36},{5,37},{6,38},{7,39},{8,40},{9,... | collective-permute-start | bytes 1160 | tf_op jit(solution)/shard_map/ppermute | solution.py:86
  230.4 2.5 %collective-permute-start.26 = (f32[6,16]{0,1:T(8,128)S(1)}, f32[6,16]{0,1:T(8,128)S(1)}, u32[]{:S(2)}, u32[]{:S(2)}) collective-permute-start(f32[6,16]{0,1:T(8,128)S(1)} %bitcast.130), channel_id=1, source_target_pairs={{0,48},{1,49},{2,50},{3,51},{4,52},{5,53},{6,54},{7,55},{8,56},{9,... | collective-permute-start | bytes 1160 | tf_op jit(solution)/shard_map/ppermute | solution.py:86

commit v6 on v5

--- a/solution.py
+++ b/solution.py
@@ -203,6 +203,7 @@
     packed = jnp.concatenate(
         [positions, velocities, accelerations, jerk_rates, elapsed_time[None, :]], axis=0
     )
+    packed, field = lax.optimization_barrier((packed, field))
     first_row = lax.axis_index(ALL) * own_stars
     local_row = every_index - first_row
     is_owned = (local_row >= 0) & (local_row < own_stars)

time: 240 us -> 236 us (0.983)
  starting transfers between devices: 36 us -> 41.8 us
  waiting for transfers between devices: 47.4 us -> 42.1 us
  local copies, waits for them, and re-layouts: 31.1 us -> 27 us
    concatenate x2 -> x1, local copies, waits for them, and re-layouts: 6.78 us -> 0.65 us  [on_device(): jnp.concatenate([positions, velocities, accelerations, jerk_rates, elapse...]
    ppermute x9, waiting for transfers between devices: 16.1 us -> 11.9 us  [reduce_level(): total = total + lax.ppermute(piece, ALL, _perm(stride, size, s, ndev))]
    ppermute x9, starting transfers between devices: 8.29 us -> 12.3 us  [reduce_level(): total = total + lax.ppermute(piece, ALL, _perm(stride, size, s, ndev))]
    optimization_barrier x0 -> x1, local copies, waits for them, and re-layouts: none -> 2.72 us  [on_device(): packed, field = lax.optimization_barrier((packed, field))]
    unnamed x16 -> x26, local copies, waits for them, and re-layouts: 6.27 us -> 7.31 us
  transfers between devices with their start and end apart: 27 -> 27, of which waited for: 21 -> 21; matrix products, arithmetic and copies ran while one was open for 11% -> 5% of each run, Pallas kernels for 0% -> 0%
where the time goes in v6:
time: 236 us; the launch traced here: 232 us
  Pallas kernels  114 us (48%)
  waiting for transfers between devices  42.1 us (18%)
  starting transfers between devices  41.8 us (18%)
  local copies, waits for them, and re-layouts  27 us (11%)
  other arithmetic  6.42 us (3%)
    pallas_call x1, Pallas kernels, pair_forces(): pl.pallas_call(forces_kernel, out_shape=jax.ShapeDtypeStruct((num_k, 8),...  114 us
    ppermute x5, waiting for transfers between devices, concat_level(): lax.ppermute(x, ALL, _perm(stride, size, s, ndev))  19.3 us
    ppermute x9, starting transfers between devices, gather_level(): lax.ppermute(x, ALL, _perm(stride, size, s, ndev))  14.8 us
    ppermute x9, starting transfers between devices, reduce_level(): total = total + lax.ppermute(piece, ALL, _perm(stride, size, s, ndev))  12.3 us
    ppermute x9, waiting for transfers between devices, reduce_level(): total = total + lax.ppermute(piece, ALL, _perm(stride, size, s, ndev))  11.9 us
    ppermute x5, starting transfers between devices, concat_level(): lax.ppermute(x, ALL, _perm(stride, size, s, ndev))  8.32 us
    gather x2, local copies, waits for them, and re-layouts, on_device(): picked = jnp.take(packed, jnp.clip(local_row, 0, own_stars - 1), axis=1)  7.97 us
    unnamed x26, local copies, waits for them, and re-layouts  7.31 us
  transfers between devices with their start and end apart: 27, of which 21 were waited for; matrix products, arithmetic and copies ran while one was open for 5% of the time, Pallas kernels for 0%

profile of v6, /device:TPU:1, one launch (start us, length us, event | category | flops | bytes accessed | tf_op | source)
XLA Modules:
  0.0 232.1 jit_solution(6537330371294668010)
XLA Ops:
  0.6 1.5 collective-permute-start
  2.1 0.8 broadcast_multiply_fusion.1
  2.9 1.2 multiply_add_fusion.1
  4.1 0.9 constant_dynamic-update-slice_fusion.4
  5.1 1.5 collective-permute-start.9
  6.7 0.7 constant_dynamic-update-slice_fusion.10
  7.5 0.7 pad_add_fusion.3
  8.9 1.2 collective-permute-start.1
  10.1 2.5 %collective-permute-start.2 = (s32[32]{0:T(128)S(1)}, s32[32]{0:T(128)S(1)}, u32[]{:S(2)}, u32[]{:S(2)}) collective-permute-start(s32[32]{0:T(128)S(1)} %select_n.416), channel_id=1, source_target_pairs={{0,4},{1,5},{2,6},{3,7},{4,0},{5,1},{6,2},{7,3},{8,12},{9,13},{10,... | collective-permute-start | bytes 392 | tf_op jit(solution)/shard_map/ppermute | solution.py:68
  12.5 1.2 collective-permute-start.3
  14.0 0.9 collective-permute-done.3
  16.0 2.2 collective-permute-done.4
  18.8 1.6 collective-permute-start.5
  20.4 3.3 %collective-permute-start.6 = (s32[256]{0:T(256)S(1)}, s32[256]{0:T(256)S(1)}, u32[]{:S(2)}, u32[]{:S(2)}) collective-permute-start(s32[256]{0:T(256)S(1)} %fusion.26), channel_id=1, source_target_pairs={{0,32},{1,33},{2,34},{3,35},{4,36},{5,37},{6,38},{7,39},{8,40},{9,... | collective-permute-start | bytes 3080 | tf_op jit(solution)/shard_map/ppermute | solution.py:68
  23.7 0.7 collective-permute-start.7
  24.7 1.5 collective-permute-done.7
  26.7 0.9 pad_maximum_fusion
  28.2 3.0 %collective-permute-start.11 = (f32[7,16384]{1,0:T(8,128)S(1)}, f32[7,16384]{1,0:T(8,128)S(1)}, u32[]{:S(2)}, u32[]{:S(2)}) collective-permute-start(f32[7,16384]{1,0:T(8,128)S(1)} %pad_maximum_fusion), channel_id=1, source_target_pairs={{0,4},{1,5},{2,6},{3,7},{4,0},{5,1},{6,2},{7,3},{8,12},{9,13},{10,... | collective-permute-start | bytes 1376264 | tf_op jit(solution)/shard_map/ppermute | solution.py:184
  31.5 0.8 constant_dynamic-update-slice_fusion.3
  32.3 5.2 %collective-permute-done.10 = f32[7,16384]{1,0:T(8,128)S(1)} collective-permute-done((f32[7,16384]{1,0:T(8,128)S(1)}, f32[7,16384]{1,0:T(8,128)S(1)}, u32[]{:S(2)}, u32[]{:S(2)}) %collective-permute-start.10) | collective-permute-done | bytes 458784 | tf_op jit(solution)/shard_map/ppermute | solution.py:184
  37.5 0.9 constant_dynamic-update-slice_fusion.2
  38.4 11.2 %collective-permute-done.11 = f32[7,16384]{1,0:T(8,128)S(1)} collective-permute-done((f32[7,16384]{1,0:T(8,128)S(1)}, f32[7,16384]{1,0:T(8,128)S(1)}, u32[]{:S(2)}, u32[]{:S(2)}) %collective-permute-start.11) | collective-permute-done | bytes 458784 | tf_op jit(solution)/shard_map/ppermute | solution.py:184
  49.6 0.9 constant_dynamic-update-slice_fusion.1
  50.5 2.8 %collective-permute-done.12 = f32[7,16384]{1,0:T(8,128)S(1)} collective-permute-done((f32[7,16384]{1,0:T(8,128)S(1)}, f32[7,16384]{1,0:T(8,128)S(1)}, u32[]{:S(2)}, u32[]{:S(2)}) %collective-permute-start.12) | collective-permute-done | bytes 458784 | tf_op jit(solution)/shard_map/ppermute | solution.py:184
  53.3 0.9 constant_dynamic-update-slice_fusion
  54.2 1.4 copy-done.5
  55.6 2.9 %collective-permute-start.13 = (f32[7,65536]{1,0:T(8,128)}, f32[7,65536]{1,0:T(8,128)S(1)}, u32[]{:S(2)}, u32[]{:S(2)}) collective-permute-start(f32[7,65536]{1,0:T(8,128)} %copy-done.5), channel_id=1, source_target_pairs={{0,1},{1,0},{2,3},{3,2},{4,5},{5,4},{6,7},{7,6},{8,9},{9,8},{10,11... | collective-permute-start | bytes 5505032 | tf_op jit(solution)/shard_map/ppermute | solution.py:184
  58.5 2.6 %collective-permute-start.8 = (s32[1024]{0:T(1024)S(1)}, s32[1024]{0:T(1024)S(1)}, u32[]{:S(2)}, u32[]{:S(2)}) collective-permute-start(s32[1024]{0:T(1024)S(1)} %bitcast.131), channel_id=1, source_target_pairs={{0,64},{1,65},{2,66},{3,67},{4,68},{5,69},{6,70},{7,71},{8,72},{9,... | collective-permute-start | bytes 12296 | tf_op jit(solution)/shard_map/ppermute | solution.py:68
  63.3 1.5 constant_dynamic-update-slice_fusion.5.fld_ref
  64.8 2.7 %copy.64 = f32[13,8192]{0,1:T(8,128)} copy(f32[13,8192]{1,0:T(8,128)S(1)} %concatenate.23) | data formatting | bytes 851968 | tf_op jit(solution)/shard_map/optimization_barrier | solution.py:206
  67.5 7.6 %gather_fusion.5 = f32[2048,13]{1,0:T(8,128)S(1)} fusion(f32[13,8192]{0,1:T(8,128)} %copy.64, s32[2048]{0:T(1024)S(1)} %broadcast_clamp_fusion), kind=kCustom, calls=%fused_computation.5 | custom fusion | bytes 221184 | tf_op jit(solution)/shard_map/jit(_take)/gather | solution.py:210
  77.2 2.9 %collective-permute-done.14 = f32[13,1024]{1,0:T(8,128)S(1)} collective-permute-done((f32[13,1024]{1,0:T(8,128)S(1)}, f32[13,1024]{1,0:T(8,128)S(1)}, u32[]{:S(2)}, u32[]{:S(2)}) %collective-permute-start.14) | collective-permute-done | bytes 53280 | tf_op jit(solution)/shard_map/ppermute | solution.py:86
  80.6 2.4 %collective-permute-start.16 = (f32[13,256]{0,1:T(8,128)S(1)}, f32[13,256]{0,1:T(8,128)S(1)}, u32[]{:S(2)}, u32[]{:S(2)}) collective-permute-start(f32[13,256]{0,1:T(8,128)S(1)} %get-tuple-element.94), channel_id=1, source_target_pairs={{0,4},{1,5},{2,6},{3,7},{4,0},{5,1},{6,2},{7,3},{8,12},{9,13},{10,... | collective-permute-start | bytes 39944 | tf_op jit(solution)/shard_map/ppermute | solution.py:86
  83.3 4.0 %collective-permute-done.15 = f32[13,256]{0,1:T(8,128)S(1)} collective-permute-done((f32[13,256]{0,1:T(8,128)S(1)}, f32[13,256]{0,1:T(8,128)S(1)}, u32[]{:S(2)}, u32[]{:S(2)}) %collective-permute-start.15) | collective-permute-done | bytes 13344 | tf_op jit(solution)/shard_map/ppermute | solution.py:86
  88.0 3.5 %collective-permute-start.18 = (f32[13,128]{0,1:T(8,128)S(1)}, f32[13,128]{0,1:T(8,128)S(1)}, u32[]{:S(2)}, u32[]{:S(2)}) collective-permute-start(f32[13,128]{0,1:T(8,128)S(1)} %select_bitcast_fusion.4), channel_id=1, source_target_pairs={{0,1},{1,0},{2,3},{3,2},{4,5},{5,4},{6,7},{7,6},{8,9},{9,8},{10,11... | collective-permute-start | bytes 19976 | tf_op jit(solution)/shard_map/ppermute | solution.py:86
  91.4 0.9 collective-permute-done.18
  92.4 3.2 %collective-permute-start.20 = (f32[13,128]{0,1:T(8,128)S(1)}, f32[13,128]{0,1:T(8,128)S(1)}, u32[]{:S(2)}, u32[]{:S(2)}) collective-permute-start(f32[13,128]{0,1:T(8,128)S(1)} %bitcast_add_fusion.1), channel_id=1, source_target_pairs={{0,32},{1,33},{2,34},{3,35},{4,36},{5,37},{6,38},{7,39},{8,40},{9,... | collective-permute-start | bytes 19976 | tf_op jit(solution)/shard_map/ppermute | solution.py:94
  96.1 0.7 collective-permute-done.19
  96.8 1.8 collective-permute-done.20
  98.5 0.9 collective-permute-done.21
  99.4 2.7 %collective-permute-start.22 = (f32[13,128]{0,1:T(8,128)S(1)}, f32[13,128]{0,1:T(8,128)S(1)}, u32[]{:S(2)}, u32[]{:S(2)}) collective-permute-start(f32[13,128]{0,1:T(8,128)S(1)} %add_add_fusion), channel_id=1, source_target_pairs={{0,64},{1,65},{2,66},{3,67},{4,68},{5,69},{6,70},{7,71},{8,72},{9,... | collective-permute-start | bytes 19976 | tf_op jit(solution)/shard_map/ppermute | solution.py:94
  102.1 2.0 collective-permute-done.22
  104.8 113.7 %shard_map.102 = f32[128,8]{1,0:T(8,128)} custom-call(f32[128,8]{1,0:T(8,128)} %fusion.2.act_ref, f32[7,131072]{1,0:T(8,128)} %constant_dynamic-update-slice_fusion.5.fld_ref), custom_call_target="tpu_custom_call" | custom-call | tf_op jit(solution)/shard_map/pallas_call | solution.py:172
  218.5 0.9 copy.69
  219.4 2.7 %collective-permute-start.23 = (f32[6,64]{1,0:T(8,128)S(1)}, f32[6,64]{1,0:T(8,128)S(1)}, u32[]{:S(2)}, u32[]{:S(2)}) collective-permute-start(f32[6,64]{1,0:T(8,128)S(1)} %select_bitcast_fusion.5), channel_id=1, source_target_pairs={{0,64},{1,65},{2,66},{3,67},{4,68},{5,69},{6,70},{7,71},{8,72},{9,... | collective-permute-start | bytes 4616 | tf_op jit(solution)/shard_map/ppermute | solution.py:86
  222.1 1.3 collective-permute-done.23
  223.9 2.9 %collective-permute-start.25 = (f32[6,16]{0,1:T(8,128)S(1)}, f32[6,16]{0,1:T(8,128)S(1)}, u32[]{:S(2)}, u32[]{:S(2)}) collective-permute-start(f32[6,16]{0,1:T(8,128)S(1)} %bitcast.129), channel_id=1, source_target_pairs={{0,32},{1,33},{2,34},{3,35},{4,36},{5,37},{6,38},{7,39},{8,40},{9,... | collective-permute-start | bytes 1160 | tf_op jit(solution)/shard_map/ppermute | solution.py:86
  227.9 1.5 collective-permute-done.26
  (113 shorter events, 15.5 us)
Async XLA Ops:
  0.6 6.9 %collective-permute-start = (s32[16]{0:T(128)}, s32[16]{0:T(128)S(1)}, u32[]{:S(2)}, u32[]{:S(2)}) collective-permute-start(s32[16]{0:T(128)} %param.23), channel_id=1, source_target_pairs={{0,1},{1,0},{2,3},{3,2},{4,5},{5,4},{6,7},{7,6},{8,9},{9,8},{10,11... | collective-permute-start | bytes 200 | tf_op jit(solution)/shard_map/ppermute | solution.py:68
  4.1 57.1 %copy-start = (f32[3,8192]{1,0:T(4,128)S(1)}, f32[3,8192]{1,0:T(4,128)}, u32[]{:S(2)}) copy-start(f32[3,8192]{1,0:T(4,128)} %param.17) | copy-start | bytes 294916
  4.1 57.1 %copy-start.1 = (f32[3,8192]{1,0:T(4,128)S(1)}, f32[3,8192]{1,0:T(4,128)}, u32[]{:S(2)}) copy-start(f32[3,8192]{1,0:T(4,128)} %param.18) | copy-start | bytes 294916
  4.1 57.1 %copy-start.2 = (f32[3,8192]{1,0:T(4,128)S(1)}, f32[3,8192]{1,0:T(4,128)}, u32[]{:S(2)}) copy-start(f32[3,8192]{1,0:T(4,128)} %param.19) | copy-start | bytes 294916
  4.1 57.1 %copy-start.3 = (f32[3,8192]{1,0:T(4,128)S(1)}, f32[3,8192]{1,0:T(4,128)}, u32[]{:S(2)}) copy-start(f32[3,8192]{1,0:T(4,128)} %param.20) | copy-start | bytes 294916
  4.1 57.1 %copy-start.4 = (f32[8192]{0:T(1024)S(1)}, f32[8192]{0:T(1024)}, u32[]{:S(2)}) copy-start(f32[8192]{0:T(1024)} %param.22) | copy-start | bytes 98308
  5.1 21.6 %collective-permute-start.9 = (f32[7,8192]{1,0:T(8,128)S(1)}, f32[7,8192]{1,0:T(8,128)S(1)}, u32[]{:S(2)}, u32[]{:S(2)}) collective-permute-start(f32[7,8192]{1,0:T(8,128)S(1)} %get-tuple-element.91), channel_id=1, source_target_pairs={{0,8},{1,9},{2,10},{3,11},{4,12},{5,13},{6,14},{7,15},{8,0},{9,1},... | collective-permute-start | bytes 688136 | tf_op jit(solution)/shard_map/ppermute | solution.py:184
  8.9 4.9 %collective-permute-start.1 = (s32[32]{0:T(128)S(1)}, s32[32]{0:T(128)S(1)}, u32[]{:S(2)}, u32[]{:S(2)}) collective-permute-start(s32[32]{0:T(128)S(1)} %select_n.416), channel_id=1, source_target_pairs={{0,2},{1,3},{2,4},{3,5},{4,6},{5,7},{6,0},{7,1},{8,10},{9,11},{10,... | collective-permute-start | bytes 392 | tf_op jit(solution)/shard_map/ppermute | solution.py:68
  10.1 3.9 %collective-permute-start.2 = (s32[32]{0:T(128)S(1)}, s32[32]{0:T(128)S(1)}, u32[]{:S(2)}, u32[]{:S(2)}) collective-permute-start(s32[32]{0:T(128)S(1)} %select_n.416), channel_id=1, source_target_pairs={{0,4},{1,5},{2,6},{3,7},{4,0},{5,1},{6,2},{7,3},{8,12},{9,13},{10,... | collective-permute-start | bytes 392 | tf_op jit(solution)/shard_map/ppermute | solution.py:68
  12.5 2.4 %collective-permute-start.3 = (s32[32]{0:T(128)S(1)}, s32[32]{0:T(128)S(1)}, u32[]{:S(2)}, u32[]{:S(2)}) collective-permute-start(s32[32]{0:T(128)S(1)} %select_n.416), channel_id=1, source_target_pairs={{0,6},{1,7},{2,0},{3,1},{4,2},{5,3},{6,4},{7,5},{8,14},{9,15},{10,... | collective-permute-start | bytes 392 | tf_op jit(solution)/shard_map/ppermute | solution.py:68
  15.7 2.4 %collective-permute-start.4 = (s32[128]{0:T(128)S(1)}, s32[128]{0:T(128)S(1)}, u32[]{:S(2)}, u32[]{:S(2)}) collective-permute-start(s32[128]{0:T(128)S(1)} %select_n.421), channel_id=1, source_target_pairs={{0,8},{1,9},{2,10},{3,11},{4,12},{5,13},{6,14},{7,15},{8,0},{9,1},... | collective-permute-start | bytes 1544 | tf_op jit(solution)/shard_map/ppermute | solution.py:68
  18.8 5.8 %collective-permute-start.5 = (s32[256]{0:T(256)S(1)}, s32[256]{0:T(256)S(1)}, u32[]{:S(2)}, u32[]{:S(2)}) collective-permute-start(s32[256]{0:T(256)S(1)} %fusion.26), channel_id=1, source_target_pairs={{0,16},{1,17},{2,18},{3,19},{4,20},{5,21},{6,22},{7,23},{8,24},{9,... | collective-permute-start | bytes 3080 | tf_op jit(solution)/shard_map/ppermute | solution.py:68
  20.4 4.3 %collective-permute-start.6 = (s32[256]{0:T(256)S(1)}, s32[256]{0:T(256)S(1)}, u32[]{:S(2)}, u32[]{:S(2)}) collective-permute-start(s32[256]{0:T(256)S(1)} %fusion.26), channel_id=1, source_target_pairs={{0,32},{1,33},{2,34},{3,35},{4,36},{5,37},{6,38},{7,39},{8,40},{9,... | collective-permute-start | bytes 3080 | tf_op jit(solution)/shard_map/ppermute | solution.py:68
  23.7 2.4 %collective-permute-start.7 = (s32[256]{0:T(256)S(1)}, s32[256]{0:T(256)S(1)}, u32[]{:S(2)}, u32[]{:S(2)}) collective-permute-start(s32[256]{0:T(256)S(1)} %fusion.26), channel_id=1, source_target_pairs={{0,48},{1,49},{2,50},{3,51},{4,52},{5,53},{6,54},{7,55},{8,56},{9,... | collective-permute-start | bytes 3080 | tf_op jit(solution)/shard_map/ppermute | solution.py:68
  27.6 9.9 %collective-permute-start.10 = (f32[7,16384]{1,0:T(8,128)S(1)}, f32[7,16384]{1,0:T(8,128)S(1)}, u32[]{:S(2)}, u32[]{:S(2)}) collective-permute-start(f32[7,16384]{1,0:T(8,128)S(1)} %pad_maximum_fusion), channel_id=1, source_target_pairs={{0,2},{1,3},{2,4},{3,5},{4,6},{5,7},{6,0},{7,1},{8,10},{9,11},{10,... | collective-permute-start | bytes 1376264 | tf_op jit(solution)/shard_map/ppermute | solution.py:184
  28.2 21.4 %collective-permute-start.11 = (f32[7,16384]{1,0:T(8,128)S(1)}, f32[7,16384]{1,0:T(8,128)S(1)}, u32[]{:S(2)}, u32[]{:S(2)}) collective-permute-start(f32[7,16384]{1,0:T(8,128)S(1)} %pad_maximum_fusion), channel_id=1, source_target_pairs={{0,4},{1,5},{2,6},{3,7},{4,0},{5,1},{6,2},{7,3},{8,12},{9,13},{10,... | collective-permute-start | bytes 1376264 | tf_op jit(solution)/shard_map/ppermute | solution.py:184
  31.2 22.1 %collective-permute-start.12 = (f32[7,16384]{1,0:T(8,128)S(1)}, f32[7,16384]{1,0:T(8,128)S(1)}, u32[]{:S(2)}, u32[]{:S(2)}) collective-permute-start(f32[7,16384]{1,0:T(8,128)S(1)} %pad_maximum_fusion), channel_id=1, source_target_pairs={{0,6},{1,7},{2,0},{3,1},{4,2},{5,3},{6,4},{7,5},{8,14},{9,15},{10,... | collective-permute-start | bytes 1376264 | tf_op jit(solution)/shard_map/ppermute | solution.py:184
  54.2 1.4 copy-start.5
  55.6 7.7 %collective-permute-start.13 = (f32[7,65536]{1,0:T(8,128)}, f32[7,65536]{1,0:T(8,128)S(1)}, u32[]{:S(2)}, u32[]{:S(2)}) collective-permute-start(f32[7,65536]{1,0:T(8,128)} %copy-done.5), channel_id=1, source_target_pairs={{0,1},{1,0},{2,3},{3,2},{4,5},{5,4},{6,7},{7,6},{8,9},{9,8},{10,11... | collective-permute-start | bytes 5505032 | tf_op jit(solution)/shard_map/ppermute | solution.py:184
  58.5 4.0 %collective-permute-start.8 = (s32[1024]{0:T(1024)S(1)}, s32[1024]{0:T(1024)S(1)}, u32[]{:S(2)}, u32[]{:S(2)}) collective-permute-start(s32[1024]{0:T(1024)S(1)} %bitcast.131), channel_id=1, source_target_pairs={{0,64},{1,65},{2,66},{3,67},{4,68},{5,69},{6,70},{7,71},{8,72},{9,... | collective-permute-start | bytes 12296 | tf_op jit(solution)/shard_map/ppermute | solution.py:68
  75.5 28.7 %copy-start.6 = (pred[8]{0:T(512)(128)(4,1)S(1)}, pred[8]{0:T(512)(128)(4,1)}, u32[]{:S(2)}) copy-start(pred[8]{0:T(512)(128)(4,1)} %constant.352.clone.1) | copy-start | bytes 28
  77.0 3.2 %collective-permute-start.14 = (f32[13,1024]{1,0:T(8,128)S(1)}, f32[13,1024]{1,0:T(8,128)S(1)}, u32[]{:S(2)}, u32[]{:S(2)}) collective-permute-start(f32[13,1024]{1,0:T(8,128)S(1)} %bitcast.119), channel_id=1, source_target_pairs={{0,8},{1,9},{2,10},{3,11},{4,12},{5,13},{6,14},{7,15},{8,0},{9,1},... | collective-permute-start | bytes 159752 | tf_op jit(solution)/shard_map/ppermute | solution.py:86
  80.5 6.8 %collective-permute-start.15 = (f32[13,256]{0,1:T(8,128)S(1)}, f32[13,256]{0,1:T(8,128)S(1)}, u32[]{:S(2)}, u32[]{:S(2)}) collective-permute-start(f32[13,256]{0,1:T(8,128)S(1)} %get-tuple-element.92), channel_id=1, source_target_pairs={{0,2},{1,3},{2,4},{3,5},{4,6},{5,7},{6,0},{7,1},{8,10},{9,11},{10,... | collective-permute-start | bytes 39944 | tf_op jit(solution)/shard_map/ppermute | solution.py:86
  80.6 6.7 %collective-permute-start.16 = (f32[13,256]{0,1:T(8,128)S(1)}, f32[13,256]{0,1:T(8,128)S(1)}, u32[]{:S(2)}, u32[]{:S(2)}) collective-permute-start(f32[13,256]{0,1:T(8,128)S(1)} %get-tuple-element.94), channel_id=1, source_target_pairs={{0,4},{1,5},{2,6},{3,7},{4,0},{5,1},{6,2},{7,3},{8,12},{9,13},{10,... | collective-permute-start | bytes 39944 | tf_op jit(solution)/shard_map/ppermute | solution.py:86
  83.0 5.0 %collective-permute-start.17 = (f32[13,256]{0,1:T(8,128)S(1)}, f32[13,256]{0,1:T(8,128)S(1)}, u32[]{:S(2)}, u32[]{:S(2)}) collective-permute-start(f32[13,256]{0,1:T(8,128)S(1)} %get-tuple-element.93), channel_id=1, source_target_pairs={{0,6},{1,7},{2,0},{3,1},{4,2},{5,3},{6,4},{7,5},{8,14},{9,15},{10,... | collective-permute-start | bytes 39944 | tf_op jit(solution)/shard_map/ppermute | solution.py:86
  88.0 4.4 %collective-permute-start.18 = (f32[13,128]{0,1:T(8,128)S(1)}, f32[13,128]{0,1:T(8,128)S(1)}, u32[]{:S(2)}, u32[]{:S(2)}) collective-permute-start(f32[13,128]{0,1:T(8,128)S(1)} %select_bitcast_fusion.4), channel_id=1, source_target_pairs={{0,1},{1,0},{2,3},{3,2},{4,5},{5,4},{6,7},{7,6},{8,9},{9,8},{10,11... | collective-permute-start | bytes 19976 | tf_op jit(solution)/shard_map/ppermute | solution.py:86
  92.4 4.4 %collective-permute-start.19 = (f32[13,128]{0,1:T(8,128)S(1)}, f32[13,128]{0,1:T(8,128)S(1)}, u32[]{:S(2)}, u32[]{:S(2)}) collective-permute-start(f32[13,128]{0,1:T(8,128)S(1)} %bitcast_add_fusion.1), channel_id=1, source_target_pairs={{0,16},{1,17},{2,18},{3,19},{4,20},{5,21},{6,22},{7,23},{8,24},{9,... | collective-permute-start | bytes 19976 | tf_op jit(solution)/shard_map/ppermute | solution.py:94
  92.4 6.1 %collective-permute-start.20 = (f32[13,128]{0,1:T(8,128)S(1)}, f32[13,128]{0,1:T(8,128)S(1)}, u32[]{:S(2)}, u32[]{:S(2)}) collective-permute-start(f32[13,128]{0,1:T(8,128)S(1)} %bitcast_add_fusion.1), channel_id=1, source_target_pairs={{0,32},{1,33},{2,34},{3,35},{4,36},{5,37},{6,38},{7,39},{8,40},{9,... | collective-permute-start | bytes 19976 | tf_op jit(solution)/shard_map/ppermute | solution.py:94
  95.6 3.8 %collective-permute-start.21 = (f32[13,128]{0,1:T(8,128)S(1)}, f32[13,128]{0,1:T(8,128)S(1)}, u32[]{:S(2)}, u32[]{:S(2)}) collective-permute-start(f32[13,128]{0,1:T(8,128)S(1)} %bitcast_add_fusion.1), channel_id=1, source_target_pairs={{0,48},{1,49},{2,50},{3,51},{4,52},{5,53},{6,54},{7,55},{8,56},{9,... | collective-permute-start | bytes 19976 | tf_op jit(solution)/shard_map/ppermute | solution.py:94
  99.4 4.7 %collective-permute-start.22 = (f32[13,128]{0,1:T(8,128)S(1)}, f32[13,128]{0,1:T(8,128)S(1)}, u32[]{:S(2)}, u32[]{:S(2)}) collective-permute-start(f32[13,128]{0,1:T(8,128)S(1)} %add_add_fusion), channel_id=1, source_target_pairs={{0,64},{1,65},{2,66},{3,67},{4,68},{5,69},{6,70},{7,71},{8,72},{9,... | collective-permute-start | bytes 19976 | tf_op jit(solution)/shard_map/ppermute | solution.py:94
  219.4 4.0 %collective-permute-start.23 = (f32[6,64]{1,0:T(8,128)S(1)}, f32[6,64]{1,0:T(8,128)S(1)}, u32[]{:S(2)}, u32[]{:S(2)}) collective-permute-start(f32[6,64]{1,0:T(8,128)S(1)} %select_bitcast_fusion.5), channel_id=1, source_target_pairs={{0,64},{1,65},{2,66},{3,67},{4,68},{5,69},{6,70},{7,71},{8,72},{9,... | collective-permute-start | bytes 4616 | tf_op jit(solution)/shard_map/ppermute | solution.py:86
  223.6 3.7 %collective-permute-start.24 = (f32[6,16]{0,1:T(8,128)S(1)}, f32[6,16]{0,1:T(8,128)S(1)}, u32[]{:S(2)}, u32[]{:S(2)}) collective-permute-start(f32[6,16]{0,1:T(8,128)S(1)} %bitcast.128), channel_id=1, source_target_pairs={{0,16},{1,17},{2,18},{3,19},{4,20},{5,21},{6,22},{7,23},{8,24},{9,... | collective-permute-start | bytes 1160 | tf_op jit(solution)/shard_map/ppermute | solution.py:86
  223.9 4.0 %collective-permute-start.25 = (f32[6,16]{0,1:T(8,128)S(1)}, f32[6,16]{0,1:T(8,128)S(1)}, u32[]{:S(2)}, u32[]{:S(2)}) collective-permute-start(f32[6,16]{0,1:T(8,128)S(1)} %bitcast.129), channel_id=1, source_target_pairs={{0,32},{1,33},{2,34},{3,35},{4,36},{5,37},{6,38},{7,39},{8,40},{9,... | collective-permute-start | bytes 1160 | tf_op jit(solution)/shard_map/ppermute | solution.py:86
  226.8 2.5 %collective-permute-start.26 = (f32[6,16]{0,1:T(8,128)S(1)}, f32[6,16]{0,1:T(8,128)S(1)}, u32[]{:S(2)}, u32[]{:S(2)}) collective-permute-start(f32[6,16]{0,1:T(8,128)S(1)} %bitcast.130), channel_id=1, source_target_pairs={{0,48},{1,49},{2,50},{3,51},{4,52},{5,53},{6,54},{7,55},{8,56},{9,... | collective-permute-start | bytes 1160 | tf_op jit(solution)/shard_map/ppermute | solution.py:86

commit v7 on v6

--- a/solution.py
+++ b/solution.py
@@ -11,9 +11,9 @@
 
 softening = 0.001
 ALL = ("blk", "group")
-GROUP_LEVELS = (("core", 1, 2), ("x", 2, 4), ("y_lo", 8, 2))
-BLK_LEVELS = (("z", 16, 4), ("y_hi", 64, 2))
-LEVELS = GROUP_LEVELS + BLK_LEVELS
+LEVELS = (("core", 1, 2), ("x", 2, 4), ("y_lo", 8, 2), ("z", 16, 4), ("y_hi", 64, 2))
+FIELD_LEVELS = (("y_lo", 8, 2), ("core", 1, 2))
+ACTIVE_LEVELS = (("y_hi", 64, 2), ("z", 16, 4), ("x", 2, 4))
 SUB = 2
 
 
@@ -186,16 +186,14 @@
 
 
 def on_device(positions, velocities, accelerations, jerk_rates, masses, elapsed_time, active_index):
-    num_blk = lax.axis_size("blk")
-    num_group = lax.axis_size("group")
-    ndev = num_blk * num_group
+    ndev = lax.axis_size("blk") * lax.axis_size("group")
     own_stars = positions.shape[1]
     own_active = active_index.shape[0]
     total_stars = own_stars * ndev
     gravity = 1.0 / total_stars
     pred_pos, pred_vel = predict(positions, velocities, accelerations, jerk_rates, elapsed_time)
     field = jnp.concatenate([pred_pos, pred_vel, masses[None, :]], axis=0)
-    for level in (GROUP_LEVELS[2], GROUP_LEVELS[1], GROUP_LEVELS[0]):
+    for level in FIELD_LEVELS:
         field = concat_level(field, level, ndev)
     every_index = active_index
     for level in LEVELS:
@@ -212,19 +210,25 @@
     act_pos, act_vel = predict(picked[0:3], picked[3:6], picked[6:9], picked[9:12], picked[12])
     payload = jnp.concatenate([act_pos, act_vel, corrector_terms(picked)], axis=0)
     rows = payload.shape[0]
-    payload = payload.reshape(rows, num_blk, num_group, own_active)
-    payload = payload.transpose(0, 2, 1, 3).reshape(rows, ndev * own_active)
-    for level in reversed(GROUP_LEVELS):
+    sizes = {name: size for name, _, size in LEVELS}
+    order = ("y_hi", "z", "y_lo", "x", "core")
+    payload = payload.reshape((rows,) + tuple(sizes[n] for n in order) + (own_active,))
+    front = [order.index(n) + 1 for n, _, _ in FIELD_LEVELS]
+    back = [order.index(n) + 1 for n, _, _ in ACTIVE_LEVELS]
+    payload = payload.transpose([0] + front + back + [len(order) + 1]).reshape(rows, ndev * own_active)
+    for level in FIELD_LEVELS:
         payload = reduce_level(payload, level, ndev)
-    for level in BLK_LEVELS:
+    for level in ACTIVE_LEVELS:
         payload = sum_level(payload, level, ndev)
     num_k = payload.shape[1]
     active_t = jnp.concatenate([payload[0:6], jnp.zeros((2, num_k), jnp.float32)], axis=0).T
     partial = pair_forces(active_t, field)[:, 0:6].T
-    for level in reversed(BLK_LEVELS):
+    for level in ACTIVE_LEVELS:
         partial = reduce_level(partial, level, ndev)
-    mine = lax.axis_index("blk") * own_active
-    terms = lax.dynamic_slice_in_dim(payload[6:13], mine, own_active, axis=1)
+    mine = 0
+    for _, stride, size in ACTIVE_LEVELS:
+        mine = mine * size + _coord(stride, size)
+    terms = lax.dynamic_slice_in_dim(payload[6:13], mine * own_active, own_active, axis=1)
     return corrector(terms, partial * gravity)
 
 

time: 236 us -> 247 us (1.047)
  waiting for transfers between devices: 42.1 us -> 68 us
  starting transfers between devices: 41.8 us -> 31.2 us
  Pallas kernels: 114 us -> 110 us
  local copies, waits for them, and re-layouts: 27 us -> 24.5 us
    ppermute x4 -> x7, waiting for transfers between devices: 5.36 us -> 34.7 us  [sum_level(): total = total + lax.ppermute(x, ALL, _perm(stride, size, s, ndev))]
    ppermute x5 -> x2, waiting for transfers between devices: 19.3 us -> 1.48 us  [concat_level(): lax.ppermute(x, ALL, _perm(stride, size, s, ndev))]
    ppermute x9, waiting for transfers between devices: 11.9 us -> 22.9 us  [reduce_level(): total = total + lax.ppermute(piece, ALL, _perm(stride, size, s, ndev))]
    ppermute x9, starting transfers between devices: 12.3 us -> 6.56 us  [reduce_level(): total = total + lax.ppermute(piece, ALL, _perm(stride, size, s, ndev))]
    unnamed x26 -> x12, local copies, waits for them, and re-layouts: 7.31 us -> 2.65 us
    pallas_call x1, Pallas kernels: 114 us -> 110 us  [pair_forces(): pl.pallas_call(forces_kernel, out_shape=jax.ShapeDtypeStruct((num_k, 8),...]
    ppermute x9, waiting for transfers between devices: 5.54 us -> 8.97 us  [gather_level(): lax.ppermute(x, ALL, _perm(stride, size, s, ndev))]
    concatenate x1, local copies, waits for them, and re-layouts: 0.65 us -> 4.05 us  [on_device(): jnp.concatenate([positions, velocities, accelerations, jerk_rates, elapse...]
  transfers between devices with their start and end apart: 27 -> 27, of which waited for: 21 -> 21; matrix products, arithmetic and copies ran while one was open for 5% -> 4% of each run, Pallas kernels for 0% -> 0%
where the time goes in v7:
time: 247 us; the launch traced here: 242 us
  Pallas kernels  110 us (45%)
  waiting for transfers between devices  68 us (28%)
  starting transfers between devices  31.2 us (13%)
  local copies, waits for them, and re-layouts  24.5 us (10%)
  other arithmetic  7.68 us (3%)
    pallas_call x1, Pallas kernels, pair_forces(): pl.pallas_call(forces_kernel, out_shape=jax.ShapeDtypeStruct((num_k, 8),...  110 us
    ppermute x7, waiting for transfers between devices, sum_level(): total = total + lax.ppermute(x, ALL, _perm(stride, size, s, ndev))  34.7 us
    ppermute x9, waiting for transfers between devices, reduce_level(): total = total + lax.ppermute(piece, ALL, _perm(stride, size, s, ndev))  22.9 us
    ppermute x9, starting transfers between devices, gather_level(): lax.ppermute(x, ALL, _perm(stride, size, s, ndev))  11.8 us
    ppermute x9, waiting for transfers between devices, gather_level(): lax.ppermute(x, ALL, _perm(stride, size, s, ndev))  8.97 us
    gather x2, local copies, waits for them, and re-layouts, on_device(): picked = jnp.take(packed, jnp.clip(local_row, 0, own_stars - 1), axis=1)  7.97 us
    ppermute x2, starting transfers between devices, concat_level(): lax.ppermute(x, ALL, _perm(stride, size, s, ndev))  7.18 us
    ppermute x9, starting transfers between devices, reduce_level(): total = total + lax.ppermute(piece, ALL, _perm(stride, size, s, ndev))  6.56 us
  transfers between devices with their start and end apart: 27, of which 21 were waited for; matrix products, arithmetic and copies ran while one was open for 4% of the time, Pallas kernels for 0%

profile of v7, /device:TPU:1, one launch (start us, length us, event | category | flops | bytes accessed | tf_op | source)
XLA Modules:
  0.0 242.3 jit_solution(12795373523609944456)
XLA Ops:
  0.6 0.8 broadcast_multiply_fusion.1
  1.4 1.2 multiply_add_fusion.1
  2.6 0.8 pad_maximum_fusion.2
  3.5 2.2 collective-permute-start.9
  5.7 1.0 collective-permute-start
  9.0 2.5 %collective-permute-start.3 = (s32[32]{0:T(128)S(1)}, s32[32]{0:T(128)S(1)}, u32[]{:S(2)}, u32[]{:S(2)}) collective-permute-start(s32[32]{0:T(128)S(1)} %select_n.425), channel_id=1, source_target_pairs={{0,6},{1,7},{2,0},{3,1},{4,2},{5,3},{6,4},{7,5},{8,14},{9,15},{10,... | collective-permute-start | bytes 392 | tf_op jit(solution)/shard_map/ppermute | solution.py:68
  12.6 2.7 %collective-permute-done.2 = s32[32]{0:T(128)S(1)} collective-permute-done((s32[32]{0:T(128)S(1)}, s32[32]{0:T(128)S(1)}, u32[]{:S(2)}, u32[]{:S(2)}) %collective-permute-start.2) | collective-permute-done | bytes 160 | tf_op jit(solution)/shard_map/ppermute | solution.py:68
  16.6 2.2 collective-permute-done.4
  19.4 3.8 %collective-permute-start.7 = (s32[256]{0:T(256)S(1)}, s32[256]{0:T(256)S(1)}, u32[]{:S(2)}, u32[]{:S(2)}) collective-permute-start(s32[256]{0:T(256)S(1)} %fusion.28), channel_id=1, source_target_pairs={{0,48},{1,49},{2,50},{3,51},{4,52},{5,53},{6,54},{7,55},{8,56},{9,... | collective-permute-start | bytes 3080 | tf_op jit(solution)/shard_map/ppermute | solution.py:68
  23.9 3.2 %collective-permute-done.6 = s32[256]{0:T(256)S(1)} collective-permute-done((s32[256]{0:T(256)S(1)}, s32[256]{0:T(256)S(1)}, u32[]{:S(2)}, u32[]{:S(2)}) %collective-permute-start.6) | collective-permute-done | bytes 1056 | tf_op jit(solution)/shard_map/ppermute | solution.py:68
  27.7 2.6 %collective-permute-start.8 = (s32[1024]{0:T(1024)S(1)}, s32[1024]{0:T(1024)S(1)}, u32[]{:S(2)}, u32[]{:S(2)}) collective-permute-start(s32[1024]{0:T(1024)S(1)} %bitcast.128), channel_id=1, source_target_pairs={{0,64},{1,65},{2,66},{3,67},{4,68},{5,69},{6,70},{7,71},{8,72},{9,... | collective-permute-start | bytes 12296 | tf_op jit(solution)/shard_map/ppermute | solution.py:68
  30.4 4.0 %concatenate.19 = f32[13,8192]{1,0:T(8,128)S(1)} concatenate(f32[3,8192]{1,0:T(4,128)} %param.17, f32[3,8192]{1,0:T(4,128)} %param.18, f32[3,8192]{1,0:T(4,128)} %param.19, f32[3,8192]{1,0:T(4,128)} %param.20, f32[1,8192]{1,0:T(1,128)} %bitcast.112), dimensions={0} | concatenate | bytes 851968 | tf_op jit(solution)/shard_map/concatenate | solution.py:201
  35.2 0.9 pad_maximum_fusion.1
  36.1 5.0 %collective-permute-start.10 = (f32[7,16384]{1,0:T(8,128)S(1)}, f32[7,16384]{1,0:T(8,128)S(1)}, u32[]{:S(2)}, u32[]{:S(2)}) collective-permute-start(f32[7,16384]{1,0:T(8,128)S(1)} %pad_maximum_fusion.1), channel_id=1, source_target_pairs={{0,1},{1,0},{2,3},{3,2},{4,5},{5,4},{6,7},{7,6},{8,9},{9,8},{10,11... | collective-permute-start | bytes 1376264 | tf_op jit(solution)/shard_map/ppermute | solution.py:184
  41.1 1.5 collective-permute-done.10
  42.6 1.2 pad_maximum_fusion.fld_ref
  43.8 2.6 %copy.81 = f32[13,8192]{0,1:T(8,128)} copy(f32[13,8192]{1,0:T(8,128)S(1)} %concatenate.19) | data formatting | bytes 851968 | tf_op jit(solution)/shard_map/optimization_barrier | solution.py:204
  46.5 7.6 %gather_fusion.5 = f32[2048,13]{1,0:T(8,128)S(1)} fusion(f32[13,8192]{0,1:T(8,128)} %copy.81, s32[2048]{0:T(1024)S(1)} %broadcast_clamp_fusion), kind=kCustom, calls=%fused_computation.5 | custom fusion | bytes 221184 | tf_op jit(solution)/shard_map/jit(_take)/gather | solution.py:208
  54.8 1.1 reshape.478
  55.9 1.0 copy.83
  57.1 13.1 %collective-permute-done.11 = f32[13,1024]{0,1:T(8,128)S(1)} collective-permute-done((f32[13,1024]{0,1:T(8,128)S(1)}, f32[13,1024]{0,1:T(8,128)S(1)}, u32[]{:S(2)}, u32[]{:S(2)}) %collective-permute-start.11) | collective-permute-done | bytes 53280 | tf_op jit(solution)/shard_map/ppermute | solution.py:86
  70.3 1.3 collective-permute-start.12
  71.6 1.2 collective-permute-done.12
  72.8 0.8 collective-permute-start.13
  73.6 8.3 %collective-permute-done.13 = f32[13,512]{0,1:T(8,128)S(1)} collective-permute-done((f32[13,512]{0,1:T(8,128)S(1)}, f32[13,512]{0,1:T(8,128)S(1)}, u32[]{:S(2)}, u32[]{:S(2)}) %collective-permute-start.13) | collective-permute-done | bytes 26656 | tf_op jit(solution)/shard_map/ppermute | solution.py:94
  82.2 1.5 collective-permute-start.15
  83.8 0.8 collective-permute-start.14
  84.6 4.0 %collective-permute-done.16 = f32[13,512]{0,1:T(8,128)S(1)} collective-permute-done((f32[13,512]{0,1:T(8,128)S(1)}, f32[13,512]{0,1:T(8,128)S(1)}, u32[]{:S(2)}, u32[]{:S(2)}) %collective-permute-start.16) | collective-permute-done | bytes 26656 | tf_op jit(solution)/shard_map/ppermute | solution.py:94
  88.6 1.6 collective-permute-done.15
  90.2 7.4 %collective-permute-done.14 = f32[13,512]{0,1:T(8,128)S(1)} collective-permute-done((f32[13,512]{0,1:T(8,128)S(1)}, f32[13,512]{0,1:T(8,128)S(1)}, u32[]{:S(2)}, u32[]{:S(2)}) %collective-permute-start.14) | collective-permute-done | bytes 26656 | tf_op jit(solution)/shard_map/ppermute | solution.py:94
  97.8 1.3 collective-permute-start.18
  99.1 0.8 collective-permute-start.17
  99.8 5.3 %collective-permute-done.19 = f32[13,512]{0,1:T(8,128)S(1)} collective-permute-done((f32[13,512]{0,1:T(8,128)S(1)}, f32[13,512]{0,1:T(8,128)S(1)}, u32[]{:S(2)}, u32[]{:S(2)}) %collective-permute-start.19) | collective-permute-done | bytes 26656 | tf_op jit(solution)/shard_map/ppermute | solution.py:94
  105.1 1.4 collective-permute-done.18
  106.5 6.7 %collective-permute-done.17 = f32[13,512]{0,1:T(8,128)S(1)} collective-permute-done((f32[13,512]{0,1:T(8,128)S(1)}, f32[13,512]{0,1:T(8,128)S(1)}, u32[]{:S(2)}, u32[]{:S(2)}) %collective-permute-start.17) | collective-permute-done | bytes 26656 | tf_op jit(solution)/shard_map/ppermute | solution.py:94
  113.2 0.7 fusion.act_ref
  113.9 109.8 %shard_map.102 = f32[512,8]{1,0:T(8,128)} custom-call(f32[512,8]{1,0:T(8,128)} %fusion.act_ref, f32[7,32768]{1,0:T(8,128)} %pad_maximum_fusion.fld_ref), custom_call_target="tpu_custom_call" | custom-call | tf_op jit(solution)/shard_map/pallas_call | solution.py:172
  223.7 1.1 copy.84
  224.8 0.8 collective-permute-start.20
  225.6 3.3 %collective-permute-done.20 = f32[6,256]{1,0:T(8,128)S(1)} collective-permute-done((f32[6,256]{1,0:T(8,128)S(1)}, f32[6,256]{1,0:T(8,128)S(1)}, u32[]{:S(2)}, u32[]{:S(2)}) %collective-permute-start.20) | collective-permute-done | bytes 6176 | tf_op jit(solution)/shard_map/ppermute | solution.py:86
  229.1 1.5 collective-permute-start.22
  230.5 0.8 collective-permute-start.21
  231.5 1.6 collective-permute-done.22
  233.1 1.1 collective-permute-done.21
  234.5 1.2 collective-permute-start.25
  235.8 0.8 collective-permute-start.24
  236.9 1.6 collective-permute-done.25
  238.5 1.0 collective-permute-done.24
  (100 shorter events, 12.7 us)
Async XLA Ops:
  0.6 42.0 %copy-start = (f32[8192]{0:T(1024)S(1)}, f32[8192]{0:T(1024)}, u32[]{:S(2)}) copy-start(f32[8192]{0:T(1024)} %param.21) | copy-start | bytes 98308
  3.5 31.7 %collective-permute-start.9 = (f32[7,8192]{1,0:T(8,128)S(1)}, f32[7,8192]{1,0:T(8,128)S(1)}, u32[]{:S(2)}, u32[]{:S(2)}) collective-permute-start(f32[7,8192]{1,0:T(8,128)S(1)} %pad_maximum_fusion.2), channel_id=1, source_target_pairs={{0,8},{1,9},{2,10},{3,11},{4,12},{5,13},{6,14},{7,15},{8,0},{9,1},... | collective-permute-start | bytes 688136 | tf_op jit(solution)/shard_map/ppermute | solution.py:184
  5.7 1.9 collective-permute-start
  9.0 3.7 %collective-permute-start.3 = (s32[32]{0:T(128)S(1)}, s32[32]{0:T(128)S(1)}, u32[]{:S(2)}, u32[]{:S(2)}) collective-permute-start(s32[32]{0:T(128)S(1)} %select_n.425), channel_id=1, source_target_pairs={{0,6},{1,7},{2,0},{3,1},{4,2},{5,3},{6,4},{7,5},{8,14},{9,15},{10,... | collective-permute-start | bytes 392 | tf_op jit(solution)/shard_map/ppermute | solution.py:68
  11.4 3.9 %collective-permute-start.2 = (s32[32]{0:T(128)S(1)}, s32[32]{0:T(128)S(1)}, u32[]{:S(2)}, u32[]{:S(2)}) collective-permute-start(s32[32]{0:T(128)S(1)} %select_n.425), channel_id=1, source_target_pairs={{0,4},{1,5},{2,6},{3,7},{4,0},{5,1},{6,2},{7,3},{8,12},{9,13},{10,... | collective-permute-start | bytes 392 | tf_op jit(solution)/shard_map/ppermute | solution.py:68
  12.0 3.6 %collective-permute-start.1 = (s32[32]{0:T(128)S(1)}, s32[32]{0:T(128)S(1)}, u32[]{:S(2)}, u32[]{:S(2)}) collective-permute-start(s32[32]{0:T(128)S(1)} %select_n.425), channel_id=1, source_target_pairs={{0,2},{1,3},{2,4},{3,5},{4,6},{5,7},{6,0},{7,1},{8,10},{9,11},{10,... | collective-permute-start | bytes 392 | tf_op jit(solution)/shard_map/ppermute | solution.py:68
  16.3 2.4 %collective-permute-start.4 = (s32[128]{0:T(128)S(1)}, s32[128]{0:T(128)S(1)}, u32[]{:S(2)}, u32[]{:S(2)}) collective-permute-start(s32[128]{0:T(128)S(1)} %select_n.430), channel_id=1, source_target_pairs={{0,8},{1,9},{2,10},{3,11},{4,12},{5,13},{6,14},{7,15},{8,0},{9,1},... | collective-permute-start | bytes 1544 | tf_op jit(solution)/shard_map/ppermute | solution.py:68
  19.4 4.5 %collective-permute-start.7 = (s32[256]{0:T(256)S(1)}, s32[256]{0:T(256)S(1)}, u32[]{:S(2)}, u32[]{:S(2)}) collective-permute-start(s32[256]{0:T(256)S(1)} %fusion.28), channel_id=1, source_target_pairs={{0,48},{1,49},{2,50},{3,51},{4,52},{5,53},{6,54},{7,55},{8,56},{9,... | collective-permute-start | bytes 3080 | tf_op jit(solution)/shard_map/ppermute | solution.py:68
  23.1 3.9 %collective-permute-start.6 = (s32[256]{0:T(256)S(1)}, s32[256]{0:T(256)S(1)}, u32[]{:S(2)}, u32[]{:S(2)}) collective-permute-start(s32[256]{0:T(256)S(1)} %fusion.28), channel_id=1, source_target_pairs={{0,32},{1,33},{2,34},{3,35},{4,36},{5,37},{6,38},{7,39},{8,40},{9,... | collective-permute-start | bytes 3080 | tf_op jit(solution)/shard_map/ppermute | solution.py:68
  23.2 3.9 %collective-permute-start.5 = (s32[256]{0:T(256)S(1)}, s32[256]{0:T(256)S(1)}, u32[]{:S(2)}, u32[]{:S(2)}) collective-permute-start(s32[256]{0:T(256)S(1)} %fusion.28), channel_id=1, source_target_pairs={{0,16},{1,17},{2,18},{3,19},{4,20},{5,21},{6,22},{7,23},{8,24},{9,... | collective-permute-start | bytes 3080 | tf_op jit(solution)/shard_map/ppermute | solution.py:68
  27.7 6.7 %collective-permute-start.8 = (s32[1024]{0:T(1024)S(1)}, s32[1024]{0:T(1024)S(1)}, u32[]{:S(2)}, u32[]{:S(2)}) collective-permute-start(s32[1024]{0:T(1024)S(1)} %bitcast.128), channel_id=1, source_target_pairs={{0,64},{1,65},{2,66},{3,67},{4,68},{5,69},{6,70},{7,71},{8,72},{9,... | collective-permute-start | bytes 12296 | tf_op jit(solution)/shard_map/ppermute | solution.py:68
  36.1 6.5 %collective-permute-start.10 = (f32[7,16384]{1,0:T(8,128)S(1)}, f32[7,16384]{1,0:T(8,128)S(1)}, u32[]{:S(2)}, u32[]{:S(2)}) collective-permute-start(f32[7,16384]{1,0:T(8,128)S(1)} %pad_maximum_fusion.1), channel_id=1, source_target_pairs={{0,1},{1,0},{2,3},{3,2},{4,5},{5,4},{6,7},{7,6},{8,9},{9,8},{10,11... | collective-permute-start | bytes 1376264 | tf_op jit(solution)/shard_map/ppermute | solution.py:184
  56.9 56.3 %copy-start.1 = (pred[8]{0:T(512)(128)(4,1)S(1)}, pred[8]{0:T(512)(128)(4,1)}, u32[]{:S(2)}) copy-start(pred[8]{0:T(512)(128)(4,1)} %constant.364.clone.1) | copy-start | bytes 28
  57.0 13.2 %collective-permute-start.11 = (f32[13,1024]{0,1:T(8,128)S(1)}, f32[13,1024]{0,1:T(8,128)S(1)}, u32[]{:S(2)}, u32[]{:S(2)}) collective-permute-start(f32[13,1024]{0,1:T(8,128)S(1)} %select_bitcast_fusion), channel_id=1, source_target_pairs={{0,8},{1,9},{2,10},{3,11},{4,12},{5,13},{6,14},{7,15},{8,0},{9,1},... | collective-permute-start | bytes 159752 | tf_op jit(solution)/shard_map/ppermute | solution.py:86
  70.3 2.5 %collective-permute-start.12 = (f32[13,512]{0,1:T(8,128)S(1)}, f32[13,512]{0,1:T(8,128)S(1)}, u32[]{:S(2)}, u32[]{:S(2)}) collective-permute-start(f32[13,512]{0,1:T(8,128)S(1)} %select_bitcast_fusion.1), channel_id=1, source_target_pairs={{0,1},{1,0},{2,3},{3,2},{4,5},{5,4},{6,7},{7,6},{8,9},{9,8},{10,11... | collective-permute-start | bytes 79880 | tf_op jit(solution)/shard_map/ppermute | solution.py:86
  72.8 9.1 %collective-permute-start.13 = (f32[13,512]{0,1:T(8,128)S(1)}, f32[13,512]{0,1:T(8,128)S(1)}, u32[]{:S(2)}, u32[]{:S(2)}) collective-permute-start(f32[13,512]{0,1:T(8,128)S(1)} %bitcast_add_fusion.1), channel_id=1, source_target_pairs={{0,64},{1,65},{2,66},{3,67},{4,68},{5,69},{6,70},{7,71},{8,72},{9,... | collective-permute-start | bytes 79880 | tf_op jit(solution)/shard_map/ppermute | solution.py:94
  81.9 6.7 %collective-permute-start.16 = (f32[13,512]{0,1:T(8,128)S(1)}, f32[13,512]{0,1:T(8,128)S(1)}, u32[]{:S(2)}, u32[]{:S(2)}) collective-permute-start(f32[13,512]{0,1:T(8,128)S(1)} %add.438), channel_id=1, source_target_pairs={{0,48},{1,49},{2,50},{3,51},{4,52},{5,53},{6,54},{7,55},{8,56},{9,... | collective-permute-start | bytes 79880 | tf_op jit(solution)/shard_map/ppermute | solution.py:94
  82.2 7.9 %collective-permute-start.15 = (f32[13,512]{0,1:T(8,128)S(1)}, f32[13,512]{0,1:T(8,128)S(1)}, u32[]{:S(2)}, u32[]{:S(2)}) collective-permute-start(f32[13,512]{0,1:T(8,128)S(1)} %add.438), channel_id=1, source_target_pairs={{0,32},{1,33},{2,34},{3,35},{4,36},{5,37},{6,38},{7,39},{8,40},{9,... | collective-permute-start | bytes 79880 | tf_op jit(solution)/shard_map/ppermute | solution.py:94
  83.8 13.8 %collective-permute-start.14 = (f32[13,512]{0,1:T(8,128)S(1)}, f32[13,512]{0,1:T(8,128)S(1)}, u32[]{:S(2)}, u32[]{:S(2)}) collective-permute-start(f32[13,512]{0,1:T(8,128)S(1)} %add.438), channel_id=1, source_target_pairs={{0,16},{1,17},{2,18},{3,19},{4,20},{5,21},{6,22},{7,23},{8,24},{9,... | collective-permute-start | bytes 79880 | tf_op jit(solution)/shard_map/ppermute | solution.py:94
  97.6 7.4 %collective-permute-start.19 = (f32[13,512]{0,1:T(8,128)S(1)}, f32[13,512]{0,1:T(8,128)S(1)}, u32[]{:S(2)}, u32[]{:S(2)}) collective-permute-start(f32[13,512]{0,1:T(8,128)S(1)} %add_add_fusion.1), channel_id=1, source_target_pairs={{0,6},{1,7},{2,0},{3,1},{4,2},{5,3},{6,4},{7,5},{8,14},{9,15},{10,... | collective-permute-start | bytes 79880 | tf_op jit(solution)/shard_map/ppermute | solution.py:94
  97.8 8.7 %collective-permute-start.18 = (f32[13,512]{0,1:T(8,128)S(1)}, f32[13,512]{0,1:T(8,128)S(1)}, u32[]{:S(2)}, u32[]{:S(2)}) collective-permute-start(f32[13,512]{0,1:T(8,128)S(1)} %add_add_fusion.1), channel_id=1, source_target_pairs={{0,4},{1,5},{2,6},{3,7},{4,0},{5,1},{6,2},{7,3},{8,12},{9,13},{10,... | collective-permute-start | bytes 79880 | tf_op jit(solution)/shard_map/ppermute | solution.py:94
  99.1 14.1 %collective-permute-start.17 = (f32[13,512]{0,1:T(8,128)S(1)}, f32[13,512]{0,1:T(8,128)S(1)}, u32[]{:S(2)}, u32[]{:S(2)}) collective-permute-start(f32[13,512]{0,1:T(8,128)S(1)} %add_add_fusion.1), channel_id=1, source_target_pairs={{0,2},{1,3},{2,4},{3,5},{4,6},{5,7},{6,0},{7,1},{8,10},{9,11},{10,... | collective-permute-start | bytes 79880 | tf_op jit(solution)/shard_map/ppermute | solution.py:94
  224.8 4.1 %collective-permute-start.20 = (f32[6,256]{1,0:T(8,128)S(1)}, f32[6,256]{1,0:T(8,128)S(1)}, u32[]{:S(2)}, u32[]{:S(2)}) collective-permute-start(f32[6,256]{1,0:T(8,128)S(1)} %select_bitcast_fusion.3), channel_id=1, source_target_pairs={{0,64},{1,65},{2,66},{3,67},{4,68},{5,69},{6,70},{7,71},{8,72},{9,... | collective-permute-start | bytes 18440 | tf_op jit(solution)/shard_map/ppermute | solution.py:86
  229.0 2.5 %collective-permute-start.23 = (f32[6,64]{1,0:T(8,128)S(1)}, f32[6,64]{1,0:T(8,128)S(1)}, u32[]{:S(2)}, u32[]{:S(2)}) collective-permute-start(f32[6,64]{1,0:T(8,128)S(1)} %bitcast.127), channel_id=1, source_target_pairs={{0,48},{1,49},{2,50},{3,51},{4,52},{5,53},{6,54},{7,55},{8,56},{9,... | collective-permute-start | bytes 4616 | tf_op jit(solution)/shard_map/ppermute | solution.py:86
  229.1 4.0 %collective-permute-start.22 = (f32[6,64]{1,0:T(8,128)S(1)}, f32[6,64]{1,0:T(8,128)S(1)}, u32[]{:S(2)}, u32[]{:S(2)}) collective-permute-start(f32[6,64]{1,0:T(8,128)S(1)} %fusion.6), channel_id=1, source_target_pairs={{0,32},{1,33},{2,34},{3,35},{4,36},{5,37},{6,38},{7,39},{8,40},{9,... | collective-permute-start | bytes 4616 | tf_op jit(solution)/shard_map/ppermute | solution.py:86
  230.5 3.7 %collective-permute-start.21 = (f32[6,64]{1,0:T(8,128)S(1)}, f32[6,64]{1,0:T(8,128)S(1)}, u32[]{:S(2)}, u32[]{:S(2)}) collective-permute-start(f32[6,64]{1,0:T(8,128)S(1)} %fusion.7), channel_id=1, source_target_pairs={{0,16},{1,17},{2,18},{3,19},{4,20},{5,21},{6,22},{7,23},{8,24},{9,... | collective-permute-start | bytes 4616 | tf_op jit(solution)/shard_map/ppermute | solution.py:86
  234.4 2.5 %collective-permute-start.26 = (f32[6,16]{0,1:T(8,128)S(1)}, f32[6,16]{0,1:T(8,128)S(1)}, u32[]{:S(2)}, u32[]{:S(2)}) collective-permute-start(f32[6,16]{0,1:T(8,128)S(1)} %bitcast.124), channel_id=1, source_target_pairs={{0,6},{1,7},{2,0},{3,1},{4,2},{5,3},{6,4},{7,5},{8,14},{9,15},{10,... | collective-permute-start | bytes 1160 | tf_op jit(solution)/shard_map/ppermute | solution.py:86
  234.5 4.0 %collective-permute-start.25 = (f32[6,16]{0,1:T(8,128)S(1)}, f32[6,16]{0,1:T(8,128)S(1)}, u32[]{:S(2)}, u32[]{:S(2)}) collective-permute-start(f32[6,16]{0,1:T(8,128)S(1)} %bitcast.125), channel_id=1, source_target_pairs={{0,4},{1,5},{2,6},{3,7},{4,0},{5,1},{6,2},{7,3},{8,12},{9,13},{10,... | collective-permute-start | bytes 1160 | tf_op jit(solution)/shard_map/ppermute | solution.py:86
  235.8 3.7 %collective-permute-start.24 = (f32[6,16]{0,1:T(8,128)S(1)}, f32[6,16]{0,1:T(8,128)S(1)}, u32[]{:S(2)}, u32[]{:S(2)}) collective-permute-start(f32[6,16]{0,1:T(8,128)S(1)} %bitcast.126), channel_id=1, source_target_pairs={{0,2},{1,3},{2,4},{3,5},{4,6},{5,7},{6,0},{7,1},{8,10},{9,11},{10,... | collective-permute-start | bytes 1160 | tf_op jit(solution)/shard_map/ppermute | solution.py:86

commit v8 on v4

--- a/solution.py
+++ b/solution.py
@@ -136,7 +136,7 @@
         accs = lax.fori_loop(0, num_j // 128, jstep, init, unroll=16)
         for s in range(SUB):
             for c in range(6):
-                out_ref[pl.ds(k0 + 8 * s, 8), c:c + 1] = jnp.sum(accs[s][c], axis=1, keepdims=True)
+                out_ref[pl.ds(k0 + 8 * s, 8), pl.ds(c * 128, 128)] = accs[s][c]
         return carry
 
     lax.fori_loop(0, num_k // step_k, kblock, 0)
@@ -146,7 +146,7 @@
     num_k = active_t.shape[0]
     return pl.pallas_call(
         forces_kernel,
-        out_shape=jax.ShapeDtypeStruct((num_k, 8), jnp.float32),
+        out_shape=jax.ShapeDtypeStruct((num_k, 6 * 128), jnp.float32),
     )(active_t, field_b)
 
 
@@ -177,7 +177,7 @@
     for level in LEVELS:
         active = sum_level(active, level, ndev)
     active_t = jnp.concatenate([active, jnp.zeros((2, num_k), jnp.float32)], axis=0).T
-    partial = pair_forces(active_t, field_b)[:, 0:6].T
+    partial = jnp.sum(pair_forces(active_t, field_b).reshape(num_k, 6, 128), axis=2).T
     payload = jnp.concatenate([partial, corrector_terms(picked)], axis=0)
     for level in reversed(LEVELS):
         payload = reduce_level(payload, level, ndev)

time: 223 us -> 223 us (level)
  Pallas kernels: 118 us -> 110 us
  local copies, waits for them, and re-layouts: 23.2 us -> 28.2 us
  other arithmetic: 2.71 us -> 6.09 us
    pallas_call x1, Pallas kernels: 118 us -> 110 us  [pair_forces(): pl.pallas_call(forces_kernel, out_shape=jax.ShapeDtypeStruct((num_k, 6 *...]
    pallas_call x0 -> x1, local copies, waits for them, and re-layouts: none -> 6.62 us  [pair_forces(): pl.pallas_call(forces_kernel, out_shape=jax.ShapeDtypeStruct((num_k, 6 *...]
    reduce_sum x0 -> x1, other arithmetic: none -> 3.28 us  [on_device(): jnp.sum(pair_forces(active_t, field_b).reshape(num_k, 6, 128), axis=2)]
where the time goes in v8:
time: 223 us
  Pallas kernels  110 us (49%)
  starting transfers between devices  40.8 us (18%)
  waiting for transfers between devices  37 us (17%)
  local copies, waits for them, and re-layouts  28.2 us (13%)
  other arithmetic  6.09 us (3%)
    pallas_call x1, Pallas kernels, pair_forces(): pl.pallas_call(forces_kernel, out_shape=jax.ShapeDtypeStruct((num_k, 6 *...  110 us
    ppermute x9, starting transfers between devices, reduce_level(): total = total + lax.ppermute(piece, ALL, _perm(stride, size, s, ndev))  16 us
    ppermute x9, waiting for transfers between devices, sum_level(): total = total + lax.ppermute(x, ALL, _perm(stride, size, s, ndev))  15.3 us
    ppermute x9, starting transfers between devices, gather_level(): lax.ppermute(x, ALL, _perm(stride, size, s, ndev))  13.9 us
    ppermute x9, waiting for transfers between devices, reduce_level(): total = total + lax.ppermute(piece, ALL, _perm(stride, size, s, ndev))  13.8 us
    ppermute x9, starting transfers between devices, sum_level(): total = total + lax.ppermute(x, ALL, _perm(stride, size, s, ndev))  10.9 us
    gather x2, local copies, waits for them, and re-layouts, on_device(): picked = jnp.take(packed, jnp.clip(local_row, 0, own_stars - 1), axis=1)  7.98 us
    ppermute x9, waiting for transfers between devices, gather_level(): lax.ppermute(x, ALL, _perm(stride, size, s, ndev))  7.85 us
  transfers between devices with their start and end apart: 27, of which 23 were waited for; matrix products, arithmetic and copies ran while one was open for 3% of the time, Pallas kernels for 0%

profile of v8, /device:TPU:1, one launch (start us, length us, event | category | flops | bytes accessed | tf_op | source)
XLA Modules:
  0.0 222.8 jit_solution(12225430164686927349)
XLA Ops:
  0.6 1.5 collective-permute-start
  2.3 0.7 collective-permute-done
  3.0 0.7 pad_add_fusion.3
  4.4 2.6 %collective-permute-start.3 = (s32[32]{0:T(128)S(1)}, s32[32]{0:T(128)S(1)}, u32[]{:S(2)}, u32[]{:S(2)}) collective-permute-start(s32[32]{0:T(128)S(1)} %select_n.413), channel_id=1, source_target_pairs={{0,6},{1,7},{2,0},{3,1},{4,2},{5,3},{6,4},{7,5},{8,14},{9,15},{10,... | collective-permute-start | bytes 392 | tf_op jit(solution)/shard_map/ppermute | solution.py:64
  7.5 0.6 collective-permute-start.1
  8.2 2.7 %collective-permute-done.2 = s32[32]{0:T(128)S(1)} collective-permute-done((s32[32]{0:T(128)S(1)}, s32[32]{0:T(128)S(1)}, u32[]{:S(2)}, u32[]{:S(2)}) %collective-permute-start.2) | collective-permute-done | bytes 160 | tf_op jit(solution)/shard_map/ppermute | solution.py:64
  11.9 1.3 collective-permute-start.4
  13.3 1.0 collective-permute-done.4
  15.0 3.8 %collective-permute-start.7 = (s32[256]{0:T(256)S(1)}, s32[256]{0:T(256)S(1)}, u32[]{:S(2)}, u32[]{:S(2)}) collective-permute-start(s32[256]{0:T(256)S(1)} %fusion.37), channel_id=1, source_target_pairs={{0,48},{1,49},{2,50},{3,51},{4,52},{5,53},{6,54},{7,55},{8,56},{9,... | collective-permute-start | bytes 3080 | tf_op jit(solution)/shard_map/ppermute | solution.py:64
  18.7 0.7 collective-permute-start.5
  19.5 3.2 %collective-permute-done.6 = s32[256]{0:T(256)S(1)} collective-permute-done((s32[256]{0:T(256)S(1)}, s32[256]{0:T(256)S(1)}, u32[]{:S(2)}, u32[]{:S(2)}) %collective-permute-start.6) | collective-permute-done | bytes 1056 | tf_op jit(solution)/shard_map/ppermute | solution.py:64
  22.7 0.6 gather_fusion.3
  23.3 2.9 %collective-permute-start.8 = (s32[1024]{0:T(1024)S(1)}, s32[1024]{0:T(1024)S(1)}, u32[]{:S(2)}, u32[]{:S(2)}) collective-permute-start(s32[1024]{0:T(1024)S(1)} %bitcast.135), channel_id=1, source_target_pairs={{0,64},{1,65},{2,66},{3,67},{4,68},{5,69},{6,70},{7,71},{8,72},{9,... | collective-permute-start | bytes 12296 | tf_op jit(solution)/shard_map/ppermute | solution.py:64
  26.3 4.0 %concatenate.15 = f32[13,8192]{1,0:T(8,128)S(1)} concatenate(f32[3,8192]{1,0:T(4,128)} %param.17, f32[3,8192]{1,0:T(4,128)} %param.18, f32[3,8192]{1,0:T(4,128)} %param.19, f32[3,8192]{1,0:T(4,128)} %param.20, f32[1,8192]{1,0:T(1,128)} %bitcast.116), dimensions={0} | concatenate | bytes 851968 | tf_op jit(solution)/shard_map/concatenate | solution.py:166
  30.4 2.7 %copy.79 = f32[13,8192]{0,1:T(8,128)} copy(f32[13,8192]{1,0:T(8,128)S(1)} %concatenate.15) | data formatting | bytes 851968 | tf_op jit(solution)/shard_map/concatenate | solution.py:166
  33.8 7.6 %gather_fusion.5 = f32[2048,13]{1,0:T(8,128)S(1)} fusion(f32[13,8192]{0,1:T(8,128)} %copy.79, s32[2048]{0:T(1024)S(1)} %broadcast_clamp_fusion), kind=kCustom, calls=%fused_computation.5 | custom fusion | bytes 221184 | tf_op jit(solution)/shard_map/jit(_take)/gather | solution.py:172
  42.0 5.0 %collective-permute-start.9 = (f32[6,2048]{1,0:T(8,128)S(1)}, f32[6,2048]{1,0:T(8,128)S(1)}, u32[]{:S(2)}, u32[]{:S(2)}) collective-permute-start(f32[6,2048]{1,0:T(8,128)S(1)} %pad_maximum_fusion.1), channel_id=1, source_target_pairs={{0,1},{1,0},{2,3},{3,2},{4,5},{5,4},{6,7},{7,6},{8,9},{9,8},{10,11... | collective-permute-start | bytes 147464 | tf_op jit(solution)/shard_map/ppermute | solution.py:90
  47.0 0.9 collective-permute-done.9
  48.0 1.3 collective-permute-start.11
  49.3 0.8 collective-permute-start.10
  50.1 1.0 collective-permute-done.12
  51.1 1.6 collective-permute-done.11
  52.7 2.1 collective-permute-done.10
  55.3 2.7 %collective-permute-done.13 = f32[6,2048]{1,0:T(8,128)S(1)} collective-permute-done((f32[6,2048]{1,0:T(8,128)S(1)}, f32[6,2048]{1,0:T(8,128)S(1)}, u32[]{:S(2)}, u32[]{:S(2)}) %collective-permute-start.13) | collective-permute-done | bytes 49184 | tf_op jit(solution)/shard_map/ppermute | solution.py:90
  58.4 1.5 collective-permute-start.15
  59.9 0.8 collective-permute-start.14
  61.2 1.8 collective-permute-done.15
  63.0 1.3 collective-permute-done.14
  64.3 0.6 collective-permute-start.17
  65.4 3.6 %collective-permute-done.17 = f32[6,2048]{1,0:T(8,128)S(1)} collective-permute-done((f32[6,2048]{1,0:T(8,128)S(1)}, f32[6,2048]{1,0:T(8,128)S(1)}, u32[]{:S(2)}, u32[]{:S(2)}) %collective-permute-start.17) | collective-permute-done | bytes 49184 | tf_op jit(solution)/shard_map/ppermute | solution.py:90
  69.5 1.0 pad_bitcast_fusion.act_ref
  70.5 1.5 broadcast_in_dim.160.fld_ref
  72.0 109.6 %shard_map.102 = f32[2048,768]{1,0:T(8,128)} custom-call(f32[2048,8]{1,0:T(8,128)} %pad_bitcast_fusion.act_ref, f32[8,8,8192]{2,1,0:T(8,128)} %broadcast_in_dim.160.fld_ref), custom_call_target="tpu_custom_call" | custom-call | tf_op jit(solution)/shard_map/pallas_call | solution.py:147
  181.7 6.6 %copy.83 = f32[2048,768]{0,1:T(8,128)} copy(f32[2048,768]{1,0:T(8,128)} %shard_map.102) | data formatting | bytes 12582912 | tf_op jit(solution)/shard_map/pallas_call | solution.py:147
  188.3 3.3 %reduce_sum.9 = f32[2048,6]{0,1:T(8,128)S(1)} reduce(f32[2048,6,128]{0,2,1:T(8,128)} %bitcast.114, f32[]{:T(128)} %constant.346.clone.1), dimensions={2}, to_apply=%region_0.1 | reduce | flops 1560576 | bytes 6340612 | tf_op jit(solution)/shard_map/reduce_sum | solution.py:180
  191.9 0.6 collective-permute-start.18
  192.4 4.1 %collective-permute-done.18 = f32[13,1024]{1,0:T(8,128)S(1)} collective-permute-done((f32[13,1024]{1,0:T(8,128)S(1)}, f32[13,1024]{1,0:T(8,128)S(1)}, u32[]{:S(2)}, u32[]{:S(2)}) %collective-permute-start.18) | collective-permute-done | bytes 53280 | tf_op jit(solution)/shard_map/ppermute | solution.py:82
  196.7 1.2 collective-permute-start.21
  197.9 0.6 collective-permute-start.20
  199.4 2.6 %collective-permute-done.20 = f32[13,256]{1,0:T(8,128)S(1)} collective-permute-done((f32[13,256]{1,0:T(8,128)S(1)}, f32[13,256]{1,0:T(8,128)S(1)}, u32[]{:S(2)}, u32[]{:S(2)}) %collective-permute-start.20) | collective-permute-done | bytes 13344 | tf_op jit(solution)/shard_map/ppermute | solution.py:82
  202.9 2.1 collective-permute-done.22
  205.1 0.9 collective-permute-start.25
  206.0 0.6 collective-permute-start.24
  207.0 1.0 collective-permute-done.25
  208.0 2.0 collective-permute-done.24
  210.4 11.0 %collective-permute-start.26 = (f32[13,16]{1,0:T(8,128)S(1)}, f32[13,16]{1,0:T(8,128)S(1)}, u32[]{:S(2)}, u32[]{:S(2)}) collective-permute-start(f32[13,16]{1,0:T(8,128)S(1)} %bitcast.134), channel_id=1, source_target_pairs={{0,1},{1,0},{2,3},{3,2},{4,5},{5,4},{6,7},{7,6},{8,9},{9,8},{10,11... | collective-permute-start | bytes 2504 | tf_op jit(solution)/shard_map/ppermute | solution.py:82
  221.3 0.8 collective-permute-done.26
  222.2 0.6 fusion.19
  (113 shorter events, 10.0 us)
Async XLA Ops:
  0.6 2.4 %collective-permute-start = (s32[16]{0:T(128)}, s32[16]{0:T(128)S(1)}, u32[]{:S(2)}, u32[]{:S(2)}) collective-permute-start(s32[16]{0:T(128)} %param.23), channel_id=1, source_target_pairs={{0,1},{1,0},{2,3},{3,2},{4,5},{5,4},{6,7},{7,6},{8,9},{9,8},{10,11... | collective-permute-start | bytes 200 | tf_op jit(solution)/shard_map/ppermute | solution.py:64
  4.4 3.8 %collective-permute-start.3 = (s32[32]{0:T(128)S(1)}, s32[32]{0:T(128)S(1)}, u32[]{:S(2)}, u32[]{:S(2)}) collective-permute-start(s32[32]{0:T(128)S(1)} %select_n.413), channel_id=1, source_target_pairs={{0,6},{1,7},{2,0},{3,1},{4,2},{5,3},{6,4},{7,5},{8,14},{9,15},{10,... | collective-permute-start | bytes 392 | tf_op jit(solution)/shard_map/ppermute | solution.py:64
  7.0 3.9 %collective-permute-start.2 = (s32[32]{0:T(128)S(1)}, s32[32]{0:T(128)S(1)}, u32[]{:S(2)}, u32[]{:S(2)}) collective-permute-start(s32[32]{0:T(128)S(1)} %select_n.413), channel_id=1, source_target_pairs={{0,4},{1,5},{2,6},{3,7},{4,0},{5,1},{6,2},{7,3},{8,12},{9,13},{10,... | collective-permute-start | bytes 392 | tf_op jit(solution)/shard_map/ppermute | solution.py:64
  7.5 3.6 %collective-permute-start.1 = (s32[32]{0:T(128)S(1)}, s32[32]{0:T(128)S(1)}, u32[]{:S(2)}, u32[]{:S(2)}) collective-permute-start(s32[32]{0:T(128)S(1)} %select_n.413), channel_id=1, source_target_pairs={{0,2},{1,3},{2,4},{3,5},{4,6},{5,7},{6,0},{7,1},{8,10},{9,11},{10,... | collective-permute-start | bytes 392 | tf_op jit(solution)/shard_map/ppermute | solution.py:64
  11.9 2.4 %collective-permute-start.4 = (s32[128]{0:T(128)S(1)}, s32[128]{0:T(128)S(1)}, u32[]{:S(2)}, u32[]{:S(2)}) collective-permute-start(s32[128]{0:T(128)S(1)} %select_n.418), channel_id=1, source_target_pairs={{0,8},{1,9},{2,10},{3,11},{4,12},{5,13},{6,14},{7,15},{8,0},{9,1},... | collective-permute-start | bytes 1544 | tf_op jit(solution)/shard_map/ppermute | solution.py:64
  15.0 4.5 %collective-permute-start.7 = (s32[256]{0:T(256)S(1)}, s32[256]{0:T(256)S(1)}, u32[]{:S(2)}, u32[]{:S(2)}) collective-permute-start(s32[256]{0:T(256)S(1)} %fusion.37), channel_id=1, source_target_pairs={{0,48},{1,49},{2,50},{3,51},{4,52},{5,53},{6,54},{7,55},{8,56},{9,... | collective-permute-start | bytes 3080 | tf_op jit(solution)/shard_map/ppermute | solution.py:64
  18.7 3.9 %collective-permute-start.6 = (s32[256]{0:T(256)S(1)}, s32[256]{0:T(256)S(1)}, u32[]{:S(2)}, u32[]{:S(2)}) collective-permute-start(s32[256]{0:T(256)S(1)} %fusion.37), channel_id=1, source_target_pairs={{0,32},{1,33},{2,34},{3,35},{4,36},{5,37},{6,38},{7,39},{8,40},{9,... | collective-permute-start | bytes 3080 | tf_op jit(solution)/shard_map/ppermute | solution.py:64
  18.7 3.9 %collective-permute-start.5 = (s32[256]{0:T(256)S(1)}, s32[256]{0:T(256)S(1)}, u32[]{:S(2)}, u32[]{:S(2)}) collective-permute-start(s32[256]{0:T(256)S(1)} %fusion.37), channel_id=1, source_target_pairs={{0,16},{1,17},{2,18},{3,19},{4,20},{5,21},{6,22},{7,23},{8,24},{9,... | collective-permute-start | bytes 3080 | tf_op jit(solution)/shard_map/ppermute | solution.py:64
  23.3 9.7 %collective-permute-start.8 = (s32[1024]{0:T(1024)S(1)}, s32[1024]{0:T(1024)S(1)}, u32[]{:S(2)}, u32[]{:S(2)}) collective-permute-start(s32[1024]{0:T(1024)S(1)} %bitcast.135), channel_id=1, source_target_pairs={{0,64},{1,65},{2,66},{3,67},{4,68},{5,69},{6,70},{7,71},{8,72},{9,... | collective-permute-start | bytes 12296 | tf_op jit(solution)/shard_map/ppermute | solution.py:64
  30.3 25.0 %copy-start.4 = (f32[8192]{0:T(1024)S(1)}, f32[8192]{0:T(1024)}, u32[]{:S(2)}) copy-start(f32[8192]{0:T(1024)} %param.22) | copy-start | bytes 98308
  30.3 30.4 %copy-start = (f32[3,8192]{1,0:T(4,128)S(1)}, f32[3,8192]{1,0:T(4,128)}, u32[]{:S(2)}) copy-start(f32[3,8192]{1,0:T(4,128)} %param.17) | copy-start | bytes 294916
  30.3 30.4 %copy-start.1 = (f32[3,8192]{1,0:T(4,128)S(1)}, f32[3,8192]{1,0:T(4,128)}, u32[]{:S(2)}) copy-start(f32[3,8192]{1,0:T(4,128)} %param.18) | copy-start | bytes 294916
  30.4 30.4 %copy-start.2 = (f32[3,8192]{1,0:T(4,128)S(1)}, f32[3,8192]{1,0:T(4,128)}, u32[]{:S(2)}) copy-start(f32[3,8192]{1,0:T(4,128)} %param.19) | copy-start | bytes 294916
  30.4 30.4 %copy-start.3 = (f32[3,8192]{1,0:T(4,128)S(1)}, f32[3,8192]{1,0:T(4,128)}, u32[]{:S(2)}) copy-start(f32[3,8192]{1,0:T(4,128)} %param.20) | copy-start | bytes 294916
  30.4 34.5 %copy-start.5 = (f32[8192]{0:T(1024)S(1)}, f32[8192]{0:T(1024)}, u32[]{:S(2)}) copy-start(f32[8192]{0:T(1024)} %param.21) | copy-start | bytes 98308
  42.0 5.9 %collective-permute-start.9 = (f32[6,2048]{1,0:T(8,128)S(1)}, f32[6,2048]{1,0:T(8,128)S(1)}, u32[]{:S(2)}, u32[]{:S(2)}) collective-permute-start(f32[6,2048]{1,0:T(8,128)S(1)} %pad_maximum_fusion.1), channel_id=1, source_target_pairs={{0,1},{1,0},{2,3},{3,2},{4,5},{5,4},{6,7},{7,6},{8,9},{9,8},{10,11... | collective-permute-start | bytes 147464 | tf_op jit(solution)/shard_map/ppermute | solution.py:90
  47.9 3.2 %collective-permute-start.12 = (f32[6,2048]{1,0:T(8,128)S(1)}, f32[6,2048]{1,0:T(8,128)S(1)}, u32[]{:S(2)}, u32[]{:S(2)}) collective-permute-start(f32[6,2048]{1,0:T(8,128)S(1)} %fusion.35), channel_id=1, source_target_pairs={{0,6},{1,7},{2,0},{3,1},{4,2},{5,3},{6,4},{7,5},{8,14},{9,15},{10,... | collective-permute-start | bytes 147464 | tf_op jit(solution)/shard_map/ppermute | solution.py:90
  48.0 4.7 %collective-permute-start.11 = (f32[6,2048]{1,0:T(8,128)S(1)}, f32[6,2048]{1,0:T(8,128)S(1)}, u32[]{:S(2)}, u32[]{:S(2)}) collective-permute-start(f32[6,2048]{1,0:T(8,128)S(1)} %fusion.35), channel_id=1, source_target_pairs={{0,4},{1,5},{2,6},{3,7},{4,0},{5,1},{6,2},{7,3},{8,12},{9,13},{10,... | collective-permute-start | bytes 147464 | tf_op jit(solution)/shard_map/ppermute | solution.py:90
  49.3 5.5 %collective-permute-start.10 = (f32[6,2048]{1,0:T(8,128)S(1)}, f32[6,2048]{1,0:T(8,128)S(1)}, u32[]{:S(2)}, u32[]{:S(2)}) collective-permute-start(f32[6,2048]{1,0:T(8,128)S(1)} %fusion.35), channel_id=1, source_target_pairs={{0,2},{1,3},{2,4},{3,5},{4,6},{5,7},{6,0},{7,1},{8,10},{9,11},{10,... | collective-permute-start | bytes 147464 | tf_op jit(solution)/shard_map/ppermute | solution.py:90
  54.8 3.2 %collective-permute-start.13 = (f32[6,2048]{1,0:T(8,128)S(1)}, f32[6,2048]{1,0:T(8,128)S(1)}, u32[]{:S(2)}, u32[]{:S(2)}) collective-permute-start(f32[6,2048]{1,0:T(8,128)S(1)} %add_add_fusion.1), channel_id=1, source_target_pairs={{0,8},{1,9},{2,10},{3,11},{4,12},{5,13},{6,14},{7,15},{8,0},{9,1},... | collective-permute-start | bytes 147464 | tf_op jit(solution)/shard_map/ppermute | solution.py:90
  58.0 3.2 %collective-permute-start.16 = (f32[6,2048]{1,0:T(8,128)S(1)}, f32[6,2048]{1,0:T(8,128)S(1)}, u32[]{:S(2)}, u32[]{:S(2)}) collective-permute-start(f32[6,2048]{1,0:T(8,128)S(1)} %add.420), channel_id=1, source_target_pairs={{0,48},{1,49},{2,50},{3,51},{4,52},{5,53},{6,54},{7,55},{8,56},{9,... | collective-permute-start | bytes 147464 | tf_op jit(solution)/shard_map/ppermute | solution.py:90
  58.4 4.6 %collective-permute-start.15 = (f32[6,2048]{1,0:T(8,128)S(1)}, f32[6,2048]{1,0:T(8,128)S(1)}, u32[]{:S(2)}, u32[]{:S(2)}) collective-permute-start(f32[6,2048]{1,0:T(8,128)S(1)} %add.420), channel_id=1, source_target_pairs={{0,32},{1,33},{2,34},{3,35},{4,36},{5,37},{6,38},{7,39},{8,40},{9,... | collective-permute-start | bytes 147464 | tf_op jit(solution)/shard_map/ppermute | solution.py:90
  59.9 4.3 %collective-permute-start.14 = (f32[6,2048]{1,0:T(8,128)S(1)}, f32[6,2048]{1,0:T(8,128)S(1)}, u32[]{:S(2)}, u32[]{:S(2)}) collective-permute-start(f32[6,2048]{1,0:T(8,128)S(1)} %add.420), channel_id=1, source_target_pairs={{0,16},{1,17},{2,18},{3,19},{4,20},{5,21},{6,22},{7,23},{8,24},{9,... | collective-permute-start | bytes 147464 | tf_op jit(solution)/shard_map/ppermute | solution.py:90
  64.3 4.7 %collective-permute-start.17 = (f32[6,2048]{1,0:T(8,128)S(1)}, f32[6,2048]{1,0:T(8,128)S(1)}, u32[]{:S(2)}, u32[]{:S(2)}) collective-permute-start(f32[6,2048]{1,0:T(8,128)S(1)} %add_add_fusion), channel_id=1, source_target_pairs={{0,64},{1,65},{2,66},{3,67},{4,68},{5,69},{6,70},{7,71},{8,72},{9,... | collective-permute-start | bytes 147464 | tf_op jit(solution)/shard_map/ppermute | solution.py:90
  191.9 4.7 %collective-permute-start.18 = (f32[13,1024]{1,0:T(8,128)S(1)}, f32[13,1024]{1,0:T(8,128)S(1)}, u32[]{:S(2)}, u32[]{:S(2)}) collective-permute-start(f32[13,1024]{1,0:T(8,128)S(1)} %bitcast.122), channel_id=1, source_target_pairs={{0,64},{1,65},{2,66},{3,67},{4,68},{5,69},{6,70},{7,71},{8,72},{9,... | collective-permute-start | bytes 159752 | tf_op jit(solution)/shard_map/ppermute | solution.py:82
  196.7 2.7 %collective-permute-start.21 = (f32[13,256]{1,0:T(8,128)S(1)}, f32[13,256]{1,0:T(8,128)S(1)}, u32[]{:S(2)}, u32[]{:S(2)}) collective-permute-start(f32[13,256]{1,0:T(8,128)S(1)} %bitcast.130), channel_id=1, source_target_pairs={{0,48},{1,49},{2,50},{3,51},{4,52},{5,53},{6,54},{7,55},{8,56},{9,... | collective-permute-start | bytes 39944 | tf_op jit(solution)/shard_map/ppermute | solution.py:82
  197.9 4.1 %collective-permute-start.20 = (f32[13,256]{1,0:T(8,128)S(1)}, f32[13,256]{1,0:T(8,128)S(1)}, u32[]{:S(2)}, u32[]{:S(2)}) collective-permute-start(f32[13,256]{1,0:T(8,128)S(1)} %fusion.2), channel_id=1, source_target_pairs={{0,32},{1,33},{2,34},{3,35},{4,36},{5,37},{6,38},{7,39},{8,40},{9,... | collective-permute-start | bytes 39944 | tf_op jit(solution)/shard_map/ppermute | solution.py:82
  198.5 3.8 %collective-permute-start.19 = (f32[13,256]{1,0:T(8,128)S(1)}, f32[13,256]{1,0:T(8,128)S(1)}, u32[]{:S(2)}, u32[]{:S(2)}) collective-permute-start(f32[13,256]{1,0:T(8,128)S(1)} %fusion.3), channel_id=1, source_target_pairs={{0,16},{1,17},{2,18},{3,19},{4,20},{5,21},{6,22},{7,23},{8,24},{9,... | collective-permute-start | bytes 39944 | tf_op jit(solution)/shard_map/ppermute | solution.py:82
  202.4 2.6 %collective-permute-start.22 = (f32[13,128]{1,0:T(8,128)S(1)}, f32[13,128]{1,0:T(8,128)S(1)}, u32[]{:S(2)}, u32[]{:S(2)}) collective-permute-start(f32[13,128]{1,0:T(8,128)S(1)} %bitcast.132), channel_id=1, source_target_pairs={{0,8},{1,9},{2,10},{3,11},{4,12},{5,13},{6,14},{7,15},{8,0},{9,1},... | collective-permute-start | bytes 19976 | tf_op jit(solution)/shard_map/ppermute | solution.py:82
  205.1 2.9 %collective-permute-start.25 = (f32[13,32]{1,0:T(8,128)S(1)}, f32[13,32]{1,0:T(8,128)S(1)}, u32[]{:S(2)}, u32[]{:S(2)}) collective-permute-start(f32[13,32]{1,0:T(8,128)S(1)} %bitcast.133), channel_id=1, source_target_pairs={{0,6},{1,7},{2,0},{3,1},{4,2},{5,3},{6,4},{7,5},{8,14},{9,15},{10,... | collective-permute-start | bytes 5000 | tf_op jit(solution)/shard_map/ppermute | solution.py:82
  206.0 4.0 %collective-permute-start.24 = (f32[13,32]{1,0:T(8,128)S(1)}, f32[13,32]{1,0:T(8,128)S(1)}, u32[]{:S(2)}, u32[]{:S(2)}) collective-permute-start(f32[13,32]{1,0:T(8,128)S(1)} %fusion.10), channel_id=1, source_target_pairs={{0,4},{1,5},{2,6},{3,7},{4,0},{5,1},{6,2},{7,3},{8,12},{9,13},{10,... | collective-permute-start | bytes 5000 | tf_op jit(solution)/shard_map/ppermute | solution.py:82
  206.6 3.7 %collective-permute-start.23 = (f32[13,32]{1,0:T(8,128)S(1)}, f32[13,32]{1,0:T(8,128)S(1)}, u32[]{:S(2)}, u32[]{:S(2)}) collective-permute-start(f32[13,32]{1,0:T(8,128)S(1)} %fusion.11), channel_id=1, source_target_pairs={{0,2},{1,3},{2,4},{3,5},{4,6},{5,7},{6,0},{7,1},{8,10},{9,11},{10,... | collective-permute-start | bytes 5000 | tf_op jit(solution)/shard_map/ppermute | solution.py:82
  210.4 11.8 %collective-permute-start.26 = (f32[13,16]{1,0:T(8,128)S(1)}, f32[13,16]{1,0:T(8,128)S(1)}, u32[]{:S(2)}, u32[]{:S(2)}) collective-permute-start(f32[13,16]{1,0:T(8,128)S(1)} %bitcast.134), channel_id=1, source_target_pairs={{0,1},{1,0},{2,3},{3,2},{4,5},{5,4},{6,7},{7,6},{8,9},{9,8},{10,11... | collective-permute-start | bytes 2504 | tf_op jit(solution)/shard_map/ppermute | solution.py:82

commit v9 on v8

--- a/solution.py
+++ b/solution.py
@@ -136,7 +136,7 @@
         accs = lax.fori_loop(0, num_j // 128, jstep, init, unroll=16)
         for s in range(SUB):
             for c in range(6):
-                out_ref[pl.ds(k0 + 8 * s, 8), pl.ds(c * 128, 128)] = accs[s][c]
+                out_ref[c, pl.ds(k0 + 8 * s, 8), :] = accs[s][c]
         return carry
 
     lax.fori_loop(0, num_k // step_k, kblock, 0)
@@ -146,7 +146,7 @@
     num_k = active_t.shape[0]
     return pl.pallas_call(
         forces_kernel,
-        out_shape=jax.ShapeDtypeStruct((num_k, 6 * 128), jnp.float32),
+        out_shape=jax.ShapeDtypeStruct((6, num_k, 128), jnp.float32),
     )(active_t, field_b)
 
 
@@ -177,7 +177,7 @@
     for level in LEVELS:
         active = sum_level(active, level, ndev)
     active_t = jnp.concatenate([active, jnp.zeros((2, num_k), jnp.float32)], axis=0).T
-    partial = jnp.sum(pair_forces(active_t, field_b).reshape(num_k, 6, 128), axis=2).T
+    partial = jnp.sum(pair_forces(active_t, field_b), axis=2)
     payload = jnp.concatenate([partial, corrector_terms(picked)], axis=0)
     for level in reversed(LEVELS):
         payload = reduce_level(payload, level, ndev)

time: 223 us -> 218 us (0.978)
  local copies, waits for them, and re-layouts: 28.2 us -> 21.6 us
    pallas_call x1 -> x0, local copies, waits for them, and re-layouts: 6.62 us -> none  [pair_forces(): pl.pallas_call(forces_kernel, out_shape=jax.ShapeDtypeStruct((num_k, 6 *...]
  transfers between devices with their start and end apart: 27 -> 27, of which waited for: 23 -> 23; matrix products, arithmetic and copies ran while one was open for 3% -> 4% of each run, Pallas kernels for 0% -> 0%
where the time goes in v9:
time: 218 us; the launch traced here: 217 us
  Pallas kernels  110 us (50%)
  starting transfers between devices  40.8 us (19%)
  waiting for transfers between devices  37 us (17%)
  local copies, waits for them, and re-layouts  21.6 us (10%)
  other arithmetic  7.28 us (3%)
    pallas_call x1, Pallas kernels, pair_forces(): pl.pallas_call(forces_kernel, out_shape=jax.ShapeDtypeStruct((6, num_k, 1...  110 us
    ppermute x9, starting transfers between devices, reduce_level(): total = total + lax.ppermute(piece, ALL, _perm(stride, size, s, ndev))  16 us
    ppermute x9, waiting for transfers between devices, sum_level(): total = total + lax.ppermute(x, ALL, _perm(stride, size, s, ndev))  15.3 us
    ppermute x9, starting transfers between devices, gather_level(): lax.ppermute(x, ALL, _perm(stride, size, s, ndev))  13.9 us
    ppermute x9, waiting for transfers between devices, reduce_level(): total = total + lax.ppermute(piece, ALL, _perm(stride, size, s, ndev))  13.8 us
    ppermute x9, starting transfers between devices, sum_level(): total = total + lax.ppermute(x, ALL, _perm(stride, size, s, ndev))  10.9 us
    gather x2, local copies, waits for them, and re-layouts, on_device(): picked = jnp.take(packed, jnp.clip(local_row, 0, own_stars - 1), axis=1)  7.98 us
    ppermute x9, waiting for transfers between devices, gather_level(): lax.ppermute(x, ALL, _perm(stride, size, s, ndev))  7.85 us
  transfers between devices with their start and end apart: 27, of which 23 were waited for; matrix products, arithmetic and copies ran while one was open for 4% of the time, Pallas kernels for 0%

profile of v9, /device:TPU:1, one launch (start us, length us, event | category | flops | bytes accessed | tf_op | source)
XLA Modules:
  0.0 217.4 jit_solution(968451300676938481)
XLA Ops:
  0.6 1.5 collective-permute-start
  2.3 0.7 collective-permute-done
  3.0 0.7 pad_add_fusion.3
  4.4 2.6 %collective-permute-start.3 = (s32[32]{0:T(128)S(1)}, s32[32]{0:T(128)S(1)}, u32[]{:S(2)}, u32[]{:S(2)}) collective-permute-start(s32[32]{0:T(128)S(1)} %select_n.413), channel_id=1, source_target_pairs={{0,6},{1,7},{2,0},{3,1},{4,2},{5,3},{6,4},{7,5},{8,14},{9,15},{10,... | collective-permute-start | bytes 392 | tf_op jit(solution)/shard_map/ppermute | solution.py:64
  7.5 0.6 collective-permute-start.1
  8.2 2.7 %collective-permute-done.2 = s32[32]{0:T(128)S(1)} collective-permute-done((s32[32]{0:T(128)S(1)}, s32[32]{0:T(128)S(1)}, u32[]{:S(2)}, u32[]{:S(2)}) %collective-permute-start.2) | collective-permute-done | bytes 160 | tf_op jit(solution)/shard_map/ppermute | solution.py:64
  11.9 1.3 collective-permute-start.4
  13.3 1.0 collective-permute-done.4
  15.0 3.8 %collective-permute-start.7 = (s32[256]{0:T(256)S(1)}, s32[256]{0:T(256)S(1)}, u32[]{:S(2)}, u32[]{:S(2)}) collective-permute-start(s32[256]{0:T(256)S(1)} %fusion.37), channel_id=1, source_target_pairs={{0,48},{1,49},{2,50},{3,51},{4,52},{5,53},{6,54},{7,55},{8,56},{9,... | collective-permute-start | bytes 3080 | tf_op jit(solution)/shard_map/ppermute | solution.py:64
  18.7 0.7 collective-permute-start.5
  19.5 3.2 %collective-permute-done.6 = s32[256]{0:T(256)S(1)} collective-permute-done((s32[256]{0:T(256)S(1)}, s32[256]{0:T(256)S(1)}, u32[]{:S(2)}, u32[]{:S(2)}) %collective-permute-start.6) | collective-permute-done | bytes 1056 | tf_op jit(solution)/shard_map/ppermute | solution.py:64
  22.7 0.6 gather_fusion.3
  23.3 2.9 %collective-permute-start.8 = (s32[1024]{0:T(1024)S(1)}, s32[1024]{0:T(1024)S(1)}, u32[]{:S(2)}, u32[]{:S(2)}) collective-permute-start(s32[1024]{0:T(1024)S(1)} %bitcast.131), channel_id=1, source_target_pairs={{0,64},{1,65},{2,66},{3,67},{4,68},{5,69},{6,70},{7,71},{8,72},{9,... | collective-permute-start | bytes 12296 | tf_op jit(solution)/shard_map/ppermute | solution.py:64
  26.3 4.0 %concatenate.15 = f32[13,8192]{1,0:T(8,128)S(1)} concatenate(f32[3,8192]{1,0:T(4,128)} %param.17, f32[3,8192]{1,0:T(4,128)} %param.18, f32[3,8192]{1,0:T(4,128)} %param.19, f32[3,8192]{1,0:T(4,128)} %param.20, f32[1,8192]{1,0:T(1,128)} %bitcast.113), dimensions={0} | concatenate | bytes 851968 | tf_op jit(solution)/shard_map/concatenate | solution.py:166
  30.4 2.7 %copy.84 = f32[13,8192]{0,1:T(8,128)} copy(f32[13,8192]{1,0:T(8,128)S(1)} %concatenate.15) | data formatting | bytes 851968 | tf_op jit(solution)/shard_map/concatenate | solution.py:166
  33.1 0.6 gather_fusion.4
  33.8 7.6 %gather_fusion.5 = f32[2048,13]{1,0:T(8,128)S(1)} fusion(f32[13,8192]{0,1:T(8,128)} %copy.84, s32[2048]{0:T(1024)S(1)} %broadcast_clamp_fusion), kind=kCustom, calls=%fused_computation.5 | custom fusion | bytes 221184 | tf_op jit(solution)/shard_map/jit(_take)/gather | solution.py:172
  42.0 5.0 %collective-permute-start.9 = (f32[6,2048]{1,0:T(8,128)S(1)}, f32[6,2048]{1,0:T(8,128)S(1)}, u32[]{:S(2)}, u32[]{:S(2)}) collective-permute-start(f32[6,2048]{1,0:T(8,128)S(1)} %pad_maximum_fusion.1), channel_id=1, source_target_pairs={{0,1},{1,0},{2,3},{3,2},{4,5},{5,4},{6,7},{7,6},{8,9},{9,8},{10,11... | collective-permute-start | bytes 147464 | tf_op jit(solution)/shard_map/ppermute | solution.py:90
  47.0 0.9 collective-permute-done.9
  48.0 1.3 collective-permute-start.11
  49.3 0.8 collective-permute-start.10
  50.1 1.0 collective-permute-done.12
  51.1 1.6 collective-permute-done.11
  52.7 2.1 collective-permute-done.10
  55.3 2.7 %collective-permute-done.13 = f32[6,2048]{1,0:T(8,128)S(1)} collective-permute-done((f32[6,2048]{1,0:T(8,128)S(1)}, f32[6,2048]{1,0:T(8,128)S(1)}, u32[]{:S(2)}, u32[]{:S(2)}) %collective-permute-start.13) | collective-permute-done | bytes 49184 | tf_op jit(solution)/shard_map/ppermute | solution.py:90
  58.4 1.5 collective-permute-start.15
  59.9 0.8 collective-permute-start.14
  61.2 1.8 collective-permute-done.15
  63.0 1.3 collective-permute-done.14
  64.3 0.6 collective-permute-start.17
  65.4 3.6 %collective-permute-done.17 = f32[6,2048]{1,0:T(8,128)S(1)} collective-permute-done((f32[6,2048]{1,0:T(8,128)S(1)}, f32[6,2048]{1,0:T(8,128)S(1)}, u32[]{:S(2)}, u32[]{:S(2)}) %collective-permute-start.17) | collective-permute-done | bytes 49184 | tf_op jit(solution)/shard_map/ppermute | solution.py:90
  69.5 1.0 pad_bitcast_fusion.act_ref
  70.5 1.5 broadcast_in_dim.160.fld_ref
  72.1 109.6 %shard_map.102 = f32[6,2048,128]{2,1,0:T(8,128)} custom-call(f32[2048,8]{1,0:T(8,128)} %pad_bitcast_fusion.act_ref, f32[8,8,8192]{2,1,0:T(8,128)} %broadcast_in_dim.160.fld_ref), custom_call_target="tpu_custom_call" | custom-call | tf_op jit(solution)/shard_map/pallas_call | solution.py:147
  181.7 4.5 %reduce_sum.9 = f32[6,2048]{1,0:T(8,128)S(1)} reduce(f32[6,2048,128]{2,1,0:T(8,128)} %shard_map.102, f32[]{:T(128)} %constant.346.clone.1), dimensions={2}, to_apply=%region_0.1 | reduce | flops 1560576 | bytes 6340612 | tf_op jit(solution)/shard_map/reduce_sum | solution.py:180
  186.4 0.6 collective-permute-start.18
  187.0 4.1 %collective-permute-done.18 = f32[13,1024]{1,0:T(8,128)S(1)} collective-permute-done((f32[13,1024]{1,0:T(8,128)S(1)}, f32[13,1024]{1,0:T(8,128)S(1)}, u32[]{:S(2)}, u32[]{:S(2)}) %collective-permute-start.18) | collective-permute-done | bytes 53280 | tf_op jit(solution)/shard_map/ppermute | solution.py:82
  191.3 1.2 collective-permute-start.21
  192.5 0.6 collective-permute-start.20
  193.9 2.6 %collective-permute-done.20 = f32[13,256]{1,0:T(8,128)S(1)} collective-permute-done((f32[13,256]{1,0:T(8,128)S(1)}, f32[13,256]{1,0:T(8,128)S(1)}, u32[]{:S(2)}, u32[]{:S(2)}) %collective-permute-start.20) | collective-permute-done | bytes 13344 | tf_op jit(solution)/shard_map/ppermute | solution.py:82
  197.4 2.1 collective-permute-done.22
  199.7 0.9 collective-permute-start.25
  200.5 0.6 collective-permute-start.24
  201.6 1.0 collective-permute-done.25
  202.5 2.0 collective-permute-done.24
  205.0 11.0 %collective-permute-start.26 = (f32[13,16]{1,0:T(8,128)S(1)}, f32[13,16]{1,0:T(8,128)S(1)}, u32[]{:S(2)}, u32[]{:S(2)}) collective-permute-start(f32[13,16]{1,0:T(8,128)S(1)} %bitcast.130), channel_id=1, source_target_pairs={{0,1},{1,0},{2,3},{3,2},{4,5},{5,4},{6,7},{7,6},{8,9},{9,8},{10,11... | collective-permute-start | bytes 2504 | tf_op jit(solution)/shard_map/ppermute | solution.py:82
  215.9 0.8 collective-permute-done.26
  216.8 0.6 fusion.19
  (112 shorter events, 9.5 us)
Async XLA Ops:
  0.6 2.4 %collective-permute-start = (s32[16]{0:T(128)}, s32[16]{0:T(128)S(1)}, u32[]{:S(2)}, u32[]{:S(2)}) collective-permute-start(s32[16]{0:T(128)} %param.23), channel_id=1, source_target_pairs={{0,1},{1,0},{2,3},{3,2},{4,5},{5,4},{6,7},{7,6},{8,9},{9,8},{10,11... | collective-permute-start | bytes 200 | tf_op jit(solution)/shard_map/ppermute | solution.py:64
  4.4 3.8 %collective-permute-start.3 = (s32[32]{0:T(128)S(1)}, s32[32]{0:T(128)S(1)}, u32[]{:S(2)}, u32[]{:S(2)}) collective-permute-start(s32[32]{0:T(128)S(1)} %select_n.413), channel_id=1, source_target_pairs={{0,6},{1,7},{2,0},{3,1},{4,2},{5,3},{6,4},{7,5},{8,14},{9,15},{10,... | collective-permute-start | bytes 392 | tf_op jit(solution)/shard_map/ppermute | solution.py:64
  7.0 3.9 %collective-permute-start.2 = (s32[32]{0:T(128)S(1)}, s32[32]{0:T(128)S(1)}, u32[]{:S(2)}, u32[]{:S(2)}) collective-permute-start(s32[32]{0:T(128)S(1)} %select_n.413), channel_id=1, source_target_pairs={{0,4},{1,5},{2,6},{3,7},{4,0},{5,1},{6,2},{7,3},{8,12},{9,13},{10,... | collective-permute-start | bytes 392 | tf_op jit(solution)/shard_map/ppermute | solution.py:64
  7.5 3.6 %collective-permute-start.1 = (s32[32]{0:T(128)S(1)}, s32[32]{0:T(128)S(1)}, u32[]{:S(2)}, u32[]{:S(2)}) collective-permute-start(s32[32]{0:T(128)S(1)} %select_n.413), channel_id=1, source_target_pairs={{0,2},{1,3},{2,4},{3,5},{4,6},{5,7},{6,0},{7,1},{8,10},{9,11},{10,... | collective-permute-start | bytes 392 | tf_op jit(solution)/shard_map/ppermute | solution.py:64
  11.9 2.4 %collective-permute-start.4 = (s32[128]{0:T(128)S(1)}, s32[128]{0:T(128)S(1)}, u32[]{:S(2)}, u32[]{:S(2)}) collective-permute-start(s32[128]{0:T(128)S(1)} %select_n.418), channel_id=1, source_target_pairs={{0,8},{1,9},{2,10},{3,11},{4,12},{5,13},{6,14},{7,15},{8,0},{9,1},... | collective-permute-start | bytes 1544 | tf_op jit(solution)/shard_map/ppermute | solution.py:64
  15.0 4.5 %collective-permute-start.7 = (s32[256]{0:T(256)S(1)}, s32[256]{0:T(256)S(1)}, u32[]{:S(2)}, u32[]{:S(2)}) collective-permute-start(s32[256]{0:T(256)S(1)} %fusion.37), channel_id=1, source_target_pairs={{0,48},{1,49},{2,50},{3,51},{4,52},{5,53},{6,54},{7,55},{8,56},{9,... | collective-permute-start | bytes 3080 | tf_op jit(solution)/shard_map/ppermute | solution.py:64
  18.7 3.9 %collective-permute-start.6 = (s32[256]{0:T(256)S(1)}, s32[256]{0:T(256)S(1)}, u32[]{:S(2)}, u32[]{:S(2)}) collective-permute-start(s32[256]{0:T(256)S(1)} %fusion.37), channel_id=1, source_target_pairs={{0,32},{1,33},{2,34},{3,35},{4,36},{5,37},{6,38},{7,39},{8,40},{9,... | collective-permute-start | bytes 3080 | tf_op jit(solution)/shard_map/ppermute | solution.py:64
  18.7 3.9 %collective-permute-start.5 = (s32[256]{0:T(256)S(1)}, s32[256]{0:T(256)S(1)}, u32[]{:S(2)}, u32[]{:S(2)}) collective-permute-start(s32[256]{0:T(256)S(1)} %fusion.37), channel_id=1, source_target_pairs={{0,16},{1,17},{2,18},{3,19},{4,20},{5,21},{6,22},{7,23},{8,24},{9,... | collective-permute-start | bytes 3080 | tf_op jit(solution)/shard_map/ppermute | solution.py:64
  23.3 9.7 %collective-permute-start.8 = (s32[1024]{0:T(1024)S(1)}, s32[1024]{0:T(1024)S(1)}, u32[]{:S(2)}, u32[]{:S(2)}) collective-permute-start(s32[1024]{0:T(1024)S(1)} %bitcast.131), channel_id=1, source_target_pairs={{0,64},{1,65},{2,66},{3,67},{4,68},{5,69},{6,70},{7,71},{8,72},{9,... | collective-permute-start | bytes 12296 | tf_op jit(solution)/shard_map/ppermute | solution.py:64
  30.3 25.0 %copy-start.4 = (f32[8192]{0:T(1024)S(1)}, f32[8192]{0:T(1024)}, u32[]{:S(2)}) copy-start(f32[8192]{0:T(1024)} %param.22) | copy-start | bytes 98308
  30.3 30.4 %copy-start = (f32[3,8192]{1,0:T(4,128)S(1)}, f32[3,8192]{1,0:T(4,128)}, u32[]{:S(2)}) copy-start(f32[3,8192]{1,0:T(4,128)} %param.17) | copy-start | bytes 294916
  30.3 30.4 %copy-start.1 = (f32[3,8192]{1,0:T(4,128)S(1)}, f32[3,8192]{1,0:T(4,128)}, u32[]{:S(2)}) copy-start(f32[3,8192]{1,0:T(4,128)} %param.18) | copy-start | bytes 294916
  30.4 30.4 %copy-start.2 = (f32[3,8192]{1,0:T(4,128)S(1)}, f32[3,8192]{1,0:T(4,128)}, u32[]{:S(2)}) copy-start(f32[3,8192]{1,0:T(4,128)} %param.19) | copy-start | bytes 294916
  30.4 30.4 %copy-start.3 = (f32[3,8192]{1,0:T(4,128)S(1)}, f32[3,8192]{1,0:T(4,128)}, u32[]{:S(2)}) copy-start(f32[3,8192]{1,0:T(4,128)} %param.20) | copy-start | bytes 294916
  30.4 34.5 %copy-start.5 = (f32[8192]{0:T(1024)S(1)}, f32[8192]{0:T(1024)}, u32[]{:S(2)}) copy-start(f32[8192]{0:T(1024)} %param.21) | copy-start | bytes 98308
  42.0 5.9 %collective-permute-start.9 = (f32[6,2048]{1,0:T(8,128)S(1)}, f32[6,2048]{1,0:T(8,128)S(1)}, u32[]{:S(2)}, u32[]{:S(2)}) collective-permute-start(f32[6,2048]{1,0:T(8,128)S(1)} %pad_maximum_fusion.1), channel_id=1, source_target_pairs={{0,1},{1,0},{2,3},{3,2},{4,5},{5,4},{6,7},{7,6},{8,9},{9,8},{10,11... | collective-permute-start | bytes 147464 | tf_op jit(solution)/shard_map/ppermute | solution.py:90
  47.9 3.2 %collective-permute-start.12 = (f32[6,2048]{1,0:T(8,128)S(1)}, f32[6,2048]{1,0:T(8,128)S(1)}, u32[]{:S(2)}, u32[]{:S(2)}) collective-permute-start(f32[6,2048]{1,0:T(8,128)S(1)} %fusion.35), channel_id=1, source_target_pairs={{0,6},{1,7},{2,0},{3,1},{4,2},{5,3},{6,4},{7,5},{8,14},{9,15},{10,... | collective-permute-start | bytes 147464 | tf_op jit(solution)/shard_map/ppermute | solution.py:90
  48.0 4.7 %collective-permute-start.11 = (f32[6,2048]{1,0:T(8,128)S(1)}, f32[6,2048]{1,0:T(8,128)S(1)}, u32[]{:S(2)}, u32[]{:S(2)}) collective-permute-start(f32[6,2048]{1,0:T(8,128)S(1)} %fusion.35), channel_id=1, source_target_pairs={{0,4},{1,5},{2,6},{3,7},{4,0},{5,1},{6,2},{7,3},{8,12},{9,13},{10,... | collective-permute-start | bytes 147464 | tf_op jit(solution)/shard_map/ppermute | solution.py:90
  49.3 5.5 %collective-permute-start.10 = (f32[6,2048]{1,0:T(8,128)S(1)}, f32[6,2048]{1,0:T(8,128)S(1)}, u32[]{:S(2)}, u32[]{:S(2)}) collective-permute-start(f32[6,2048]{1,0:T(8,128)S(1)} %fusion.35), channel_id=1, source_target_pairs={{0,2},{1,3},{2,4},{3,5},{4,6},{5,7},{6,0},{7,1},{8,10},{9,11},{10,... | collective-permute-start | bytes 147464 | tf_op jit(solution)/shard_map/ppermute | solution.py:90
  54.8 3.2 %collective-permute-start.13 = (f32[6,2048]{1,0:T(8,128)S(1)}, f32[6,2048]{1,0:T(8,128)S(1)}, u32[]{:S(2)}, u32[]{:S(2)}) collective-permute-start(f32[6,2048]{1,0:T(8,128)S(1)} %add_add_fusion.1), channel_id=1, source_target_pairs={{0,8},{1,9},{2,10},{3,11},{4,12},{5,13},{6,14},{7,15},{8,0},{9,1},... | collective-permute-start | bytes 147464 | tf_op jit(solution)/shard_map/ppermute | solution.py:90
  58.0 3.2 %collective-permute-start.16 = (f32[6,2048]{1,0:T(8,128)S(1)}, f32[6,2048]{1,0:T(8,128)S(1)}, u32[]{:S(2)}, u32[]{:S(2)}) collective-permute-start(f32[6,2048]{1,0:T(8,128)S(1)} %add.420), channel_id=1, source_target_pairs={{0,48},{1,49},{2,50},{3,51},{4,52},{5,53},{6,54},{7,55},{8,56},{9,... | collective-permute-start | bytes 147464 | tf_op jit(solution)/shard_map/ppermute | solution.py:90
  58.4 4.6 %collective-permute-start.15 = (f32[6,2048]{1,0:T(8,128)S(1)}, f32[6,2048]{1,0:T(8,128)S(1)}, u32[]{:S(2)}, u32[]{:S(2)}) collective-permute-start(f32[6,2048]{1,0:T(8,128)S(1)} %add.420), channel_id=1, source_target_pairs={{0,32},{1,33},{2,34},{3,35},{4,36},{5,37},{6,38},{7,39},{8,40},{9,... | collective-permute-start | bytes 147464 | tf_op jit(solution)/shard_map/ppermute | solution.py:90
  59.9 4.3 %collective-permute-start.14 = (f32[6,2048]{1,0:T(8,128)S(1)}, f32[6,2048]{1,0:T(8,128)S(1)}, u32[]{:S(2)}, u32[]{:S(2)}) collective-permute-start(f32[6,2048]{1,0:T(8,128)S(1)} %add.420), channel_id=1, source_target_pairs={{0,16},{1,17},{2,18},{3,19},{4,20},{5,21},{6,22},{7,23},{8,24},{9,... | collective-permute-start | bytes 147464 | tf_op jit(solution)/shard_map/ppermute | solution.py:90
  64.3 4.7 %collective-permute-start.17 = (f32[6,2048]{1,0:T(8,128)S(1)}, f32[6,2048]{1,0:T(8,128)S(1)}, u32[]{:S(2)}, u32[]{:S(2)}) collective-permute-start(f32[6,2048]{1,0:T(8,128)S(1)} %add_add_fusion), channel_id=1, source_target_pairs={{0,64},{1,65},{2,66},{3,67},{4,68},{5,69},{6,70},{7,71},{8,72},{9,... | collective-permute-start | bytes 147464 | tf_op jit(solution)/shard_map/ppermute | solution.py:90
  186.4 4.7 %collective-permute-start.18 = (f32[13,1024]{1,0:T(8,128)S(1)}, f32[13,1024]{1,0:T(8,128)S(1)}, u32[]{:S(2)}, u32[]{:S(2)}) collective-permute-start(f32[13,1024]{1,0:T(8,128)S(1)} %bitcast.118), channel_id=1, source_target_pairs={{0,64},{1,65},{2,66},{3,67},{4,68},{5,69},{6,70},{7,71},{8,72},{9,... | collective-permute-start | bytes 159752 | tf_op jit(solution)/shard_map/ppermute | solution.py:82
  191.3 2.7 %collective-permute-start.21 = (f32[13,256]{1,0:T(8,128)S(1)}, f32[13,256]{1,0:T(8,128)S(1)}, u32[]{:S(2)}, u32[]{:S(2)}) collective-permute-start(f32[13,256]{1,0:T(8,128)S(1)} %bitcast.126), channel_id=1, source_target_pairs={{0,48},{1,49},{2,50},{3,51},{4,52},{5,53},{6,54},{7,55},{8,56},{9,... | collective-permute-start | bytes 39944 | tf_op jit(solution)/shard_map/ppermute | solution.py:82
  192.5 4.1 %collective-permute-start.20 = (f32[13,256]{1,0:T(8,128)S(1)}, f32[13,256]{1,0:T(8,128)S(1)}, u32[]{:S(2)}, u32[]{:S(2)}) collective-permute-start(f32[13,256]{1,0:T(8,128)S(1)} %fusion.2), channel_id=1, source_target_pairs={{0,32},{1,33},{2,34},{3,35},{4,36},{5,37},{6,38},{7,39},{8,40},{9,... | collective-permute-start | bytes 39944 | tf_op jit(solution)/shard_map/ppermute | solution.py:82
  193.1 3.8 %collective-permute-start.19 = (f32[13,256]{1,0:T(8,128)S(1)}, f32[13,256]{1,0:T(8,128)S(1)}, u32[]{:S(2)}, u32[]{:S(2)}) collective-permute-start(f32[13,256]{1,0:T(8,128)S(1)} %fusion.3), channel_id=1, source_target_pairs={{0,16},{1,17},{2,18},{3,19},{4,20},{5,21},{6,22},{7,23},{8,24},{9,... | collective-permute-start | bytes 39944 | tf_op jit(solution)/shard_map/ppermute | solution.py:82
  196.9 2.6 %collective-permute-start.22 = (f32[13,128]{1,0:T(8,128)S(1)}, f32[13,128]{1,0:T(8,128)S(1)}, u32[]{:S(2)}, u32[]{:S(2)}) collective-permute-start(f32[13,128]{1,0:T(8,128)S(1)} %bitcast.128), channel_id=1, source_target_pairs={{0,8},{1,9},{2,10},{3,11},{4,12},{5,13},{6,14},{7,15},{8,0},{9,1},... | collective-permute-start | bytes 19976 | tf_op jit(solution)/shard_map/ppermute | solution.py:82
  199.7 2.9 %collective-permute-start.25 = (f32[13,32]{1,0:T(8,128)S(1)}, f32[13,32]{1,0:T(8,128)S(1)}, u32[]{:S(2)}, u32[]{:S(2)}) collective-permute-start(f32[13,32]{1,0:T(8,128)S(1)} %bitcast.129), channel_id=1, source_target_pairs={{0,6},{1,7},{2,0},{3,1},{4,2},{5,3},{6,4},{7,5},{8,14},{9,15},{10,... | collective-permute-start | bytes 5000 | tf_op jit(solution)/shard_map/ppermute | solution.py:82
  200.5 4.0 %collective-permute-start.24 = (f32[13,32]{1,0:T(8,128)S(1)}, f32[13,32]{1,0:T(8,128)S(1)}, u32[]{:S(2)}, u32[]{:S(2)}) collective-permute-start(f32[13,32]{1,0:T(8,128)S(1)} %fusion.10), channel_id=1, source_target_pairs={{0,4},{1,5},{2,6},{3,7},{4,0},{5,1},{6,2},{7,3},{8,12},{9,13},{10,... | collective-permute-start | bytes 5000 | tf_op jit(solution)/shard_map/ppermute | solution.py:82
  201.1 3.7 %collective-permute-start.23 = (f32[13,32]{1,0:T(8,128)S(1)}, f32[13,32]{1,0:T(8,128)S(1)}, u32[]{:S(2)}, u32[]{:S(2)}) collective-permute-start(f32[13,32]{1,0:T(8,128)S(1)} %fusion.11), channel_id=1, source_target_pairs={{0,2},{1,3},{2,4},{3,5},{4,6},{5,7},{6,0},{7,1},{8,10},{9,11},{10,... | collective-permute-start | bytes 5000 | tf_op jit(solution)/shard_map/ppermute | solution.py:82
  205.0 11.8 %collective-permute-start.26 = (f32[13,16]{1,0:T(8,128)S(1)}, f32[13,16]{1,0:T(8,128)S(1)}, u32[]{:S(2)}, u32[]{:S(2)}) collective-permute-start(f32[13,16]{1,0:T(8,128)S(1)} %bitcast.130), channel_id=1, source_target_pairs={{0,1},{1,0},{2,3},{3,2},{4,5},{5,4},{6,7},{7,6},{8,9},{9,8},{10,11... | collective-permute-start | bytes 2504 | tf_op jit(solution)/shard_map/ppermute | solution.py:82

commit v10 on v9

--- a/solution.py
+++ b/solution.py
@@ -1,11 +1,9 @@
-import functools
-
 import jax
 import jax.numpy as jnp
 from jax import lax
 from jax.experimental import pallas as pl
-from jax.experimental.pallas import tpu as pltpu
 from jax.sharding import PartitionSpec as P
+
 
 softening = 0.001
 ALL = ("blk", "group")
@@ -150,7 +148,7 @@
     )(active_t, field_b)
 
 
-def on_device(positions, velocities, accelerations, jerk_rates, masses, elapsed_time, active_index):
+def step(positions, velocities, accelerations, jerk_rates, masses, elapsed_time, active_index):
     ndev = lax.axis_size("blk") * lax.axis_size("group")
     own_stars = positions.shape[1]
     total_stars = own_stars * ndev
@@ -177,16 +175,28 @@
     for level in LEVELS:
         active = sum_level(active, level, ndev)
     active_t = jnp.concatenate([active, jnp.zeros((2, num_k), jnp.float32)], axis=0).T
-    partial = jnp.sum(pair_forces(active_t, field_b), axis=2)
-    payload = jnp.concatenate([partial, corrector_terms(picked)], axis=0)
-    for level in reversed(LEVELS):
+    terms = corrector_terms(picked)
+    _, stride, size = LEVELS[-1]
+    half = num_k // size
+    upper = _coord(stride, size)
+    send_at = ((upper + 1) % size) * half
+    keep_at = upper * half
+
+    def half_payload(start):
+        act = lax.dynamic_slice_in_dim(active_t, start, half, axis=0)
+        part = jnp.sum(pair_forces(act, field_b), axis=2)
+        return jnp.concatenate([part, lax.dynamic_slice_in_dim(terms, start, half, axis=1)], axis=0)
+
+    sent = lax.ppermute(half_payload(send_at), ALL, _perm(stride, size, 1, ndev))
+    payload = half_payload(keep_at) + sent
+    for level in reversed(LEVELS[:-1]):
         payload = reduce_level(payload, level, ndev)
     return corrector(payload[6:13], payload[0:6] * gravity)
 
 
 def solution(mesh):
     return jax.shard_map(
-        on_device,
+        step,
         mesh=mesh,
         in_specs=(
             P(None, ALL),

time: 218 us -> 215 us (0.986)
  waiting for transfers between devices: 37 us -> 32.7 us
    ppermute x9 -> x8, waiting for transfers between devices: 13.8 us -> 9.56 us  [reduce_level(): total = total + lax.ppermute(piece, ALL, _perm(stride, size, s, ndev))]
    pallas_call x1 -> x2, Pallas kernels: 110 us -> 112 us  [pair_forces(): pl.pallas_call(forces_kernel, out_shape=jax.ShapeDtypeStruct((6, num_k, 1...]
    ppermute x9 -> x8, starting transfers between devices: 16 us -> 14.4 us  [reduce_level(): total = total + lax.ppermute(piece, ALL, _perm(stride, size, s, ndev))]
    reduce_sum x1 -> x2, other arithmetic: 4.48 us -> 5.54 us  [half_payload(): part = jnp.sum(pair_forces(act, field_b), axis=2)]
  transfers between devices with their start and end apart: 27 -> 27, of which waited for: 23 -> 22; matrix products, arithmetic and copies ran while one was open for 4% -> 5% of each run, Pallas kernels for 0% -> 26%
where the time goes in v10:
time: 215 us
  Pallas kernels  112 us (52%)
  starting transfers between devices  39.7 us (18%)
  waiting for transfers between devices  32.7 us (15%)
  local copies, waits for them, and re-layouts  21.4 us (10%)
  other arithmetic  8.19 us (4%)
    pallas_call x2, Pallas kernels, pair_forces(): pl.pallas_call(forces_kernel, out_shape=jax.ShapeDtypeStruct((6, num_k, 1...  112 us
    ppermute x9, waiting for transfers between devices, sum_level(): total = total + lax.ppermute(x, ALL, _perm(stride, size, s, ndev))  15.3 us
    ppermute x8, starting transfers between devices, reduce_level(): total = total + lax.ppermute(piece, ALL, _perm(stride, size, s, ndev))  14.4 us
    ppermute x9, starting transfers between devices, gather_level(): lax.ppermute(x, ALL, _perm(stride, size, s, ndev))  13.9 us
    ppermute x9, starting transfers between devices, sum_level(): total = total + lax.ppermute(x, ALL, _perm(stride, size, s, ndev))  10.9 us
    ppermute x8, waiting for transfers between devices, reduce_level(): total = total + lax.ppermute(piece, ALL, _perm(stride, size, s, ndev))  9.56 us
    gather x2, local copies, waits for them, and re-layouts, step(): picked = jnp.take(packed, jnp.clip(local_row, 0, own_stars - 1), axis=1)  7.98 us
    ppermute x9, waiting for transfers between devices, gather_level(): lax.ppermute(x, ALL, _perm(stride, size, s, ndev))  7.85 us
  transfers between devices with their start and end apart: 27, of which 22 were waited for; matrix products, arithmetic and copies ran while one was open for 5% of the time, Pallas kernels for 26%

profile of v10, /device:TPU:1, one launch (start us, length us, event | category | flops | bytes accessed | tf_op | source)
XLA Modules:
  0.0 215.1 jit_solution(8999921797930710677)
XLA Ops:
  0.6 1.5 collective-permute-start
  2.3 0.7 collective-permute-done
  3.0 0.7 pad_add_fusion.3
  4.4 2.6 %collective-permute-start.3 = (s32[32]{0:T(128)S(1)}, s32[32]{0:T(128)S(1)}, u32[]{:S(2)}, u32[]{:S(2)}) collective-permute-start(s32[32]{0:T(128)S(1)} %select_n.415), channel_id=1, source_target_pairs={{0,6},{1,7},{2,0},{3,1},{4,2},{5,3},{6,4},{7,5},{8,14},{9,15},{10,... | collective-permute-start | bytes 392 | tf_op jit(solution)/shard_map/ppermute | solution.py:62
  7.5 0.6 collective-permute-start.1
  8.2 2.7 %collective-permute-done.2 = s32[32]{0:T(128)S(1)} collective-permute-done((s32[32]{0:T(128)S(1)}, s32[32]{0:T(128)S(1)}, u32[]{:S(2)}, u32[]{:S(2)}) %collective-permute-start.2) | collective-permute-done | bytes 160 | tf_op jit(solution)/shard_map/ppermute | solution.py:62
  11.9 1.3 collective-permute-start.4
  13.3 1.0 collective-permute-done.4
  15.0 3.8 %collective-permute-start.7 = (s32[256]{0:T(256)S(1)}, s32[256]{0:T(256)S(1)}, u32[]{:S(2)}, u32[]{:S(2)}) collective-permute-start(s32[256]{0:T(256)S(1)} %fusion.33), channel_id=1, source_target_pairs={{0,48},{1,49},{2,50},{3,51},{4,52},{5,53},{6,54},{7,55},{8,56},{9,... | collective-permute-start | bytes 3080 | tf_op jit(solution)/shard_map/ppermute | solution.py:62
  18.7 0.7 collective-permute-start.5
  19.5 3.2 %collective-permute-done.6 = s32[256]{0:T(256)S(1)} collective-permute-done((s32[256]{0:T(256)S(1)}, s32[256]{0:T(256)S(1)}, u32[]{:S(2)}, u32[]{:S(2)}) %collective-permute-start.6) | collective-permute-done | bytes 1056 | tf_op jit(solution)/shard_map/ppermute | solution.py:62
  23.3 2.9 %collective-permute-start.8 = (s32[1024]{0:T(1024)S(1)}, s32[1024]{0:T(1024)S(1)}, u32[]{:S(2)}, u32[]{:S(2)}) collective-permute-start(s32[1024]{0:T(1024)S(1)} %bitcast.122), channel_id=1, source_target_pairs={{0,64},{1,65},{2,66},{3,67},{4,68},{5,69},{6,70},{7,71},{8,72},{9,... | collective-permute-start | bytes 12296 | tf_op jit(solution)/shard_map/ppermute | solution.py:62
  26.3 4.0 %concatenate.21 = f32[13,8192]{1,0:T(8,128)S(1)} concatenate(f32[3,8192]{1,0:T(4,128)} %param.15, f32[3,8192]{1,0:T(4,128)} %param.16, f32[3,8192]{1,0:T(4,128)} %param.17, f32[3,8192]{1,0:T(4,128)} %param.18, f32[1,8192]{1,0:T(1,128)} %bitcast.105), dimensions={0} | concatenate | bytes 851968 | tf_op jit(solution)/shard_map/concatenate | solution.py:164
  30.4 2.7 %copy.79 = f32[13,8192]{0,1:T(8,128)} copy(f32[13,8192]{1,0:T(8,128)S(1)} %concatenate.21) | data formatting | bytes 851968 | tf_op jit(solution)/shard_map/concatenate | solution.py:164
  33.8 7.6 %gather_fusion.5 = f32[2048,13]{1,0:T(8,128)S(1)} fusion(f32[13,8192]{0,1:T(8,128)} %copy.79, s32[2048]{0:T(1024)S(1)} %broadcast_clamp_fusion), kind=kCustom, calls=%fused_computation.5 | custom fusion | bytes 221184 | tf_op jit(solution)/shard_map/jit(_take)/gather | solution.py:170
  42.0 5.0 %collective-permute-start.9 = (f32[6,2048]{1,0:T(8,128)S(1)}, f32[6,2048]{1,0:T(8,128)S(1)}, u32[]{:S(2)}, u32[]{:S(2)}) collective-permute-start(f32[6,2048]{1,0:T(8,128)S(1)} %pad_maximum_fusion), channel_id=1, source_target_pairs={{0,1},{1,0},{2,3},{3,2},{4,5},{5,4},{6,7},{7,6},{8,9},{9,8},{10,11... | collective-permute-start | bytes 147464 | tf_op jit(solution)/shard_map/ppermute | solution.py:88
  47.0 0.9 collective-permute-done.9
  48.0 1.3 collective-permute-start.11
  49.3 0.8 collective-permute-start.10
  50.3 0.8 collective-permute-done.12
  51.1 1.6 collective-permute-done.11
  52.7 2.1 collective-permute-done.10
  55.4 2.6 %collective-permute-done.13 = f32[6,2048]{1,0:T(8,128)S(1)} collective-permute-done((f32[6,2048]{1,0:T(8,128)S(1)}, f32[6,2048]{1,0:T(8,128)S(1)}, u32[]{:S(2)}, u32[]{:S(2)}) %collective-permute-start.13) | collective-permute-done | bytes 49184 | tf_op jit(solution)/shard_map/ppermute | solution.py:88
  58.4 1.6 collective-permute-start.15
  59.9 0.8 collective-permute-start.14
  61.2 1.8 collective-permute-done.15
  63.0 1.3 collective-permute-done.14
  65.2 3.8 %collective-permute-done.17 = f32[6,2048]{1,0:T(8,128)S(1)} collective-permute-done((f32[6,2048]{1,0:T(8,128)S(1)}, f32[6,2048]{1,0:T(8,128)S(1)}, u32[]{:S(2)}, u32[]{:S(2)}) %collective-permute-start.17) | collective-permute-done | bytes 49184 | tf_op jit(solution)/shard_map/ppermute | solution.py:88
  69.5 1.1 fusion
  70.6 1.5 broadcast_in_dim.151.fld_ref
  72.0 55.9 %shard_map.103 = f32[6,1024,128]{2,1,0:T(8,128)} custom-call(f32[1024,8]{1,0:T(8,128)} %get-tuple-element.59.act_ref, f32[8,8,8192]{2,1,0:T(8,128)} %broadcast_in_dim.151.fld_ref), custom_call_target="tpu_custom_call" | custom-call | tf_op jit(solution)/shard_map/pallas_call | solution.py:145
  127.9 2.8 %reduce_sum.19 = f32[6,1024]{1,0:T(8,128)S(1)} reduce(f32[6,1024,128]{2,1,0:T(8,128)} %shard_map.103, f32[]{:T(128)} %constant.337.clone.1), dimensions={2}, to_apply=%region_1.2 | reduce | flops 780288 | bytes 3170308 | tf_op jit(solution)/shard_map/reduce_sum | solution.py:187
  131.3 55.9 %shard_map.102 = f32[6,1024,128]{2,1,0:T(8,128)} custom-call(f32[1024,8]{1,0:T(8,128)} %get-tuple-element.58.act_ref, f32[8,8,8192]{2,1,0:T(8,128)} %broadcast_in_dim.151.fld_ref), custom_call_target="tpu_custom_call" | custom-call | tf_op jit(solution)/shard_map/pallas_call | solution.py:145
  187.2 2.8 %reduce_sum.18 = f32[6,1024]{1,0:T(8,128)S(1)} reduce(f32[6,1024,128]{2,1,0:T(8,128)} %shard_map.102, f32[]{:T(128)} %constant.337.clone.1), dimensions={2}, to_apply=%region_0.1 | reduce | flops 780288 | bytes 3170308 | tf_op jit(solution)/shard_map/reduce_sum | solution.py:187
  190.1 1.2 collective-permute-start.21
  191.3 0.9 collective-permute-start.20
  192.8 2.6 %collective-permute-done.20 = f32[13,256]{1,0:T(8,128)S(1)} collective-permute-done((f32[13,256]{1,0:T(8,128)S(1)}, f32[13,256]{1,0:T(8,128)S(1)}, u32[]{:S(2)}, u32[]{:S(2)}) %collective-permute-start.20) | collective-permute-done | bytes 13344 | tf_op jit(solution)/shard_map/ppermute | solution.py:80
  195.4 0.6 collective-permute-done.19
  196.1 0.7 collective-permute-start.22
  196.7 1.9 collective-permute-done.22
  199.1 0.8 collective-permute-start.24
  199.9 0.8 collective-permute-start.23
  200.7 1.0 collective-permute-done.25
  201.6 1.5 collective-permute-done.24
  203.1 0.6 collective-permute-done.23
  203.9 9.7 %collective-permute-start.26 = (f32[13,16]{1,0:T(8,128)S(1)}, f32[13,16]{1,0:T(8,128)S(1)}, u32[]{:S(2)}, u32[]{:S(2)}) collective-permute-start(f32[13,16]{1,0:T(8,128)S(1)} %bitcast.121), channel_id=1, source_target_pairs={{0,1},{1,0},{2,3},{3,2},{4,5},{5,4},{6,7},{7,6},{8,9},{9,8},{10,11... | collective-permute-start | bytes 2504 | tf_op jit(solution)/shard_map/ppermute | solution.py:80
  213.6 0.8 collective-permute-done.26
  214.5 0.6 fusion.15
  (111 shorter events, 10.2 us)
Async XLA Ops:
  0.6 2.4 %collective-permute-start = (s32[16]{0:T(128)}, s32[16]{0:T(128)S(1)}, u32[]{:S(2)}, u32[]{:S(2)}) collective-permute-start(s32[16]{0:T(128)} %param.21), channel_id=1, source_target_pairs={{0,1},{1,0},{2,3},{3,2},{4,5},{5,4},{6,7},{7,6},{8,9},{9,8},{10,11... | collective-permute-start | bytes 200 | tf_op jit(solution)/shard_map/ppermute | solution.py:62
  4.4 3.8 %collective-permute-start.3 = (s32[32]{0:T(128)S(1)}, s32[32]{0:T(128)S(1)}, u32[]{:S(2)}, u32[]{:S(2)}) collective-permute-start(s32[32]{0:T(128)S(1)} %select_n.415), channel_id=1, source_target_pairs={{0,6},{1,7},{2,0},{3,1},{4,2},{5,3},{6,4},{7,5},{8,14},{9,15},{10,... | collective-permute-start | bytes 392 | tf_op jit(solution)/shard_map/ppermute | solution.py:62
  7.0 3.9 %collective-permute-start.2 = (s32[32]{0:T(128)S(1)}, s32[32]{0:T(128)S(1)}, u32[]{:S(2)}, u32[]{:S(2)}) collective-permute-start(s32[32]{0:T(128)S(1)} %select_n.415), channel_id=1, source_target_pairs={{0,4},{1,5},{2,6},{3,7},{4,0},{5,1},{6,2},{7,3},{8,12},{9,13},{10,... | collective-permute-start | bytes 392 | tf_op jit(solution)/shard_map/ppermute | solution.py:62
  7.5 3.6 %collective-permute-start.1 = (s32[32]{0:T(128)S(1)}, s32[32]{0:T(128)S(1)}, u32[]{:S(2)}, u32[]{:S(2)}) collective-permute-start(s32[32]{0:T(128)S(1)} %select_n.415), channel_id=1, source_target_pairs={{0,2},{1,3},{2,4},{3,5},{4,6},{5,7},{6,0},{7,1},{8,10},{9,11},{10,... | collective-permute-start | bytes 392 | tf_op jit(solution)/shard_map/ppermute | solution.py:62
  11.9 2.4 %collective-permute-start.4 = (s32[128]{0:T(128)S(1)}, s32[128]{0:T(128)S(1)}, u32[]{:S(2)}, u32[]{:S(2)}) collective-permute-start(s32[128]{0:T(128)S(1)} %select_n.420), channel_id=1, source_target_pairs={{0,8},{1,9},{2,10},{3,11},{4,12},{5,13},{6,14},{7,15},{8,0},{9,1},... | collective-permute-start | bytes 1544 | tf_op jit(solution)/shard_map/ppermute | solution.py:62
  15.0 4.5 %collective-permute-start.7 = (s32[256]{0:T(256)S(1)}, s32[256]{0:T(256)S(1)}, u32[]{:S(2)}, u32[]{:S(2)}) collective-permute-start(s32[256]{0:T(256)S(1)} %fusion.33), channel_id=1, source_target_pairs={{0,48},{1,49},{2,50},{3,51},{4,52},{5,53},{6,54},{7,55},{8,56},{9,... | collective-permute-start | bytes 3080 | tf_op jit(solution)/shard_map/ppermute | solution.py:62
  18.7 3.9 %collective-permute-start.6 = (s32[256]{0:T(256)S(1)}, s32[256]{0:T(256)S(1)}, u32[]{:S(2)}, u32[]{:S(2)}) collective-permute-start(s32[256]{0:T(256)S(1)} %fusion.33), channel_id=1, source_target_pairs={{0,32},{1,33},{2,34},{3,35},{4,36},{5,37},{6,38},{7,39},{8,40},{9,... | collective-permute-start | bytes 3080 | tf_op jit(solution)/shard_map/ppermute | solution.py:62
  18.7 3.9 %collective-permute-start.5 = (s32[256]{0:T(256)S(1)}, s32[256]{0:T(256)S(1)}, u32[]{:S(2)}, u32[]{:S(2)}) collective-permute-start(s32[256]{0:T(256)S(1)} %fusion.33), channel_id=1, source_target_pairs={{0,16},{1,17},{2,18},{3,19},{4,20},{5,21},{6,22},{7,23},{8,24},{9,... | collective-permute-start | bytes 3080 | tf_op jit(solution)/shard_map/ppermute | solution.py:62
  23.3 9.7 %collective-permute-start.8 = (s32[1024]{0:T(1024)S(1)}, s32[1024]{0:T(1024)S(1)}, u32[]{:S(2)}, u32[]{:S(2)}) collective-permute-start(s32[1024]{0:T(1024)S(1)} %bitcast.122), channel_id=1, source_target_pairs={{0,64},{1,65},{2,66},{3,67},{4,68},{5,69},{6,70},{7,71},{8,72},{9,... | collective-permute-start | bytes 12296 | tf_op jit(solution)/shard_map/ppermute | solution.py:62
  30.3 16.7 %copy-start.4 = (f32[8192]{0:T(1024)S(1)}, f32[8192]{0:T(1024)}, u32[]{:S(2)}) copy-start(f32[8192]{0:T(1024)} %param.20) | copy-start | bytes 98308
  30.3 19.7 %copy-start = (f32[3,8192]{1,0:T(4,128)S(1)}, f32[3,8192]{1,0:T(4,128)}, u32[]{:S(2)}) copy-start(f32[3,8192]{1,0:T(4,128)} %param.15) | copy-start | bytes 294916
  30.3 19.7 %copy-start.1 = (f32[3,8192]{1,0:T(4,128)S(1)}, f32[3,8192]{1,0:T(4,128)}, u32[]{:S(2)}) copy-start(f32[3,8192]{1,0:T(4,128)} %param.16) | copy-start | bytes 294916
  30.4 19.7 %copy-start.2 = (f32[3,8192]{1,0:T(4,128)S(1)}, f32[3,8192]{1,0:T(4,128)}, u32[]{:S(2)}) copy-start(f32[3,8192]{1,0:T(4,128)} %param.17) | copy-start | bytes 294916
  30.4 19.7 %copy-start.3 = (f32[3,8192]{1,0:T(4,128)S(1)}, f32[3,8192]{1,0:T(4,128)}, u32[]{:S(2)}) copy-start(f32[3,8192]{1,0:T(4,128)} %param.18) | copy-start | bytes 294916
  33.0 22.3 %copy-start.5 = (f32[8192]{0:T(1024)S(1)}, f32[8192]{0:T(1024)}, u32[]{:S(2)}) copy-start(f32[8192]{0:T(1024)} %param.19) | copy-start | bytes 98308
  42.0 5.9 %collective-permute-start.9 = (f32[6,2048]{1,0:T(8,128)S(1)}, f32[6,2048]{1,0:T(8,128)S(1)}, u32[]{:S(2)}, u32[]{:S(2)}) collective-permute-start(f32[6,2048]{1,0:T(8,128)S(1)} %pad_maximum_fusion), channel_id=1, source_target_pairs={{0,1},{1,0},{2,3},{3,2},{4,5},{5,4},{6,7},{7,6},{8,9},{9,8},{10,11... | collective-permute-start | bytes 147464 | tf_op jit(solution)/shard_map/ppermute | solution.py:88
  47.9 3.2 %collective-permute-start.12 = (f32[6,2048]{1,0:T(8,128)S(1)}, f32[6,2048]{1,0:T(8,128)S(1)}, u32[]{:S(2)}, u32[]{:S(2)}) collective-permute-start(f32[6,2048]{1,0:T(8,128)S(1)} %fusion.31), channel_id=1, source_target_pairs={{0,6},{1,7},{2,0},{3,1},{4,2},{5,3},{6,4},{7,5},{8,14},{9,15},{10,... | collective-permute-start | bytes 147464 | tf_op jit(solution)/shard_map/ppermute | solution.py:88
  48.0 4.7 %collective-permute-start.11 = (f32[6,2048]{1,0:T(8,128)S(1)}, f32[6,2048]{1,0:T(8,128)S(1)}, u32[]{:S(2)}, u32[]{:S(2)}) collective-permute-start(f32[6,2048]{1,0:T(8,128)S(1)} %fusion.31), channel_id=1, source_target_pairs={{0,4},{1,5},{2,6},{3,7},{4,0},{5,1},{6,2},{7,3},{8,12},{9,13},{10,... | collective-permute-start | bytes 147464 | tf_op jit(solution)/shard_map/ppermute | solution.py:88
  49.3 5.5 %collective-permute-start.10 = (f32[6,2048]{1,0:T(8,128)S(1)}, f32[6,2048]{1,0:T(8,128)S(1)}, u32[]{:S(2)}, u32[]{:S(2)}) collective-permute-start(f32[6,2048]{1,0:T(8,128)S(1)} %fusion.31), channel_id=1, source_target_pairs={{0,2},{1,3},{2,4},{3,5},{4,6},{5,7},{6,0},{7,1},{8,10},{9,11},{10,... | collective-permute-start | bytes 147464 | tf_op jit(solution)/shard_map/ppermute | solution.py:88
  54.8 3.2 %collective-permute-start.13 = (f32[6,2048]{1,0:T(8,128)S(1)}, f32[6,2048]{1,0:T(8,128)S(1)}, u32[]{:S(2)}, u32[]{:S(2)}) collective-permute-start(f32[6,2048]{1,0:T(8,128)S(1)} %add_add_fusion.1), channel_id=1, source_target_pairs={{0,8},{1,9},{2,10},{3,11},{4,12},{5,13},{6,14},{7,15},{8,0},{9,1},... | collective-permute-start | bytes 147464 | tf_op jit(solution)/shard_map/ppermute | solution.py:88
  58.0 3.2 %collective-permute-start.16 = (f32[6,2048]{1,0:T(8,128)S(1)}, f32[6,2048]{1,0:T(8,128)S(1)}, u32[]{:S(2)}, u32[]{:S(2)}) collective-permute-start(f32[6,2048]{1,0:T(8,128)S(1)} %add.425), channel_id=1, source_target_pairs={{0,48},{1,49},{2,50},{3,51},{4,52},{5,53},{6,54},{7,55},{8,56},{9,... | collective-permute-start | bytes 147464 | tf_op jit(solution)/shard_map/ppermute | solution.py:88
  58.4 4.6 %collective-permute-start.15 = (f32[6,2048]{1,0:T(8,128)S(1)}, f32[6,2048]{1,0:T(8,128)S(1)}, u32[]{:S(2)}, u32[]{:S(2)}) collective-permute-start(f32[6,2048]{1,0:T(8,128)S(1)} %add.425), channel_id=1, source_target_pairs={{0,32},{1,33},{2,34},{3,35},{4,36},{5,37},{6,38},{7,39},{8,40},{9,... | collective-permute-start | bytes 147464 | tf_op jit(solution)/shard_map/ppermute | solution.py:88
  59.9 4.3 %collective-permute-start.14 = (f32[6,2048]{1,0:T(8,128)S(1)}, f32[6,2048]{1,0:T(8,128)S(1)}, u32[]{:S(2)}, u32[]{:S(2)}) collective-permute-start(f32[6,2048]{1,0:T(8,128)S(1)} %add.425), channel_id=1, source_target_pairs={{0,16},{1,17},{2,18},{3,19},{4,20},{5,21},{6,22},{7,23},{8,24},{9,... | collective-permute-start | bytes 147464 | tf_op jit(solution)/shard_map/ppermute | solution.py:88
  64.3 4.7 %collective-permute-start.17 = (f32[6,2048]{1,0:T(8,128)S(1)}, f32[6,2048]{1,0:T(8,128)S(1)}, u32[]{:S(2)}, u32[]{:S(2)}) collective-permute-start(f32[6,2048]{1,0:T(8,128)S(1)} %add_add_fusion), channel_id=1, source_target_pairs={{0,64},{1,65},{2,66},{3,67},{4,68},{5,69},{6,70},{7,71},{8,72},{9,... | collective-permute-start | bytes 147464 | tf_op jit(solution)/shard_map/ppermute | solution.py:88
  130.7 59.3 %collective-permute-start.18 = (f32[13,1024]{1,0:T(8,128)S(1)}, f32[13,1024]{1,0:T(8,128)S(1)}, u32[]{:S(2)}, u32[]{:S(2)}) collective-permute-start(f32[13,1024]{1,0:T(8,128)S(1)} %pad_maximum_fusion.2), channel_id=1, source_target_pairs={{0,64},{1,65},{2,66},{3,67},{4,68},{5,69},{6,70},{7,71},{8,72},{9,... | collective-permute-start | bytes 159752 | tf_op jit(solution)/shard_map/ppermute | solution.py:190
  190.1 2.7 %collective-permute-start.21 = (f32[13,256]{1,0:T(8,128)S(1)}, f32[13,256]{1,0:T(8,128)S(1)}, u32[]{:S(2)}, u32[]{:S(2)}) collective-permute-start(f32[13,256]{1,0:T(8,128)S(1)} %get-tuple-element.72), channel_id=1, source_target_pairs={{0,48},{1,49},{2,50},{3,51},{4,52},{5,53},{6,54},{7,55},{8,56},{9,... | collective-permute-start | bytes 39944 | tf_op jit(solution)/shard_map/ppermute | solution.py:80
  191.3 4.1 %collective-permute-start.20 = (f32[13,256]{1,0:T(8,128)S(1)}, f32[13,256]{1,0:T(8,128)S(1)}, u32[]{:S(2)}, u32[]{:S(2)}) collective-permute-start(f32[13,256]{1,0:T(8,128)S(1)} %get-tuple-element.73), channel_id=1, source_target_pairs={{0,32},{1,33},{2,34},{3,35},{4,36},{5,37},{6,38},{7,39},{8,40},{9,... | collective-permute-start | bytes 39944 | tf_op jit(solution)/shard_map/ppermute | solution.py:80
  192.2 3.8 %collective-permute-start.19 = (f32[13,256]{1,0:T(8,128)S(1)}, f32[13,256]{1,0:T(8,128)S(1)}, u32[]{:S(2)}, u32[]{:S(2)}) collective-permute-start(f32[13,256]{1,0:T(8,128)S(1)} %get-tuple-element.71), channel_id=1, source_target_pairs={{0,16},{1,17},{2,18},{3,19},{4,20},{5,21},{6,22},{7,23},{8,24},{9,... | collective-permute-start | bytes 39944 | tf_op jit(solution)/shard_map/ppermute | solution.py:80
  196.1 2.6 %collective-permute-start.22 = (f32[13,128]{1,0:T(8,128)S(1)}, f32[13,128]{1,0:T(8,128)S(1)}, u32[]{:S(2)}, u32[]{:S(2)}) collective-permute-start(f32[13,128]{1,0:T(8,128)S(1)} %bitcast.119), channel_id=1, source_target_pairs={{0,8},{1,9},{2,10},{3,11},{4,12},{5,13},{6,14},{7,15},{8,0},{9,1},... | collective-permute-start | bytes 19976 | tf_op jit(solution)/shard_map/ppermute | solution.py:80
  198.8 2.9 %collective-permute-start.25 = (f32[13,32]{1,0:T(8,128)S(1)}, f32[13,32]{1,0:T(8,128)S(1)}, u32[]{:S(2)}, u32[]{:S(2)}) collective-permute-start(f32[13,32]{1,0:T(8,128)S(1)} %bitcast.120), channel_id=1, source_target_pairs={{0,6},{1,7},{2,0},{3,1},{4,2},{5,3},{6,4},{7,5},{8,14},{9,15},{10,... | collective-permute-start | bytes 5000 | tf_op jit(solution)/shard_map/ppermute | solution.py:80
  199.1 4.0 %collective-permute-start.24 = (f32[13,32]{1,0:T(8,128)S(1)}, f32[13,32]{1,0:T(8,128)S(1)}, u32[]{:S(2)}, u32[]{:S(2)}) collective-permute-start(f32[13,32]{1,0:T(8,128)S(1)} %fusion.6), channel_id=1, source_target_pairs={{0,4},{1,5},{2,6},{3,7},{4,0},{5,1},{6,2},{7,3},{8,12},{9,13},{10,... | collective-permute-start | bytes 5000 | tf_op jit(solution)/shard_map/ppermute | solution.py:80
  199.9 3.8 %collective-permute-start.23 = (f32[13,32]{1,0:T(8,128)S(1)}, f32[13,32]{1,0:T(8,128)S(1)}, u32[]{:S(2)}, u32[]{:S(2)}) collective-permute-start(f32[13,32]{1,0:T(8,128)S(1)} %fusion.7), channel_id=1, source_target_pairs={{0,2},{1,3},{2,4},{3,5},{4,6},{5,7},{6,0},{7,1},{8,10},{9,11},{10,... | collective-permute-start | bytes 5000 | tf_op jit(solution)/shard_map/ppermute | solution.py:80
  203.9 10.6 %collective-permute-start.26 = (f32[13,16]{1,0:T(8,128)S(1)}, f32[13,16]{1,0:T(8,128)S(1)}, u32[]{:S(2)}, u32[]{:S(2)}) collective-permute-start(f32[13,16]{1,0:T(8,128)S(1)} %bitcast.121), channel_id=1, source_target_pairs={{0,1},{1,0},{2,3},{3,2},{4,5},{5,4},{6,7},{7,6},{8,9},{9,8},{10,11... | collective-permute-start | bytes 2504 | tf_op jit(solution)/shard_map/ppermute | solution.py:80

commit v11 on v9

--- a/solution.py
+++ b/solution.py
@@ -1,11 +1,9 @@
-import functools
-
 import jax
 import jax.numpy as jnp
 from jax import lax
 from jax.experimental import pallas as pl
-from jax.experimental.pallas import tpu as pltpu
 from jax.sharding import PartitionSpec as P
+
 
 softening = 0.001
 ALL = ("blk", "group")
@@ -133,7 +131,7 @@
 
         zero = jnp.zeros((8, 128), jnp.float32)
         init = tuple(tuple(zero for _ in range(6)) for _ in range(SUB))
-        accs = lax.fori_loop(0, num_j // 128, jstep, init, unroll=16)
+        accs = lax.fori_loop(0, num_j // 128, jstep, init, unroll=32)
         for s in range(SUB):
             for c in range(6):
                 out_ref[c, pl.ds(k0 + 8 * s, 8), :] = accs[s][c]
@@ -150,14 +148,16 @@
     )(active_t, field_b)
 
 
-def on_device(positions, velocities, accelerations, jerk_rates, masses, elapsed_time, active_index):
+def step(positions, velocities, accelerations, jerk_rates, masses, elapsed_time, active_index):
     ndev = lax.axis_size("blk") * lax.axis_size("group")
     own_stars = positions.shape[1]
     total_stars = own_stars * ndev
     gravity = 1.0 / total_stars
     every_index = active_index
-    for level in LEVELS:
+    for level in LEVELS[:-1]:
         every_index = gather_level(every_index, level, ndev)
+    _, last_stride, last_size = LEVELS[-1]
+    other_index = lax.ppermute(every_index, ALL, _perm(last_stride, last_size, 1, ndev))
     pred_pos, pred_vel = predict(positions, velocities, accelerations, jerk_rates, elapsed_time)
     own_field = jnp.concatenate(
         [pred_pos, pred_vel, masses[None, :], jnp.zeros_like(masses)[None, :]], axis=0
@@ -167,10 +167,20 @@
         [positions, velocities, accelerations, jerk_rates, elapsed_time[None, :]], axis=0
     )
     first_row = lax.axis_index(ALL) * own_stars
-    local_row = every_index - first_row
-    is_owned = (local_row >= 0) & (local_row < own_stars)
-    picked = jnp.take(packed, jnp.clip(local_row, 0, own_stars - 1), axis=1)
-    picked = jnp.where(is_owned[None, :], picked, 0.0)
+
+    def pick(index):
+        local_row = index - first_row
+        is_owned = (local_row >= 0) & (local_row < own_stars)
+        rows = jnp.take(packed, jnp.clip(local_row, 0, own_stars - 1), axis=1)
+        return jnp.where(is_owned[None, :], rows, 0.0)
+
+    own_half = pick(every_index)
+    other_half = pick(other_index)
+    picked = jnp.where(
+        _coord(last_stride, last_size) == 1,
+        jnp.concatenate([other_half, own_half], axis=1),
+        jnp.concatenate([own_half, other_half], axis=1),
+    )
     act_pos, act_vel = predict(picked[0:3], picked[3:6], picked[6:9], picked[9:12], picked[12])
     num_k = picked.shape[1]
     active = jnp.concatenate([act_pos, act_vel], axis=0)
@@ -186,7 +196,7 @@
 
 def solution(mesh):
     return jax.shard_map(
-        on_device,
+        step,
         mesh=mesh,
         in_specs=(
             P(None, ALL),

time: 218 us -> 217 us (level)
    ppermute x9 -> x8, starting transfers between devices: 13.9 us -> 10.9 us  [gather_level(): lax.ppermute(x, ALL, _perm(stride, size, s, ndev))]
    ppermute x0 -> x1, starting transfers between devices: none -> 2.7 us  [step(): lax.ppermute(every_index, ALL, _perm(last_stride, last_size, 1, ndev))]
    ppermute x9 -> x8, waiting for transfers between devices: 7.85 us -> 6.84 us  [gather_level(): lax.ppermute(x, ALL, _perm(stride, size, s, ndev))]
  transfers between devices with their start and end apart: 27 -> 27, of which waited for: 23 -> 22; matrix products, arithmetic and copies ran while one was open for 4% -> 6% of each run, Pallas kernels for 0% -> 0%
where the time goes in v11:
time: 217 us; the launch traced here: 216 us
  Pallas kernels  108 us (50%)
  starting transfers between devices  38.9 us (18%)
  waiting for transfers between devices  36.9 us (17%)
  local copies, waits for them, and re-layouts  23.3 us (11%)
  other arithmetic  7.83 us (4%)
    pallas_call x1, Pallas kernels, pair_forces(): pl.pallas_call(forces_kernel, out_shape=jax.ShapeDtypeStruct((6, num_k, 1...  108 us
    ppermute x9, waiting for transfers between devices, sum_level(): total = total + lax.ppermute(x, ALL, _perm(stride, size, s, ndev))  15.8 us
    ppermute x9, starting transfers between devices, reduce_level(): total = total + lax.ppermute(piece, ALL, _perm(stride, size, s, ndev))  15.8 us
    ppermute x9, waiting for transfers between devices, reduce_level(): total = total + lax.ppermute(piece, ALL, _perm(stride, size, s, ndev))  14.2 us
    ppermute x8, starting transfers between devices, gather_level(): lax.ppermute(x, ALL, _perm(stride, size, s, ndev))  10.9 us
    gather x2, local copies, waits for them, and re-layouts, pick(): rows = jnp.take(packed, jnp.clip(local_row, 0, own_stars - 1), axis=1)  9.99 us
    ppermute x9, starting transfers between devices, sum_level(): total = total + lax.ppermute(x, ALL, _perm(stride, size, s, ndev))  9.47 us
    ppermute x8, waiting for transfers between devices, gather_level(): lax.ppermute(x, ALL, _perm(stride, size, s, ndev))  6.84 us
  transfers between devices with their start and end apart: 27, of which 22 were waited for; matrix products, arithmetic and copies ran while one was open for 6% of the time, Pallas kernels for 0%

profile of v11, /device:TPU:1, one launch (start us, length us, event | category | flops | bytes accessed | tf_op | source)
XLA Modules:
  0.0 216.2 jit_solution(10319058584353087775)
XLA Ops:
  0.6 1.5 collective-permute-start
  2.3 0.7 collective-permute-done
  3.0 0.7 pad_add_fusion.2
  4.4 2.6 %collective-permute-start.3 = (s32[32]{0:T(128)S(1)}, s32[32]{0:T(128)S(1)}, u32[]{:S(2)}, u32[]{:S(2)}) collective-permute-start(s32[32]{0:T(128)S(1)} %select_n.354), channel_id=1, source_target_pairs={{0,6},{1,7},{2,0},{3,1},{4,2},{5,3},{6,4},{7,5},{8,14},{9,15},{10,... | collective-permute-start | bytes 392 | tf_op jit(solution)/shard_map/ppermute | solution.py:62
  7.5 0.6 collective-permute-start.1
  8.2 2.7 %collective-permute-done.2 = s32[32]{0:T(128)S(1)} collective-permute-done((s32[32]{0:T(128)S(1)}, s32[32]{0:T(128)S(1)}, u32[]{:S(2)}, u32[]{:S(2)}) %collective-permute-start.2) | collective-permute-done | bytes 160 | tf_op jit(solution)/shard_map/ppermute | solution.py:62
  11.2 0.6 gather_fusion.1
  11.9 1.3 collective-permute-start.4
  13.2 4.0 %concatenate.21 = f32[13,8192]{1,0:T(8,128)S(1)} concatenate(f32[3,8192]{1,0:T(4,128)} %param.19, f32[3,8192]{1,0:T(4,128)} %param.20, f32[3,8192]{1,0:T(4,128)} %param.21, f32[3,8192]{1,0:T(4,128)} %param.22, f32[1,8192]{1,0:T(1,128)} %bitcast.96), dimensions={0} | concatenate | bytes 851968 | tf_op jit(solution)/shard_map/concatenate | solution.py:166
  17.3 2.7 %copy.78 = f32[13,8192]{0,1:T(8,128)} copy(f32[13,8192]{1,0:T(8,128)S(1)} %concatenate.21) | data formatting | bytes 851968 | tf_op jit(solution)/shard_map/concatenate | solution.py:166
  20.0 0.6 gather_fusion.2
  20.7 3.8 %collective-permute-start.7 = (s32[256]{0:T(256)S(1)}, s32[256]{0:T(256)S(1)}, u32[]{:S(2)}, u32[]{:S(2)}) collective-permute-start(s32[256]{0:T(256)S(1)} %fusion.36), channel_id=1, source_target_pairs={{0,48},{1,49},{2,50},{3,51},{4,52},{5,53},{6,54},{7,55},{8,56},{9,... | collective-permute-start | bytes 3080 | tf_op jit(solution)/shard_map/ppermute | solution.py:62
  24.4 0.7 collective-permute-start.5
  25.2 3.2 %collective-permute-done.6 = s32[256]{0:T(256)S(1)} collective-permute-done((s32[256]{0:T(256)S(1)}, s32[256]{0:T(256)S(1)}, u32[]{:S(2)}, u32[]{:S(2)}) %collective-permute-start.6) | collective-permute-done | bytes 1056 | tf_op jit(solution)/shard_map/ppermute | solution.py:62
  28.4 0.6 gather_fusion.3
  29.1 2.7 %collective-permute-start.8 = (s32[1024]{0:T(1024)S(1)}, s32[1024]{0:T(1024)S(1)}, u32[]{:S(2)}, u32[]{:S(2)}) collective-permute-start(s32[1024]{0:T(1024)S(1)} %bitcast.106), channel_id=1, source_target_pairs={{0,64},{1,65},{2,66},{3,67},{4,68},{5,69},{6,70},{7,71},{8,72},{9,... | collective-permute-start | bytes 12296 | tf_op jit(solution)/shard_map/ppermute | solution.py:160
  31.8 5.0 %gather_fusion.5 = f32[1024,13]{1,0:T(8,128)S(1)} fusion(f32[13,8192]{0,1:T(8,128)} %copy.78, s32[1024]{0:T(1024)S(1)} %fusion.19), kind=kCustom, calls=%fused_computation.1.clone | custom fusion | bytes 110592 | tf_op jit(solution)/shard_map/jit(_take)/gather | solution.py:174
  37.3 5.0 %gather_fusion.4 = f32[1024,13]{1,0:T(8,128)S(1)} fusion(f32[13,8192]{0,1:T(8,128)} %copy.78, s32[1024]{0:T(1024)S(1)} %fusion.18), kind=kCustom, calls=%fused_computation.clone | custom fusion | bytes 110592 | tf_op jit(solution)/shard_map/jit(_take)/gather | solution.py:174
  43.0 4.1 %collective-permute-start.9 = (f32[6,2048]{1,0:T(8,128)S(1)}, f32[6,2048]{1,0:T(8,128)S(1)}, u32[]{:S(2)}, u32[]{:S(2)}) collective-permute-start(f32[6,2048]{1,0:T(8,128)S(1)} %pad_maximum_fusion.1), channel_id=1, source_target_pairs={{0,1},{1,0},{2,3},{3,2},{4,5},{5,4},{6,7},{7,6},{8,9},{9,8},{10,11... | collective-permute-start | bytes 147464 | tf_op jit(solution)/shard_map/ppermute | solution.py:88
  47.2 0.9 collective-permute-done.9
  48.2 1.3 collective-permute-start.11
  49.5 0.8 collective-permute-start.10
  50.3 1.0 collective-permute-done.12
  51.3 1.6 collective-permute-done.11
  52.9 2.1 collective-permute-done.10
  55.1 3.1 %collective-permute-done.13 = f32[6,2048]{1,0:T(8,128)S(1)} collective-permute-done((f32[6,2048]{1,0:T(8,128)S(1)}, f32[6,2048]{1,0:T(8,128)S(1)}, u32[]{:S(2)}, u32[]{:S(2)}) %collective-permute-start.13) | collective-permute-done | bytes 49184 | tf_op jit(solution)/shard_map/ppermute | solution.py:88
  58.6 1.5 collective-permute-start.15
  60.1 0.8 collective-permute-start.14
  61.4 1.8 collective-permute-done.15
  63.2 1.3 collective-permute-done.14
  65.4 3.8 %collective-permute-done.17 = f32[6,2048]{1,0:T(8,128)S(1)} collective-permute-done((f32[6,2048]{1,0:T(8,128)S(1)}, f32[6,2048]{1,0:T(8,128)S(1)}, u32[]{:S(2)}, u32[]{:S(2)}) %collective-permute-start.17) | collective-permute-done | bytes 49184 | tf_op jit(solution)/shard_map/ppermute | solution.py:88
  69.7 1.0 pad_bitcast_fusion.act_ref
  70.7 1.5 broadcast_in_dim.153.fld_ref
  72.2 108.1 %shard_map.102 = f32[6,2048,128]{2,1,0:T(8,128)} custom-call(f32[2048,8]{1,0:T(8,128)} %pad_bitcast_fusion.act_ref, f32[8,8,8192]{2,1,0:T(8,128)} %broadcast_in_dim.153.fld_ref), custom_call_target="tpu_custom_call" | custom-call | tf_op jit(solution)/shard_map/pallas_call | solution.py:145
  180.4 4.5 %reduce_sum.9 = f32[6,2048]{1,0:T(8,128)S(1)} reduce(f32[6,2048,128]{2,1,0:T(8,128)} %shard_map.102, f32[]{:T(128)} %constant.324.clone.1), dimensions={2}, to_apply=%region_0.2 | reduce | flops 1560576 | bytes 6340612 | tf_op jit(solution)/shard_map/reduce_sum | solution.py:190
  185.2 0.6 collective-permute-start.18
  185.8 4.3 %collective-permute-done.18 = f32[13,1024]{1,0:T(8,128)S(1)} collective-permute-done((f32[13,1024]{1,0:T(8,128)S(1)}, f32[13,1024]{1,0:T(8,128)S(1)}, u32[]{:S(2)}, u32[]{:S(2)}) %collective-permute-start.18) | collective-permute-done | bytes 53280 | tf_op jit(solution)/shard_map/ppermute | solution.py:80
  190.2 1.2 collective-permute-start.21
  191.3 0.6 collective-permute-start.20
  192.8 2.6 %collective-permute-done.20 = f32[13,256]{1,0:T(8,128)S(1)} collective-permute-done((f32[13,256]{1,0:T(8,128)S(1)}, f32[13,256]{1,0:T(8,128)S(1)}, u32[]{:S(2)}, u32[]{:S(2)}) %collective-permute-start.20) | collective-permute-done | bytes 13344 | tf_op jit(solution)/shard_map/ppermute | solution.py:80
  196.1 2.3 %collective-permute-done.22 = f32[13,128]{1,0:T(8,128)S(1)} collective-permute-done((f32[13,128]{1,0:T(8,128)S(1)}, f32[13,128]{1,0:T(8,128)S(1)}, u32[]{:S(2)}, u32[]{:S(2)}) %collective-permute-start.22) | collective-permute-done | bytes 6688 | tf_op jit(solution)/shard_map/ppermute | solution.py:80
  198.5 0.9 collective-permute-start.25
  199.4 0.6 collective-permute-start.24
  200.4 1.0 collective-permute-done.25
  201.4 2.0 collective-permute-done.24
  203.8 11.0 %collective-permute-start.26 = (f32[13,16]{1,0:T(8,128)S(1)}, f32[13,16]{1,0:T(8,128)S(1)}, u32[]{:S(2)}, u32[]{:S(2)}) collective-permute-start(f32[13,16]{1,0:T(8,128)S(1)} %bitcast.113), channel_id=1, source_target_pairs={{0,1},{1,0},{2,3},{3,2},{4,5},{5,4},{6,7},{7,6},{8,9},{9,8},{10,11... | collective-permute-start | bytes 2504 | tf_op jit(solution)/shard_map/ppermute | solution.py:80
  214.8 0.8 collective-permute-done.26
  215.7 0.6 fusion.21
  (106 shorter events, 8.7 us)
Async XLA Ops:
  0.6 2.4 %collective-permute-start = (s32[16]{0:T(128)}, s32[16]{0:T(128)S(1)}, u32[]{:S(2)}, u32[]{:S(2)}) collective-permute-start(s32[16]{0:T(128)} %param.25), channel_id=1, source_target_pairs={{0,1},{1,0},{2,3},{3,2},{4,5},{5,4},{6,7},{7,6},{8,9},{9,8},{10,11... | collective-permute-start | bytes 200 | tf_op jit(solution)/shard_map/ppermute | solution.py:62
  4.4 3.8 %collective-permute-start.3 = (s32[32]{0:T(128)S(1)}, s32[32]{0:T(128)S(1)}, u32[]{:S(2)}, u32[]{:S(2)}) collective-permute-start(s32[32]{0:T(128)S(1)} %select_n.354), channel_id=1, source_target_pairs={{0,6},{1,7},{2,0},{3,1},{4,2},{5,3},{6,4},{7,5},{8,14},{9,15},{10,... | collective-permute-start | bytes 392 | tf_op jit(solution)/shard_map/ppermute | solution.py:62
  7.0 3.9 %collective-permute-start.2 = (s32[32]{0:T(128)S(1)}, s32[32]{0:T(128)S(1)}, u32[]{:S(2)}, u32[]{:S(2)}) collective-permute-start(s32[32]{0:T(128)S(1)} %select_n.354), channel_id=1, source_target_pairs={{0,4},{1,5},{2,6},{3,7},{4,0},{5,1},{6,2},{7,3},{8,12},{9,13},{10,... | collective-permute-start | bytes 392 | tf_op jit(solution)/shard_map/ppermute | solution.py:62
  7.5 3.6 %collective-permute-start.1 = (s32[32]{0:T(128)S(1)}, s32[32]{0:T(128)S(1)}, u32[]{:S(2)}, u32[]{:S(2)}) collective-permute-start(s32[32]{0:T(128)S(1)} %select_n.354), channel_id=1, source_target_pairs={{0,2},{1,3},{2,4},{3,5},{4,6},{5,7},{6,0},{7,1},{8,10},{9,11},{10,... | collective-permute-start | bytes 392 | tf_op jit(solution)/shard_map/ppermute | solution.py:62
  11.9 8.1 %collective-permute-start.4 = (s32[128]{0:T(128)S(1)}, s32[128]{0:T(128)S(1)}, u32[]{:S(2)}, u32[]{:S(2)}) collective-permute-start(s32[128]{0:T(128)S(1)} %select_n.359), channel_id=1, source_target_pairs={{0,8},{1,9},{2,10},{3,11},{4,12},{5,13},{6,14},{7,15},{8,0},{9,1},... | collective-permute-start | bytes 1544 | tf_op jit(solution)/shard_map/ppermute | solution.py:62
  17.2 37.9 %copy-start.4 = (f32[8192]{0:T(1024)S(1)}, f32[8192]{0:T(1024)}, u32[]{:S(2)}) copy-start(f32[8192]{0:T(1024)} %param.24) | copy-start | bytes 98308
  19.9 41.0 %copy-start = (f32[3,8192]{1,0:T(4,128)S(1)}, f32[3,8192]{1,0:T(4,128)}, u32[]{:S(2)}) copy-start(f32[3,8192]{1,0:T(4,128)} %param.19) | copy-start | bytes 294916
  19.9 41.0 %copy-start.1 = (f32[3,8192]{1,0:T(4,128)S(1)}, f32[3,8192]{1,0:T(4,128)}, u32[]{:S(2)}) copy-start(f32[3,8192]{1,0:T(4,128)} %param.20) | copy-start | bytes 294916
  19.9 41.0 %copy-start.2 = (f32[3,8192]{1,0:T(4,128)S(1)}, f32[3,8192]{1,0:T(4,128)}, u32[]{:S(2)}) copy-start(f32[3,8192]{1,0:T(4,128)} %param.21) | copy-start | bytes 294916
  19.9 41.0 %copy-start.3 = (f32[3,8192]{1,0:T(4,128)S(1)}, f32[3,8192]{1,0:T(4,128)}, u32[]{:S(2)}) copy-start(f32[3,8192]{1,0:T(4,128)} %param.22) | copy-start | bytes 294916
  19.9 45.0 %copy-start.5 = (f32[8192]{0:T(1024)S(1)}, f32[8192]{0:T(1024)}, u32[]{:S(2)}) copy-start(f32[8192]{0:T(1024)} %param.23) | copy-start | bytes 98308
  20.7 4.5 %collective-permute-start.7 = (s32[256]{0:T(256)S(1)}, s32[256]{0:T(256)S(1)}, u32[]{:S(2)}, u32[]{:S(2)}) collective-permute-start(s32[256]{0:T(256)S(1)} %fusion.36), channel_id=1, source_target_pairs={{0,48},{1,49},{2,50},{3,51},{4,52},{5,53},{6,54},{7,55},{8,56},{9,... | collective-permute-start | bytes 3080 | tf_op jit(solution)/shard_map/ppermute | solution.py:62
  24.4 3.9 %collective-permute-start.6 = (s32[256]{0:T(256)S(1)}, s32[256]{0:T(256)S(1)}, u32[]{:S(2)}, u32[]{:S(2)}) collective-permute-start(s32[256]{0:T(256)S(1)} %fusion.36), channel_id=1, source_target_pairs={{0,32},{1,33},{2,34},{3,35},{4,36},{5,37},{6,38},{7,39},{8,40},{9,... | collective-permute-start | bytes 3080 | tf_op jit(solution)/shard_map/ppermute | solution.py:62
  24.4 3.9 %collective-permute-start.5 = (s32[256]{0:T(256)S(1)}, s32[256]{0:T(256)S(1)}, u32[]{:S(2)}, u32[]{:S(2)}) collective-permute-start(s32[256]{0:T(256)S(1)} %fusion.36), channel_id=1, source_target_pairs={{0,16},{1,17},{2,18},{3,19},{4,20},{5,21},{6,22},{7,23},{8,24},{9,... | collective-permute-start | bytes 3080 | tf_op jit(solution)/shard_map/ppermute | solution.py:62
  29.1 8.2 %collective-permute-start.8 = (s32[1024]{0:T(1024)S(1)}, s32[1024]{0:T(1024)S(1)}, u32[]{:S(2)}, u32[]{:S(2)}) collective-permute-start(s32[1024]{0:T(1024)S(1)} %bitcast.106), channel_id=1, source_target_pairs={{0,64},{1,65},{2,66},{3,67},{4,68},{5,69},{6,70},{7,71},{8,72},{9,... | collective-permute-start | bytes 12296 | tf_op jit(solution)/shard_map/ppermute | solution.py:160
  43.0 5.0 %collective-permute-start.9 = (f32[6,2048]{1,0:T(8,128)S(1)}, f32[6,2048]{1,0:T(8,128)S(1)}, u32[]{:S(2)}, u32[]{:S(2)}) collective-permute-start(f32[6,2048]{1,0:T(8,128)S(1)} %pad_maximum_fusion.1), channel_id=1, source_target_pairs={{0,1},{1,0},{2,3},{3,2},{4,5},{5,4},{6,7},{7,6},{8,9},{9,8},{10,11... | collective-permute-start | bytes 147464 | tf_op jit(solution)/shard_map/ppermute | solution.py:88
  48.1 3.2 %collective-permute-start.12 = (f32[6,2048]{1,0:T(8,128)S(1)}, f32[6,2048]{1,0:T(8,128)S(1)}, u32[]{:S(2)}, u32[]{:S(2)}) collective-permute-start(f32[6,2048]{1,0:T(8,128)S(1)} %fusion.34), channel_id=1, source_target_pairs={{0,6},{1,7},{2,0},{3,1},{4,2},{5,3},{6,4},{7,5},{8,14},{9,15},{10,... | collective-permute-start | bytes 147464 | tf_op jit(solution)/shard_map/ppermute | solution.py:88
  48.2 4.7 %collective-permute-start.11 = (f32[6,2048]{1,0:T(8,128)S(1)}, f32[6,2048]{1,0:T(8,128)S(1)}, u32[]{:S(2)}, u32[]{:S(2)}) collective-permute-start(f32[6,2048]{1,0:T(8,128)S(1)} %fusion.34), channel_id=1, source_target_pairs={{0,4},{1,5},{2,6},{3,7},{4,0},{5,1},{6,2},{7,3},{8,12},{9,13},{10,... | collective-permute-start | bytes 147464 | tf_op jit(solution)/shard_map/ppermute | solution.py:88
  49.5 5.5 %collective-permute-start.10 = (f32[6,2048]{1,0:T(8,128)S(1)}, f32[6,2048]{1,0:T(8,128)S(1)}, u32[]{:S(2)}, u32[]{:S(2)}) collective-permute-start(f32[6,2048]{1,0:T(8,128)S(1)} %fusion.34), channel_id=1, source_target_pairs={{0,2},{1,3},{2,4},{3,5},{4,6},{5,7},{6,0},{7,1},{8,10},{9,11},{10,... | collective-permute-start | bytes 147464 | tf_op jit(solution)/shard_map/ppermute | solution.py:88
  55.0 3.2 %collective-permute-start.13 = (f32[6,2048]{1,0:T(8,128)S(1)}, f32[6,2048]{1,0:T(8,128)S(1)}, u32[]{:S(2)}, u32[]{:S(2)}) collective-permute-start(f32[6,2048]{1,0:T(8,128)S(1)} %add_add_fusion.1), channel_id=1, source_target_pairs={{0,8},{1,9},{2,10},{3,11},{4,12},{5,13},{6,14},{7,15},{8,0},{9,1},... | collective-permute-start | bytes 147464 | tf_op jit(solution)/shard_map/ppermute | solution.py:88
  58.2 3.2 %collective-permute-start.16 = (f32[6,2048]{1,0:T(8,128)S(1)}, f32[6,2048]{1,0:T(8,128)S(1)}, u32[]{:S(2)}, u32[]{:S(2)}) collective-permute-start(f32[6,2048]{1,0:T(8,128)S(1)} %add.373), channel_id=1, source_target_pairs={{0,48},{1,49},{2,50},{3,51},{4,52},{5,53},{6,54},{7,55},{8,56},{9,... | collective-permute-start | bytes 147464 | tf_op jit(solution)/shard_map/ppermute | solution.py:88
  58.6 4.6 %collective-permute-start.15 = (f32[6,2048]{1,0:T(8,128)S(1)}, f32[6,2048]{1,0:T(8,128)S(1)}, u32[]{:S(2)}, u32[]{:S(2)}) collective-permute-start(f32[6,2048]{1,0:T(8,128)S(1)} %add.373), channel_id=1, source_target_pairs={{0,32},{1,33},{2,34},{3,35},{4,36},{5,37},{6,38},{7,39},{8,40},{9,... | collective-permute-start | bytes 147464 | tf_op jit(solution)/shard_map/ppermute | solution.py:88
  60.1 4.3 %collective-permute-start.14 = (f32[6,2048]{1,0:T(8,128)S(1)}, f32[6,2048]{1,0:T(8,128)S(1)}, u32[]{:S(2)}, u32[]{:S(2)}) collective-permute-start(f32[6,2048]{1,0:T(8,128)S(1)} %add.373), channel_id=1, source_target_pairs={{0,16},{1,17},{2,18},{3,19},{4,20},{5,21},{6,22},{7,23},{8,24},{9,... | collective-permute-start | bytes 147464 | tf_op jit(solution)/shard_map/ppermute | solution.py:88
  64.5 4.7 %collective-permute-start.17 = (f32[6,2048]{1,0:T(8,128)S(1)}, f32[6,2048]{1,0:T(8,128)S(1)}, u32[]{:S(2)}, u32[]{:S(2)}) collective-permute-start(f32[6,2048]{1,0:T(8,128)S(1)} %add_add_fusion), channel_id=1, source_target_pairs={{0,64},{1,65},{2,66},{3,67},{4,68},{5,69},{6,70},{7,71},{8,72},{9,... | collective-permute-start | bytes 147464 | tf_op jit(solution)/shard_map/ppermute | solution.py:88
  185.2 4.9 %collective-permute-start.18 = (f32[13,1024]{1,0:T(8,128)S(1)}, f32[13,1024]{1,0:T(8,128)S(1)}, u32[]{:S(2)}, u32[]{:S(2)}) collective-permute-start(f32[13,1024]{1,0:T(8,128)S(1)} %bitcast.101), channel_id=1, source_target_pairs={{0,64},{1,65},{2,66},{3,67},{4,68},{5,69},{6,70},{7,71},{8,72},{9,... | collective-permute-start | bytes 159752 | tf_op jit(solution)/shard_map/ppermute | solution.py:80
  190.2 2.7 %collective-permute-start.21 = (f32[13,256]{1,0:T(8,128)S(1)}, f32[13,256]{1,0:T(8,128)S(1)}, u32[]{:S(2)}, u32[]{:S(2)}) collective-permute-start(f32[13,256]{1,0:T(8,128)S(1)} %bitcast.110), channel_id=1, source_target_pairs={{0,48},{1,49},{2,50},{3,51},{4,52},{5,53},{6,54},{7,55},{8,56},{9,... | collective-permute-start | bytes 39944 | tf_op jit(solution)/shard_map/ppermute | solution.py:80
  191.3 4.1 %collective-permute-start.20 = (f32[13,256]{1,0:T(8,128)S(1)}, f32[13,256]{1,0:T(8,128)S(1)}, u32[]{:S(2)}, u32[]{:S(2)}) collective-permute-start(f32[13,256]{1,0:T(8,128)S(1)} %fusion.2), channel_id=1, source_target_pairs={{0,32},{1,33},{2,34},{3,35},{4,36},{5,37},{6,38},{7,39},{8,40},{9,... | collective-permute-start | bytes 39944 | tf_op jit(solution)/shard_map/ppermute | solution.py:80
  192.0 3.8 %collective-permute-start.19 = (f32[13,256]{1,0:T(8,128)S(1)}, f32[13,256]{1,0:T(8,128)S(1)}, u32[]{:S(2)}, u32[]{:S(2)}) collective-permute-start(f32[13,256]{1,0:T(8,128)S(1)} %fusion.3), channel_id=1, source_target_pairs={{0,16},{1,17},{2,18},{3,19},{4,20},{5,21},{6,22},{7,23},{8,24},{9,... | collective-permute-start | bytes 39944 | tf_op jit(solution)/shard_map/ppermute | solution.py:80
  195.8 2.6 %collective-permute-start.22 = (f32[13,128]{1,0:T(8,128)S(1)}, f32[13,128]{1,0:T(8,128)S(1)}, u32[]{:S(2)}, u32[]{:S(2)}) collective-permute-start(f32[13,128]{1,0:T(8,128)S(1)} %bitcast.111), channel_id=1, source_target_pairs={{0,8},{1,9},{2,10},{3,11},{4,12},{5,13},{6,14},{7,15},{8,0},{9,1},... | collective-permute-start | bytes 19976 | tf_op jit(solution)/shard_map/ppermute | solution.py:80
  198.5 2.9 %collective-permute-start.25 = (f32[13,32]{1,0:T(8,128)S(1)}, f32[13,32]{1,0:T(8,128)S(1)}, u32[]{:S(2)}, u32[]{:S(2)}) collective-permute-start(f32[13,32]{1,0:T(8,128)S(1)} %bitcast.112), channel_id=1, source_target_pairs={{0,6},{1,7},{2,0},{3,1},{4,2},{5,3},{6,4},{7,5},{8,14},{9,15},{10,... | collective-permute-start | bytes 5000 | tf_op jit(solution)/shard_map/ppermute | solution.py:80
  199.4 4.0 %collective-permute-start.24 = (f32[13,32]{1,0:T(8,128)S(1)}, f32[13,32]{1,0:T(8,128)S(1)}, u32[]{:S(2)}, u32[]{:S(2)}) collective-permute-start(f32[13,32]{1,0:T(8,128)S(1)} %fusion.10), channel_id=1, source_target_pairs={{0,4},{1,5},{2,6},{3,7},{4,0},{5,1},{6,2},{7,3},{8,12},{9,13},{10,... | collective-permute-start | bytes 5000 | tf_op jit(solution)/shard_map/ppermute | solution.py:80
  200.0 3.7 %collective-permute-start.23 = (f32[13,32]{1,0:T(8,128)S(1)}, f32[13,32]{1,0:T(8,128)S(1)}, u32[]{:S(2)}, u32[]{:S(2)}) collective-permute-start(f32[13,32]{1,0:T(8,128)S(1)} %fusion.11), channel_id=1, source_target_pairs={{0,2},{1,3},{2,4},{3,5},{4,6},{5,7},{6,0},{7,1},{8,10},{9,11},{10,... | collective-permute-start | bytes 5000 | tf_op jit(solution)/shard_map/ppermute | solution.py:80
  203.8 11.8 %collective-permute-start.26 = (f32[13,16]{1,0:T(8,128)S(1)}, f32[13,16]{1,0:T(8,128)S(1)}, u32[]{:S(2)}, u32[]{:S(2)}) collective-permute-start(f32[13,16]{1,0:T(8,128)S(1)} %bitcast.113), channel_id=1, source_target_pairs={{0,1},{1,0},{2,3},{3,2},{4,5},{5,4},{6,7},{7,6},{8,9},{9,8},{10,11... | collective-permute-start | bytes 2504 | tf_op jit(solution)/shard_map/ppermute | solution.py:80

commit v12 on v9

--- a/solution.py
+++ b/solution.py
@@ -1,11 +1,9 @@
-import functools
-
 import jax
 import jax.numpy as jnp
 from jax import lax
 from jax.experimental import pallas as pl
-from jax.experimental.pallas import tpu as pltpu
 from jax.sharding import PartitionSpec as P
+
 
 softening = 0.001
 ALL = ("blk", "group")
@@ -133,13 +131,13 @@
 
         zero = jnp.zeros((8, 128), jnp.float32)
         init = tuple(tuple(zero for _ in range(6)) for _ in range(SUB))
-        accs = lax.fori_loop(0, num_j // 128, jstep, init, unroll=16)
+        accs = lax.fori_loop(0, num_j // 128, jstep, init, unroll=64)
         for s in range(SUB):
             for c in range(6):
                 out_ref[c, pl.ds(k0 + 8 * s, 8), :] = accs[s][c]
         return carry
 
-    lax.fori_loop(0, num_k // step_k, kblock, 0)
+    lax.fori_loop(0, num_k // step_k, kblock, 0, unroll=4)
 
 
 def pair_forces(active_t, field_b):
@@ -150,7 +148,7 @@
     )(active_t, field_b)
 
 
-def on_device(positions, velocities, accelerations, jerk_rates, masses, elapsed_time, active_index):
+def step(positions, velocities, accelerations, jerk_rates, masses, elapsed_time, active_index):
     ndev = lax.axis_size("blk") * lax.axis_size("group")
     own_stars = positions.shape[1]
     total_stars = own_stars * ndev
@@ -186,7 +184,7 @@
 
 def solution(mesh):
     return jax.shard_map(
-        on_device,
+        step,
         mesh=mesh,
         in_specs=(
             P(None, ALL),

time: 218 us -> 204 us (0.936)
  Pallas kernels: 110 us -> 96.2 us
    pallas_call x1, Pallas kernels: 110 us -> 96.2 us  [pair_forces(): pl.pallas_call(forces_kernel, out_shape=jax.ShapeDtypeStruct((6, num_k, 1...]
where the time goes in v12:
time: 204 us
  Pallas kernels  96.2 us (47%)
  starting transfers between devices  41 us (20%)
  waiting for transfers between devices  37 us (18%)
  local copies, waits for them, and re-layouts  21.6 us (11%)
  other arithmetic  7.28 us (4%)
    pallas_call x1, Pallas kernels, pair_forces(): pl.pallas_call(forces_kernel, out_shape=jax.ShapeDtypeStruct((6, num_k, 1...  96.2 us
    ppermute x9, starting transfers between devices, reduce_level(): total = total + lax.ppermute(piece, ALL, _perm(stride, size, s, ndev))  16 us
    ppermute x9, waiting for transfers between devices, sum_level(): total = total + lax.ppermute(x, ALL, _perm(stride, size, s, ndev))  15.3 us
    ppermute x9, starting transfers between devices, gather_level(): lax.ppermute(x, ALL, _perm(stride, size, s, ndev))  13.9 us
    ppermute x9, waiting for transfers between devices, reduce_level(): total = total + lax.ppermute(piece, ALL, _perm(stride, size, s, ndev))  13.8 us
    ppermute x9, starting transfers between devices, sum_level(): total = total + lax.ppermute(x, ALL, _perm(stride, size, s, ndev))  11.1 us
    gather x2, local copies, waits for them, and re-layouts, step(): picked = jnp.take(packed, jnp.clip(local_row, 0, own_stars - 1), axis=1)  7.98 us
    ppermute x9, waiting for transfers between devices, gather_level(): lax.ppermute(x, ALL, _perm(stride, size, s, ndev))  7.85 us
  transfers between devices with their start and end apart: 27, of which 23 were waited for; matrix products, arithmetic and copies ran while one was open for 4% of the time, Pallas kernels for 0%

profile of v12, /device:TPU:1, one launch (start us, length us, event | category | flops | bytes accessed | tf_op | source)
XLA Modules:
  0.0 204.1 jit_solution(10360373525626262437)
XLA Ops:
  0.6 1.5 collective-permute-start
  2.3 0.7 collective-permute-done
  3.0 0.7 pad_add_fusion.3
  4.4 2.6 %collective-permute-start.3 = (s32[32]{0:T(128)S(1)}, s32[32]{0:T(128)S(1)}, u32[]{:S(2)}, u32[]{:S(2)}) collective-permute-start(s32[32]{0:T(128)S(1)} %select_n.413), channel_id=1, source_target_pairs={{0,6},{1,7},{2,0},{3,1},{4,2},{5,3},{6,4},{7,5},{8,14},{9,15},{10,... | collective-permute-start | bytes 392 | tf_op jit(solution)/shard_map/ppermute | solution.py:62
  7.5 0.6 collective-permute-start.1
  8.2 2.7 %collective-permute-done.2 = s32[32]{0:T(128)S(1)} collective-permute-done((s32[32]{0:T(128)S(1)}, s32[32]{0:T(128)S(1)}, u32[]{:S(2)}, u32[]{:S(2)}) %collective-permute-start.2) | collective-permute-done | bytes 160 | tf_op jit(solution)/shard_map/ppermute | solution.py:62
  11.9 1.3 collective-permute-start.4
  13.3 1.0 collective-permute-done.4
  15.0 3.8 %collective-permute-start.7 = (s32[256]{0:T(256)S(1)}, s32[256]{0:T(256)S(1)}, u32[]{:S(2)}, u32[]{:S(2)}) collective-permute-start(s32[256]{0:T(256)S(1)} %fusion.37), channel_id=1, source_target_pairs={{0,48},{1,49},{2,50},{3,51},{4,52},{5,53},{6,54},{7,55},{8,56},{9,... | collective-permute-start | bytes 3080 | tf_op jit(solution)/shard_map/ppermute | solution.py:62
  18.7 0.7 collective-permute-start.5
  19.5 3.2 %collective-permute-done.6 = s32[256]{0:T(256)S(1)} collective-permute-done((s32[256]{0:T(256)S(1)}, s32[256]{0:T(256)S(1)}, u32[]{:S(2)}, u32[]{:S(2)}) %collective-permute-start.6) | collective-permute-done | bytes 1056 | tf_op jit(solution)/shard_map/ppermute | solution.py:62
  22.7 0.6 gather_fusion.3
  23.3 2.9 %collective-permute-start.8 = (s32[1024]{0:T(1024)S(1)}, s32[1024]{0:T(1024)S(1)}, u32[]{:S(2)}, u32[]{:S(2)}) collective-permute-start(s32[1024]{0:T(1024)S(1)} %bitcast.131), channel_id=1, source_target_pairs={{0,64},{1,65},{2,66},{3,67},{4,68},{5,69},{6,70},{7,71},{8,72},{9,... | collective-permute-start | bytes 12296 | tf_op jit(solution)/shard_map/ppermute | solution.py:62
  26.3 4.0 %concatenate.15 = f32[13,8192]{1,0:T(8,128)S(1)} concatenate(f32[3,8192]{1,0:T(4,128)} %param.17, f32[3,8192]{1,0:T(4,128)} %param.18, f32[3,8192]{1,0:T(4,128)} %param.19, f32[3,8192]{1,0:T(4,128)} %param.20, f32[1,8192]{1,0:T(1,128)} %bitcast.113), dimensions={0} | concatenate | bytes 851968 | tf_op jit(solution)/shard_map/concatenate | solution.py:164
  30.4 2.7 %copy.84 = f32[13,8192]{0,1:T(8,128)} copy(f32[13,8192]{1,0:T(8,128)S(1)} %concatenate.15) | data formatting | bytes 851968 | tf_op jit(solution)/shard_map/concatenate | solution.py:164
  33.1 0.6 gather_fusion.4
  33.8 7.6 %gather_fusion.5 = f32[2048,13]{1,0:T(8,128)S(1)} fusion(f32[13,8192]{0,1:T(8,128)} %copy.84, s32[2048]{0:T(1024)S(1)} %broadcast_clamp_fusion), kind=kCustom, calls=%fused_computation.5 | custom fusion | bytes 221184 | tf_op jit(solution)/shard_map/jit(_take)/gather | solution.py:170
  42.0 5.0 %collective-permute-start.9 = (f32[6,2048]{1,0:T(8,128)S(1)}, f32[6,2048]{1,0:T(8,128)S(1)}, u32[]{:S(2)}, u32[]{:S(2)}) collective-permute-start(f32[6,2048]{1,0:T(8,128)S(1)} %pad_maximum_fusion.1), channel_id=1, source_target_pairs={{0,1},{1,0},{2,3},{3,2},{4,5},{5,4},{6,7},{7,6},{8,9},{9,8},{10,11... | collective-permute-start | bytes 147464 | tf_op jit(solution)/shard_map/ppermute | solution.py:88
  47.0 0.9 collective-permute-done.9
  48.0 1.3 collective-permute-start.11
  49.3 0.8 collective-permute-start.10
  50.1 1.0 collective-permute-done.12
  51.1 1.6 collective-permute-done.11
  52.7 2.1 %collective-permute-done.10 = f32[6,2048]{1,0:T(8,128)S(1)} collective-permute-done((f32[6,2048]{1,0:T(8,128)S(1)}, f32[6,2048]{1,0:T(8,128)S(1)}, u32[]{:S(2)}, u32[]{:S(2)}) %collective-permute-start.10) | collective-permute-done | bytes 49184 | tf_op jit(solution)/shard_map/ppermute | solution.py:88
  55.3 2.7 %collective-permute-done.13 = f32[6,2048]{1,0:T(8,128)S(1)} collective-permute-done((f32[6,2048]{1,0:T(8,128)S(1)}, f32[6,2048]{1,0:T(8,128)S(1)}, u32[]{:S(2)}, u32[]{:S(2)}) %collective-permute-start.13) | collective-permute-done | bytes 49184 | tf_op jit(solution)/shard_map/ppermute | solution.py:88
  58.4 1.6 collective-permute-start.15
  59.9 0.8 collective-permute-start.14
  61.2 1.8 collective-permute-done.15
  63.0 1.3 collective-permute-done.14
  64.3 0.7 collective-permute-start.17
  65.5 3.6 %collective-permute-done.17 = f32[6,2048]{1,0:T(8,128)S(1)} collective-permute-done((f32[6,2048]{1,0:T(8,128)S(1)}, f32[6,2048]{1,0:T(8,128)S(1)}, u32[]{:S(2)}, u32[]{:S(2)}) %collective-permute-start.17) | collective-permute-done | bytes 49184 | tf_op jit(solution)/shard_map/ppermute | solution.py:88
  69.7 1.0 pad_bitcast_fusion.act_ref
  70.7 1.5 broadcast_in_dim.160.fld_ref
  72.2 96.2 %shard_map.102 = f32[6,2048,128]{2,1,0:T(8,128)} custom-call(f32[2048,8]{1,0:T(8,128)} %pad_bitcast_fusion.act_ref, f32[8,8,8192]{2,1,0:T(8,128)} %broadcast_in_dim.160.fld_ref), custom_call_target="tpu_custom_call" | custom-call | tf_op jit(solution)/shard_map/pallas_call | solution.py:145
  168.4 4.5 %reduce_sum.9 = f32[6,2048]{1,0:T(8,128)S(1)} reduce(f32[6,2048,128]{2,1,0:T(8,128)} %shard_map.102, f32[]{:T(128)} %constant.346.clone.1), dimensions={2}, to_apply=%region_0.1 | reduce | flops 1560576 | bytes 6340612 | tf_op jit(solution)/shard_map/reduce_sum | solution.py:178
  173.2 0.6 collective-permute-start.18
  173.7 4.1 %collective-permute-done.18 = f32[13,1024]{1,0:T(8,128)S(1)} collective-permute-done((f32[13,1024]{1,0:T(8,128)S(1)}, f32[13,1024]{1,0:T(8,128)S(1)}, u32[]{:S(2)}, u32[]{:S(2)}) %collective-permute-start.18) | collective-permute-done | bytes 53280 | tf_op jit(solution)/shard_map/ppermute | solution.py:80
  178.0 1.2 collective-permute-start.21
  179.2 0.6 collective-permute-start.20
  180.7 2.6 %collective-permute-done.20 = f32[13,256]{1,0:T(8,128)S(1)} collective-permute-done((f32[13,256]{1,0:T(8,128)S(1)}, f32[13,256]{1,0:T(8,128)S(1)}, u32[]{:S(2)}, u32[]{:S(2)}) %collective-permute-start.20) | collective-permute-done | bytes 13344 | tf_op jit(solution)/shard_map/ppermute | solution.py:80
  184.1 2.1 %collective-permute-done.22 = f32[13,128]{1,0:T(8,128)S(1)} collective-permute-done((f32[13,128]{1,0:T(8,128)S(1)}, f32[13,128]{1,0:T(8,128)S(1)}, u32[]{:S(2)}, u32[]{:S(2)}) %collective-permute-start.22) | collective-permute-done | bytes 6688 | tf_op jit(solution)/shard_map/ppermute | solution.py:80
  186.4 0.9 collective-permute-start.25
  187.2 0.6 collective-permute-start.24
  188.3 1.0 collective-permute-done.25
  189.2 2.0 collective-permute-done.24
  191.7 11.0 %collective-permute-start.26 = (f32[13,16]{1,0:T(8,128)S(1)}, f32[13,16]{1,0:T(8,128)S(1)}, u32[]{:S(2)}, u32[]{:S(2)}) collective-permute-start(f32[13,16]{1,0:T(8,128)S(1)} %bitcast.130), channel_id=1, source_target_pairs={{0,1},{1,0},{2,3},{3,2},{4,5},{5,4},{6,7},{7,6},{8,9},{9,8},{10,11... | collective-permute-start | bytes 2504 | tf_op jit(solution)/shard_map/ppermute | solution.py:80
  202.6 0.8 collective-permute-done.26
  203.5 0.6 fusion.19
  (112 shorter events, 9.5 us)
Async XLA Ops:
  0.6 2.4 %collective-permute-start = (s32[16]{0:T(128)}, s32[16]{0:T(128)S(1)}, u32[]{:S(2)}, u32[]{:S(2)}) collective-permute-start(s32[16]{0:T(128)} %param.23), channel_id=1, source_target_pairs={{0,1},{1,0},{2,3},{3,2},{4,5},{5,4},{6,7},{7,6},{8,9},{9,8},{10,11... | collective-permute-start | bytes 200 | tf_op jit(solution)/shard_map/ppermute | solution.py:62
  4.4 3.8 %collective-permute-start.3 = (s32[32]{0:T(128)S(1)}, s32[32]{0:T(128)S(1)}, u32[]{:S(2)}, u32[]{:S(2)}) collective-permute-start(s32[32]{0:T(128)S(1)} %select_n.413), channel_id=1, source_target_pairs={{0,6},{1,7},{2,0},{3,1},{4,2},{5,3},{6,4},{7,5},{8,14},{9,15},{10,... | collective-permute-start | bytes 392 | tf_op jit(solution)/shard_map/ppermute | solution.py:62
  7.0 3.9 %collective-permute-start.2 = (s32[32]{0:T(128)S(1)}, s32[32]{0:T(128)S(1)}, u32[]{:S(2)}, u32[]{:S(2)}) collective-permute-start(s32[32]{0:T(128)S(1)} %select_n.413), channel_id=1, source_target_pairs={{0,4},{1,5},{2,6},{3,7},{4,0},{5,1},{6,2},{7,3},{8,12},{9,13},{10,... | collective-permute-start | bytes 392 | tf_op jit(solution)/shard_map/ppermute | solution.py:62
  7.5 3.6 %collective-permute-start.1 = (s32[32]{0:T(128)S(1)}, s32[32]{0:T(128)S(1)}, u32[]{:S(2)}, u32[]{:S(2)}) collective-permute-start(s32[32]{0:T(128)S(1)} %select_n.413), channel_id=1, source_target_pairs={{0,2},{1,3},{2,4},{3,5},{4,6},{5,7},{6,0},{7,1},{8,10},{9,11},{10,... | collective-permute-start | bytes 392 | tf_op jit(solution)/shard_map/ppermute | solution.py:62
  11.9 2.4 %collective-permute-start.4 = (s32[128]{0:T(128)S(1)}, s32[128]{0:T(128)S(1)}, u32[]{:S(2)}, u32[]{:S(2)}) collective-permute-start(s32[128]{0:T(128)S(1)} %select_n.418), channel_id=1, source_target_pairs={{0,8},{1,9},{2,10},{3,11},{4,12},{5,13},{6,14},{7,15},{8,0},{9,1},... | collective-permute-start | bytes 1544 | tf_op jit(solution)/shard_map/ppermute | solution.py:62
  15.0 4.5 %collective-permute-start.7 = (s32[256]{0:T(256)S(1)}, s32[256]{0:T(256)S(1)}, u32[]{:S(2)}, u32[]{:S(2)}) collective-permute-start(s32[256]{0:T(256)S(1)} %fusion.37), channel_id=1, source_target_pairs={{0,48},{1,49},{2,50},{3,51},{4,52},{5,53},{6,54},{7,55},{8,56},{9,... | collective-permute-start | bytes 3080 | tf_op jit(solution)/shard_map/ppermute | solution.py:62
  18.7 3.9 %collective-permute-start.6 = (s32[256]{0:T(256)S(1)}, s32[256]{0:T(256)S(1)}, u32[]{:S(2)}, u32[]{:S(2)}) collective-permute-start(s32[256]{0:T(256)S(1)} %fusion.37), channel_id=1, source_target_pairs={{0,32},{1,33},{2,34},{3,35},{4,36},{5,37},{6,38},{7,39},{8,40},{9,... | collective-permute-start | bytes 3080 | tf_op jit(solution)/shard_map/ppermute | solution.py:62
  18.7 3.9 %collective-permute-start.5 = (s32[256]{0:T(256)S(1)}, s32[256]{0:T(256)S(1)}, u32[]{:S(2)}, u32[]{:S(2)}) collective-permute-start(s32[256]{0:T(256)S(1)} %fusion.37), channel_id=1, source_target_pairs={{0,16},{1,17},{2,18},{3,19},{4,20},{5,21},{6,22},{7,23},{8,24},{9,... | collective-permute-start | bytes 3080 | tf_op jit(solution)/shard_map/ppermute | solution.py:62
  23.3 9.7 %collective-permute-start.8 = (s32[1024]{0:T(1024)S(1)}, s32[1024]{0:T(1024)S(1)}, u32[]{:S(2)}, u32[]{:S(2)}) collective-permute-start(s32[1024]{0:T(1024)S(1)} %bitcast.131), channel_id=1, source_target_pairs={{0,64},{1,65},{2,66},{3,67},{4,68},{5,69},{6,70},{7,71},{8,72},{9,... | collective-permute-start | bytes 12296 | tf_op jit(solution)/shard_map/ppermute | solution.py:62
  30.3 25.0 %copy-start.4 = (f32[8192]{0:T(1024)S(1)}, f32[8192]{0:T(1024)}, u32[]{:S(2)}) copy-start(f32[8192]{0:T(1024)} %param.22) | copy-start | bytes 98308
  30.3 30.4 %copy-start = (f32[3,8192]{1,0:T(4,128)S(1)}, f32[3,8192]{1,0:T(4,128)}, u32[]{:S(2)}) copy-start(f32[3,8192]{1,0:T(4,128)} %param.17) | copy-start | bytes 294916
  30.3 30.4 %copy-start.1 = (f32[3,8192]{1,0:T(4,128)S(1)}, f32[3,8192]{1,0:T(4,128)}, u32[]{:S(2)}) copy-start(f32[3,8192]{1,0:T(4,128)} %param.18) | copy-start | bytes 294916
  30.4 30.4 %copy-start.2 = (f32[3,8192]{1,0:T(4,128)S(1)}, f32[3,8192]{1,0:T(4,128)}, u32[]{:S(2)}) copy-start(f32[3,8192]{1,0:T(4,128)} %param.19) | copy-start | bytes 294916
  30.4 30.4 %copy-start.3 = (f32[3,8192]{1,0:T(4,128)S(1)}, f32[3,8192]{1,0:T(4,128)}, u32[]{:S(2)}) copy-start(f32[3,8192]{1,0:T(4,128)} %param.20) | copy-start | bytes 294916
  30.4 34.7 %copy-start.5 = (f32[8192]{0:T(1024)S(1)}, f32[8192]{0:T(1024)}, u32[]{:S(2)}) copy-start(f32[8192]{0:T(1024)} %param.21) | copy-start | bytes 98308
  42.0 5.9 %collective-permute-start.9 = (f32[6,2048]{1,0:T(8,128)S(1)}, f32[6,2048]{1,0:T(8,128)S(1)}, u32[]{:S(2)}, u32[]{:S(2)}) collective-permute-start(f32[6,2048]{1,0:T(8,128)S(1)} %pad_maximum_fusion.1), channel_id=1, source_target_pairs={{0,1},{1,0},{2,3},{3,2},{4,5},{5,4},{6,7},{7,6},{8,9},{9,8},{10,11... | collective-permute-start | bytes 147464 | tf_op jit(solution)/shard_map/ppermute | solution.py:88
  47.9 3.2 %collective-permute-start.12 = (f32[6,2048]{1,0:T(8,128)S(1)}, f32[6,2048]{1,0:T(8,128)S(1)}, u32[]{:S(2)}, u32[]{:S(2)}) collective-permute-start(f32[6,2048]{1,0:T(8,128)S(1)} %fusion.35), channel_id=1, source_target_pairs={{0,6},{1,7},{2,0},{3,1},{4,2},{5,3},{6,4},{7,5},{8,14},{9,15},{10,... | collective-permute-start | bytes 147464 | tf_op jit(solution)/shard_map/ppermute | solution.py:88
  48.0 4.7 %collective-permute-start.11 = (f32[6,2048]{1,0:T(8,128)S(1)}, f32[6,2048]{1,0:T(8,128)S(1)}, u32[]{:S(2)}, u32[]{:S(2)}) collective-permute-start(f32[6,2048]{1,0:T(8,128)S(1)} %fusion.35), channel_id=1, source_target_pairs={{0,4},{1,5},{2,6},{3,7},{4,0},{5,1},{6,2},{7,3},{8,12},{9,13},{10,... | collective-permute-start | bytes 147464 | tf_op jit(solution)/shard_map/ppermute | solution.py:88
  49.3 5.5 %collective-permute-start.10 = (f32[6,2048]{1,0:T(8,128)S(1)}, f32[6,2048]{1,0:T(8,128)S(1)}, u32[]{:S(2)}, u32[]{:S(2)}) collective-permute-start(f32[6,2048]{1,0:T(8,128)S(1)} %fusion.35), channel_id=1, source_target_pairs={{0,2},{1,3},{2,4},{3,5},{4,6},{5,7},{6,0},{7,1},{8,10},{9,11},{10,... | collective-permute-start | bytes 147464 | tf_op jit(solution)/shard_map/ppermute | solution.py:88
  54.8 3.2 %collective-permute-start.13 = (f32[6,2048]{1,0:T(8,128)S(1)}, f32[6,2048]{1,0:T(8,128)S(1)}, u32[]{:S(2)}, u32[]{:S(2)}) collective-permute-start(f32[6,2048]{1,0:T(8,128)S(1)} %add_add_fusion.1), channel_id=1, source_target_pairs={{0,8},{1,9},{2,10},{3,11},{4,12},{5,13},{6,14},{7,15},{8,0},{9,1},... | collective-permute-start | bytes 147464 | tf_op jit(solution)/shard_map/ppermute | solution.py:88
  58.0 3.2 %collective-permute-start.16 = (f32[6,2048]{1,0:T(8,128)S(1)}, f32[6,2048]{1,0:T(8,128)S(1)}, u32[]{:S(2)}, u32[]{:S(2)}) collective-permute-start(f32[6,2048]{1,0:T(8,128)S(1)} %add.420), channel_id=1, source_target_pairs={{0,48},{1,49},{2,50},{3,51},{4,52},{5,53},{6,54},{7,55},{8,56},{9,... | collective-permute-start | bytes 147464 | tf_op jit(solution)/shard_map/ppermute | solution.py:88
  58.4 4.6 %collective-permute-start.15 = (f32[6,2048]{1,0:T(8,128)S(1)}, f32[6,2048]{1,0:T(8,128)S(1)}, u32[]{:S(2)}, u32[]{:S(2)}) collective-permute-start(f32[6,2048]{1,0:T(8,128)S(1)} %add.420), channel_id=1, source_target_pairs={{0,32},{1,33},{2,34},{3,35},{4,36},{5,37},{6,38},{7,39},{8,40},{9,... | collective-permute-start | bytes 147464 | tf_op jit(solution)/shard_map/ppermute | solution.py:88
  59.9 4.3 %collective-permute-start.14 = (f32[6,2048]{1,0:T(8,128)S(1)}, f32[6,2048]{1,0:T(8,128)S(1)}, u32[]{:S(2)}, u32[]{:S(2)}) collective-permute-start(f32[6,2048]{1,0:T(8,128)S(1)} %add.420), channel_id=1, source_target_pairs={{0,16},{1,17},{2,18},{3,19},{4,20},{5,21},{6,22},{7,23},{8,24},{9,... | collective-permute-start | bytes 147464 | tf_op jit(solution)/shard_map/ppermute | solution.py:88
  64.3 4.9 %collective-permute-start.17 = (f32[6,2048]{1,0:T(8,128)S(1)}, f32[6,2048]{1,0:T(8,128)S(1)}, u32[]{:S(2)}, u32[]{:S(2)}) collective-permute-start(f32[6,2048]{1,0:T(8,128)S(1)} %add_add_fusion), channel_id=1, source_target_pairs={{0,64},{1,65},{2,66},{3,67},{4,68},{5,69},{6,70},{7,71},{8,72},{9,... | collective-permute-start | bytes 147464 | tf_op jit(solution)/shard_map/ppermute | solution.py:88
  173.2 4.7 %collective-permute-start.18 = (f32[13,1024]{1,0:T(8,128)S(1)}, f32[13,1024]{1,0:T(8,128)S(1)}, u32[]{:S(2)}, u32[]{:S(2)}) collective-permute-start(f32[13,1024]{1,0:T(8,128)S(1)} %bitcast.118), channel_id=1, source_target_pairs={{0,64},{1,65},{2,66},{3,67},{4,68},{5,69},{6,70},{7,71},{8,72},{9,... | collective-permute-start | bytes 159752 | tf_op jit(solution)/shard_map/ppermute | solution.py:80
  178.0 2.7 %collective-permute-start.21 = (f32[13,256]{1,0:T(8,128)S(1)}, f32[13,256]{1,0:T(8,128)S(1)}, u32[]{:S(2)}, u32[]{:S(2)}) collective-permute-start(f32[13,256]{1,0:T(8,128)S(1)} %bitcast.126), channel_id=1, source_target_pairs={{0,48},{1,49},{2,50},{3,51},{4,52},{5,53},{6,54},{7,55},{8,56},{9,... | collective-permute-start | bytes 39944 | tf_op jit(solution)/shard_map/ppermute | solution.py:80
  179.2 4.1 %collective-permute-start.20 = (f32[13,256]{1,0:T(8,128)S(1)}, f32[13,256]{1,0:T(8,128)S(1)}, u32[]{:S(2)}, u32[]{:S(2)}) collective-permute-start(f32[13,256]{1,0:T(8,128)S(1)} %fusion.2), channel_id=1, source_target_pairs={{0,32},{1,33},{2,34},{3,35},{4,36},{5,37},{6,38},{7,39},{8,40},{9,... | collective-permute-start | bytes 39944 | tf_op jit(solution)/shard_map/ppermute | solution.py:80
  179.8 3.8 %collective-permute-start.19 = (f32[13,256]{1,0:T(8,128)S(1)}, f32[13,256]{1,0:T(8,128)S(1)}, u32[]{:S(2)}, u32[]{:S(2)}) collective-permute-start(f32[13,256]{1,0:T(8,128)S(1)} %fusion.3), channel_id=1, source_target_pairs={{0,16},{1,17},{2,18},{3,19},{4,20},{5,21},{6,22},{7,23},{8,24},{9,... | collective-permute-start | bytes 39944 | tf_op jit(solution)/shard_map/ppermute | solution.py:80
  183.7 2.6 %collective-permute-start.22 = (f32[13,128]{1,0:T(8,128)S(1)}, f32[13,128]{1,0:T(8,128)S(1)}, u32[]{:S(2)}, u32[]{:S(2)}) collective-permute-start(f32[13,128]{1,0:T(8,128)S(1)} %bitcast.128), channel_id=1, source_target_pairs={{0,8},{1,9},{2,10},{3,11},{4,12},{5,13},{6,14},{7,15},{8,0},{9,1},... | collective-permute-start | bytes 19976 | tf_op jit(solution)/shard_map/ppermute | solution.py:80
  186.4 2.9 %collective-permute-start.25 = (f32[13,32]{1,0:T(8,128)S(1)}, f32[13,32]{1,0:T(8,128)S(1)}, u32[]{:S(2)}, u32[]{:S(2)}) collective-permute-start(f32[13,32]{1,0:T(8,128)S(1)} %bitcast.129), channel_id=1, source_target_pairs={{0,6},{1,7},{2,0},{3,1},{4,2},{5,3},{6,4},{7,5},{8,14},{9,15},{10,... | collective-permute-start | bytes 5000 | tf_op jit(solution)/shard_map/ppermute | solution.py:80
  187.2 4.0 %collective-permute-start.24 = (f32[13,32]{1,0:T(8,128)S(1)}, f32[13,32]{1,0:T(8,128)S(1)}, u32[]{:S(2)}, u32[]{:S(2)}) collective-permute-start(f32[13,32]{1,0:T(8,128)S(1)} %fusion.10), channel_id=1, source_target_pairs={{0,4},{1,5},{2,6},{3,7},{4,0},{5,1},{6,2},{7,3},{8,12},{9,13},{10,... | collective-permute-start | bytes 5000 | tf_op jit(solution)/shard_map/ppermute | solution.py:80
  187.8 3.7 %collective-permute-start.23 = (f32[13,32]{1,0:T(8,128)S(1)}, f32[13,32]{1,0:T(8,128)S(1)}, u32[]{:S(2)}, u32[]{:S(2)}) collective-permute-start(f32[13,32]{1,0:T(8,128)S(1)} %fusion.11), channel_id=1, source_target_pairs={{0,2},{1,3},{2,4},{3,5},{4,6},{5,7},{6,0},{7,1},{8,10},{9,11},{10,... | collective-permute-start | bytes 5000 | tf_op jit(solution)/shard_map/ppermute | solution.py:80
  191.7 11.8 %collective-permute-start.26 = (f32[13,16]{1,0:T(8,128)S(1)}, f32[13,16]{1,0:T(8,128)S(1)}, u32[]{:S(2)}, u32[]{:S(2)}) collective-permute-start(f32[13,16]{1,0:T(8,128)S(1)} %bitcast.130), channel_id=1, source_target_pairs={{0,1},{1,0},{2,3},{3,2},{4,5},{5,4},{6,7},{7,6},{8,9},{9,8},{10,11... | collective-permute-start | bytes 2504 | tf_op jit(solution)/shard_map/ppermute | solution.py:80
